TPU v7x, 256 devices: a whole 4x4x8 slice. The times are simulated.
256 devices in a mesh: own: 32 (over x, z), row: 8 (over y, core).
Axes of the slice: x: 4, y: 4, z: 8, core: 2. Of those that a mesh axis runs over, the one named last changes fastest.
Arguments:
- sigma_anc: float32 [16384, 16384], P('row', 'own'), may hold values from -1.5 to 1.5
- row_blocks: int32 [64, 8], replicated, may hold values from 0 to 63, as said below
- panel1: float32 [64, 2048, 256], P('own', 'row'), may hold values from -0.375 to 0.375
- diag_inv1: float32 [64, 256, 256], P('own'), as said below
- mask1: int32 [64, 8], P('own', 'row'), may hold values 0 or 1
- parent_block2: float32 [64, 256, 256], P('own'), may hold values from -0.375 to 0.375
- panel2: float32 [64, 2048, 256], P('own', 'row'), may hold values from -0.375 to 0.375
- diag_inv2: float32 [64, 256, 256], P('own'), as said below
- mask2: int32 [64, 8], P('own', 'row'), may hold values 0 or 1
Outputs:
- sel1_panel: float32 [64, 2048, 256], P('own', 'row')
- sel1_diag: float32 [64, 256, 256], P('own')
- sel2_parent: float32 [64, 256, 256], P('own')
- sel2_panel: float32 [64, 2048, 256], P('own', 'row')
- sel2_diag: float32 [64, 256, 256], P('own')
Inputs may be any that keep to these rules, and one draw needn't show every extreme that they name: `row_blocks`: entry l of each row lies in block rows 8 * l to 8 * (l + 1) - 1; for supernodes s with the same s // 2, the entries of one column l lie in different aligned runs of 2 block rows. `diag_inv1`: lower triangular, with diagonal entries from 1 to 2. `diag_inv2`: lower triangular, with diagonal entries from 1 to 2.
All inputs are finite; a program needn't handle non-finite values. No bound on the sum of `mask1` or of `mask2` on one device may be relied on, other than what follows from the above.
Results may differ from a plain program's by a relative error of at most 0.000071.
Values sent between devices are 32-bit elements; how exact they have to be, the bound alone decides.
No kernel may reach another device: no remote copies, remote signals or barrier semaphores. Data moves between devices by JAX's collectives and lax.ppermute only.
A program may use at most 128 MiB of HBM per device.

v0:
```python
import jax
import jax.numpy as jnp
from jax import lax
from jax.sharding import PartitionSpec as P

B = 256


HIGH = lax.Precision.HIGHEST


def shifted(shard, axis, by):
    length = lax.axis_size(axis)
    return lax.ppermute(shard, axis, [(i, (i + by) % length) for i in range(length)])


def product(form, left, right):
    return jnp.einsum(form, left, right, precision=HIGH)


def select_send(sigma_local, row_blocks, slots):
    own_count = lax.axis_size("own")
    own_here = lax.axis_index("own")
    row_here = lax.axis_index("row")
    rows_here = sigma_local.shape[0] // B
    cols_here = sigma_local.shape[1] // B
    total = row_blocks.shape[0]
    source = jnp.arange(total, dtype=jnp.int32) % total
    rowlist = row_blocks[source].reshape(own_count, slots, -1)
    group = own_here * cols_here // rows_here
    want_col = lax.dynamic_index_in_dim(rowlist, group, 2, keepdims=False)
    local_col = want_col - own_here * cols_here
    match = ((local_col >= 0) & (local_col < cols_here)).astype(jnp.int32)
    which = jnp.sum(match * jnp.arange(slots, dtype=jnp.int32)[None, :], axis=1)
    present = jnp.sum(match, axis=1).astype(jnp.float32)
    chosen = rowlist[jnp.arange(own_count, dtype=jnp.int32), which]
    chosen_row = (
        lax.dynamic_index_in_dim(chosen, row_here, 1, keepdims=False) - row_here * rows_here
    )
    chosen_col = jnp.clip(
        lax.dynamic_index_in_dim(chosen, group, 1, keepdims=False) - own_here * cols_here,
        0,
        cols_here - 1,
    )
    blocks4 = sigma_local.reshape(rows_here, B, cols_here, B)
    return blocks4[chosen_row, :, chosen_col, :] * present[:, None, None]


def select_take(received, row_blocks, slots, cols_here):
    total = row_blocks.shape[0]
    mine = lax.axis_index("own") * slots + jnp.arange(slots, dtype=jnp.int32)
    rowlist = row_blocks[mine % total]
    sender = rowlist // cols_here
    return received[sender]


def on_device(
    sigma_anc, row_blocks, panel1, diag_inv1, mask1, parent_block2, panel2, diag_inv2, mask2
):
    slots = panel1.shape[0]
    cols_here = sigma_anc.shape[1] // B
    outgoing = select_send(sigma_anc, row_blocks, slots)
    received = lax.all_to_all(outgoing, "own", split_axis=0, concat_axis=0, tiled=True)
    blocks1 = select_take(received, row_blocks, slots, cols_here)
    keep1 = mask1.astype(jnp.float32)
    factor1 = keep1[:, :, None] * product("kij,kjc->kic", panel1, diag_inv1)
    factors1 = lax.all_gather(factor1, "row", axis=1, tiled=True).reshape(slots, -1, B, B)
    sel1_panel = -keep1[:, :, None] * product("kmij,kmjc->kic", blocks1, factors1)
    gram1 = product("kji,kjc->kic", diag_inv1, diag_inv1)
    sel1_diag = gram1 - lax.psum(product("kji,kjc->kic", factor1, sel1_panel), "row")
    par_panel, par_diag, par_keep, blocks2 = shifted(
        (sel1_panel, sel1_diag, keep1, blocks1), "own", 1
    )
    keep2 = mask2.astype(jnp.float32) * par_keep
    up_parent = product("kij,kjc->kic", parent_block2, diag_inv2)
    factor2 = keep2[:, :, None] * product("kij,kjc->kic", panel2, diag_inv2)
    factors2 = lax.all_gather(factor2, "row", axis=1, tiled=True).reshape(slots, -1, B, B)
    sel2_panel = -keep2[:, :, None] * (
        product("kij,kjc->kic", par_panel, up_parent) + product("kmij,kmjc->kic", blocks2, factors2)
    )
    cross, back = lax.psum(
        (product("kji,kjc->kic", par_panel, factor2), product("kji,kjc->kic", factor2, sel2_panel)),
        "row",
    )
    sel2_parent = -(product("kij,kjc->kic", par_diag, up_parent) + cross)
    gram2 = product("kji,kjc->kic", diag_inv2, diag_inv2)
    sel2_diag = gram2 - product("kji,kjc->kic", up_parent, sel2_parent) - back
    return (sel1_panel, sel1_diag, sel2_parent, sel2_panel, sel2_diag)


def solution(mesh):
    in_specs = (
        P("row", "own"),
        P(),
        P("own", "row", None),
        P("own", None, None),
        P("own", "row"),
        P("own", None, None),
        P("own", "row", None),
        P("own", None, None),
        P("own", "row"),
    )
    out_specs = (
        P("own", "row", None),
        P("own", None, None),
        P("own", None, None),
        P("own", "row", None),
        P("own", None, None),
    )
    return jax.shard_map(
        on_device, mesh=mesh, in_specs=in_specs, out_specs=out_specs, check_vma=False
    )
```

profile of v0, /device:TPU:1, one launch (start us, length us, event | category | flops | bytes accessed | tf_op | source)
XLA Modules:
  0.0 459.1 jit_solution(15500695550618360593)
XLA Ops:
  7.2 0.0 copy-start
  7.2 0.8 copy.67
  8.1 0.6 gather_fusion
  8.7 0.1 constant_dynamic-slice_fusion
  8.8 0.1 copy.90
  8.9 0.1 copy.69
  9.0 0.1 fusion.6
  9.1 0.7 gather_fusion.1
  9.8 5.9 %reshape.242 = f32[8,256,2,256]{3,2,1,0:T(2,128)} reshape(f32[2048,512]{1,0:T(8,128)} %param.9) | data formatting | bytes 8388608 | tf_op jit(solution)/shard_map/reshape | solution.py:45
  15.7 4.6 %copy.72 = f32[8,256,2,256]{3,1,2,0:T(8,128)} copy(f32[8,256,2,256]{3,2,1,0:T(2,128)} %reshape.242) | data formatting | bytes 8388608 | tf_op jit(solution)/shard_map/reshape | solution.py:45
  20.3 0.2 fusion.10
  20.5 6.5 %gather_fusion.2 = f32[32,256,256]{2,1,0:T(8,128)} fusion(f32[8,256,2,256]{3,1,2,0:T(8,128)} %copy.72, s32[32]{0:T(128)S(1)} %fusion.10), kind=kCustom, calls=%fused_computation.2 | custom fusion | bytes 16777472 | tf_op jit(solution)/shard_map/gather | solution.py:46
  27.0 7.8 %broadcast_multiply_fusion = f32[32,256,256]{2,1,0:T(8,128)} fusion(f32[32,256,256]{2,1,0:T(8,128)} %gather_fusion.2, f32[32]{0:T(128)S(1)} %convert_element_type.18), kind=kLoop, calls=%fused_computation.5 | loop fusion | flops 2097152 | bytes 16777344 | tf_op jit(solution)/shard_map/mul | solution.py:46
  34.8 0.0 copy-start.10
  34.8 12.1 %all-to-all-start = ((f32[32,256,256]{2,1,0:T(8,128)}), f32[32,256,256]{2,1,0:T(8,128)}, u32[]{:S(2)}, u32[]{:S(2)}) async-start(f32[32,256,256]{2,1,0:T(8,128)} %broadcast_multiply_fusion), calls=%async_computation | async-start | bytes 16777216 | tf_op jit(solution)/shard_map/all_to_all | solution.py:63
  47.0 0.0 all-gather.3.cloned.1.call-start
  47.0 0.0 copy-done.13
  47.1 0.0 copy-done.3
  47.1 0.0 copy-done.9
  47.1 1.5 convolution_multiply_fusion
  48.5 0.0 all-gather.3.cloned.1.call-update
  48.6 0.0 all-gather.5.cloned.1.call-start
  48.6 1.2 collective-permute-start.2
  49.8 185.4 %collective-permute-done.2 = f32[2,1]{0,1:T(1,128)S(1)} collective-permute-done((f32[2,1]{0,1:T(1,128)S(1)}, f32[2,1]{0,1:T(1,128)S(1)}, u32[]{:S(2)}, u32[]{:S(2)}) %collective-permute-start.2) | collective-permute-done | bytes 40 | tf_op jit(solution)/shard_map/ppermute | solution.py:14
  235.2 0.0 copy-done.12
  235.2 0.0 copy-done
  235.2 0.0 copy-done.10
  235.2 1.5 broadcast_multiply_fusion.2
  236.7 0.0 all-gather.5.cloned.1.call-update
  236.7 0.0 all-reduce.3.cloned.1.call-start
  236.8 0.6 gather_fusion.3
  237.4 0.1 reshape.233
  237.4 0.0 all-to-all-done
  237.4 6.2 %gather_fusion.4 = f32[16,256,256]{2,1,0:T(8,128)} fusion(f32[32,256,256]{2,1,0:T(8,128)} %all-to-all-done, s32[1024]{0:T(1024)S(1)} %pad_clamp_fusion), kind=kCustom, calls=%fused_computation.4 | custom fusion | bytes 8388672 | tf_op jit(solution)/shard_map/gather | solution.py:54
  243.6 9.9 %collective-permute-start.3 = (f32[2,8,256,256]{3,2,1,0:T(8,128)}, f32[2,8,256,256]{3,2,1,0:T(8,128)}, u32[]{:S(2)}, u32[]{:S(2)}) collective-permute-start(f32[2,8,256,256]{3,2,1,0:T(8,128)} %bitcast.68), channel_id=1, source_target_pairs={{0,8},{8,16},{16,24},{24,32},{32,40},{40,48},{48,56},{56,64},{64,7... | collective-permute-start | bytes 12582920 | tf_op jit(solution)/shard_map/ppermute | solution.py:14
  253.5 0.0 copy-start.1
  253.5 8.8 %fusion.2 = f32[2,256,256]{2,1,0:T(8,128)S(1)} fusion(f32[2,8,256,256]{3,2,1,0:T(8,128)} %bitcast.69, f32[2,8,256,256]{3,2,1,0:T(8,128)} %bitcast.70, f32[2]{0:T(128)S(1)} %bitcast_negate_fusion), kind=kOutput, calls=%fused_computation.14 | convolution fusion | flops 3221356544 | bytes 8912904 | tf_op jit(solution)/shard_map/kmij,kmjc->kic/dot_general | solution.py:18
  262.3 0.0 copy-start.4
  262.3 0.3 collective-permute-start.1
  262.6 0.0 copy-done.7
  262.6 0.7 fusion.21
  263.2 0.0 copy-done.2
  263.2 1.9 fusion.20
  265.1 89.9 %collective-permute-done.1 = f32[2,256,256]{2,1,0:T(8,128)S(1)} collective-permute-done((f32[2,256,256]{2,1,0:T(8,128)S(1)}, f32[2,256,256]{2,1,0:T(8,128)S(1)}, u32[]{:S(2)}, u32[]{:S(2)}) %collective-permute-start.1) | collective-permute-done | bytes 524320 | tf_op jit(solution)/shard_map/ppermute | solution.py:14
  355.0 0.0 copy-done.1
  355.0 1.8 fusion.22
  356.9 0.0 collective-permute-done.3
  356.9 8.1 %convolution_bitcast_fusion = f32[2,256,256]{2,1,0:T(8,128)S(1)} fusion(f32[2,8,256,256]{3,2,1,0:T(8,128)} %collective-permute-done.3, f32[2,8,256,256]{3,2,1,0:T(8,128)} %bitcast.71), kind=kOutput, calls=%fused_computation.8 | convolution fusion | flops 3221225472 | bytes 8912896 | tf_op jit(solution)/shard_map/kmij,kmjc->kic/dot_general | solution.py:18
  364.9 0.0 copy-done.4
  364.9 0.7 broadcast_multiply_fusion.1
  365.6 0.0 copy-start.5
  365.6 1.8 fusion.24
  367.5 0.0 all-reduce.3.cloned.1.call-update
  367.5 64.4 %all-reduce.3.cloned.1.call-done = (f32[2,256,256]{2,1,0:T(8,128)}, f32[2,256,256]{2,1,0:T(8,128)}, f32[2,256,256]{2,1,0:T(8,128)}) async-done(((f32[2,256,256]{2,1,0:T(8,128)}, f32[2,256,256]{2,1,0:T(8,128)}, f32[2,256,256]{2,1,0:T(8,128)}), (f32[2,256,256]{2,1,0:T(8,128)}, f32[2,256,256]{2,1,0:T(8,128)}, f32[2,256,256]{2,1,0:T(8,128)})) %all-reduce.3.cloned.1.call-update) | async-done | bytes 1572880 | tf_op jit(solution)/shard_map/psum | solution.py:70
  431.9 2.2 convolution_subtract_fusion.1
  434.0 0.0 copy-start.11
  434.0 1.4 collective-permute-start
  435.4 1.1 fusion.23
  436.5 12.5 %collective-permute-done = f32[2,256,256]{2,1,0:T(8,128)S(1)} collective-permute-done((f32[2,256,256]{2,1,0:T(8,128)S(1)}, f32[2,256,256]{2,1,0:T(8,128)S(1)}, u32[]{:S(2)}, u32[]{:S(2)}) %collective-permute-start) | collective-permute-done | bytes 524320 | tf_op jit(solution)/shard_map/ppermute | solution.py:14
  449.0 1.7 fusion.1
  450.7 0.0 copy-done.5
  450.7 0.0 copy-start.6
  450.7 1.8 fusion
  452.6 0.0 copy-done.6
  (22 shorter events, 0.1 us)
Async XLA Ops:
  7.2 228.0 %copy-start = (f32[2,256,256]{2,1,0:T(8,128)S(1)}, f32[2,256,256]{2,1,0:T(8,128)}, u32[]{:S(2)}) copy-start(f32[2,256,256]{2,1,0:T(8,128)} %param.16) | copy-start | bytes 1572868
  34.8 12.2 %copy-start.13 = (s32[2,1]{0,1:T(1,128)S(1)}, s32[2,1]{0,1:T(1,128)}, u32[]{:S(2)}) copy-start(s32[2,1]{0,1:T(1,128)} %param.13) | copy-start | bytes 28
  34.8 12.2 %copy-start.3 = (f32[2,256,256]{2,1,0:T(8,128)S(1)}, f32[2,256,256]{2,1,0:T(8,128)}, u32[]{:S(2)}) copy-start(f32[2,256,256]{2,1,0:T(8,128)} %param.12) | copy-start | bytes 1572868
  34.8 12.2 %copy-start.9 = (f32[2,256,256]{2,1,0:T(8,128)S(1)}, f32[2,256,256]{2,1,0:T(8,128)}, u32[]{:S(2)}) copy-start(f32[2,256,256]{2,1,0:T(8,128)} %param.11) | copy-start | bytes 1572868
  34.8 200.4 %copy-start.12 = (s32[2,1]{0,1:T(1,128)S(1)}, s32[2,1]{0,1:T(1,128)}, u32[]{:S(2)}) copy-start(s32[2,1]{0,1:T(1,128)} %param.17) | copy-start | bytes 28
  34.8 200.4 %copy-start.10 = (f32[2,256,256]{2,1,0:T(8,128)S(1)}, f32[2,256,256]{2,1,0:T(8,128)}, u32[]{:S(2)}) copy-start(f32[2,256,256]{2,1,0:T(8,128)} %param.15) | copy-start | bytes 1572868
  34.8 202.6 %all-to-all-start = ((f32[32,256,256]{2,1,0:T(8,128)}), f32[32,256,256]{2,1,0:T(8,128)}, u32[]{:S(2)}, u32[]{:S(2)}) async-start(f32[32,256,256]{2,1,0:T(8,128)} %broadcast_multiply_fusion), calls=%async_computation | async-start | bytes 16777216 | tf_op jit(solution)/shard_map/all_to_all | solution.py:63
  47.0 206.5 %all-gather.3.cloned.1.call-start = ((), (), s32[]{:S(2)}) async-start(), calls=%async_computation.1 | async-start | bytes 4718592 | tf_op jit(solution)/shard_map/all_gather | solution.py:67
  48.6 308.3 %all-gather.5.cloned.1.call-start = ((), (), s32[]{:S(2)}) async-start(), calls=%async_computation.2 | async-start | bytes 4718592 | tf_op jit(solution)/shard_map/all_gather | solution.py:77
  48.6 186.6 %collective-permute-start.2 = (f32[2,1]{0,1:T(1,128)S(1)}, f32[2,1]{0,1:T(1,128)S(1)}, u32[]{:S(2)}, u32[]{:S(2)}) collective-permute-start(f32[2,1]{0,1:T(1,128)S(1)} %get-tuple-element.12), channel_id=1, source_target_pairs={{0,8},{8,16},{16,24},{24,32},{32,40},{40,48},{48,56},{56,64},{64,7... | collective-permute-start | bytes 32 | tf_op jit(solution)/shard_map/ppermute | solution.py:14
  236.7 195.2 %all-reduce.3.cloned.1.call-start = ((), (), s32[]{:S(2)}) async-start(), calls=%async_computation.3 | async-start | bytes 3145728 | tf_op jit(solution)/shard_map/psum | solution.py:70
  243.6 113.2 %collective-permute-start.3 = (f32[2,8,256,256]{3,2,1,0:T(8,128)}, f32[2,8,256,256]{3,2,1,0:T(8,128)}, u32[]{:S(2)}, u32[]{:S(2)}) collective-permute-start(f32[2,8,256,256]{3,2,1,0:T(8,128)} %bitcast.68), channel_id=1, source_target_pairs={{0,8},{8,16},{16,24},{24,32},{32,40},{40,48},{48,56},{56,64},{64,7... | collective-permute-start | bytes 12582920 | tf_op jit(solution)/shard_map/ppermute | solution.py:14
  253.5 9.1 %copy-start.7 = (f32[2,256,256]{2,1,0:T(8,128)S(1)}, f32[2,256,256]{2,1,0:T(8,128)}, u32[]{:S(2)}) copy-start(f32[2,256,256]{2,1,0:T(8,128)} %param.14) | copy-start | bytes 1572868
  253.5 9.7 %copy-start.2 = (f32[2,256,256]{2,1,0:T(8,128)S(1)}, f32[2,256,256]{2,1,0:T(8,128)}, u32[]{:S(2)}) copy-start(f32[2,256,256]{2,1,0:T(8,128)} %convolution_multiply_fusion) | copy-start | bytes 1572868
  253.5 101.5 %copy-start.1 = (f32[2,256,256]{2,1,0:T(8,128)S(1)}, f32[2,256,256]{2,1,0:T(8,128)}, u32[]{:S(2)}) copy-start(f32[2,256,256]{2,1,0:T(8,128)} %broadcast_multiply_fusion.2) | copy-start | bytes 1572868
  262.3 102.7 %copy-start.4 = (f32[2,256,256]{2,1,0:T(8,128)}, f32[2,256,256]{2,1,0:T(8,128)S(1)}, u32[]{:S(2)}) copy-start(f32[2,256,256]{2,1,0:T(8,128)S(1)} %fusion.2) | copy-start | bytes 1572868
  262.3 92.7 %collective-permute-start.1 = (f32[2,256,256]{2,1,0:T(8,128)S(1)}, f32[2,256,256]{2,1,0:T(8,128)S(1)}, u32[]{:S(2)}, u32[]{:S(2)}) collective-permute-start(f32[2,256,256]{2,1,0:T(8,128)S(1)} %fusion.2), channel_id=1, source_target_pairs={{0,8},{8,16},{16,24},{24,32},{32,40},{40,48},{48,56},{56,64},{64,7... | collective-permute-start | bytes 1572872 | tf_op jit(solution)/shard_map/ppermute | solution.py:14
  365.6 85.1 %copy-start.5 = (f32[2,256,256]{2,1,0:T(8,128)}, f32[2,256,256]{2,1,0:T(8,128)S(1)}, u32[]{:S(2)}) copy-start(f32[2,256,256]{2,1,0:T(8,128)S(1)} %broadcast_multiply_fusion.1) | copy-start | bytes 1572868
  431.9 18.9 %copy-start.8 = (f32[2,256,256]{2,1,0:T(8,128)S(1)}, f32[2,256,256]{2,1,0:T(8,128)}, u32[]{:S(2)}) copy-start(f32[2,256,256]{2,1,0:T(8,128)} %get-tuple-element.9) | copy-start | bytes 1572868
  434.0 18.6 %copy-start.11 = (f32[2,256,256]{2,1,0:T(8,128)}, f32[2,256,256]{2,1,0:T(8,128)S(1)}, u32[]{:S(2)}) copy-start(f32[2,256,256]{2,1,0:T(8,128)S(1)} %convolution_subtract_fusion.1) | copy-start | bytes 1572868
  434.0 15.0 %collective-permute-start = (f32[2,256,256]{2,1,0:T(8,128)S(1)}, f32[2,256,256]{2,1,0:T(8,128)S(1)}, u32[]{:S(2)}, u32[]{:S(2)}) collective-permute-start(f32[2,256,256]{2,1,0:T(8,128)S(1)} %convolution_subtract_fusion.1), channel_id=1, source_target_pairs={{0,8},{8,16},{16,24},{24,32},{32,40},{40,48},{48,56},{56,64},{64,7... | collective-permute-start | bytes 1572872 | tf_op jit(solution)/shard_map/ppermute | solution.py:14
  450.7 1.9 copy-start.6
Sparse Core Ops, SparseCore 0:
  50.2 36.7 all-gather.2
  236.8 40.5 all-gather.4
  367.6 64.1 all-reduce.2
where the time goes:
time: 461 us; the launch traced here: 459 us
  waiting for transfers between devices  352 us (76%)
  matrix products  33.4 us (7%)
  local copies, waits for them, and re-layouts  26.3 us (6%)
  starting transfers between devices  25 us (5%)
  between operations  14 us (3%)
  other arithmetic  8.18 us (2%)
    ppermute x4, waiting for transfers between devices, shifted(): lax.ppermute(shard, axis, [(i, (i + by) % length) for i in range(length)])  288 us
    psum x1, waiting for transfers between devices, on_device(): lax.psum(product('kji,kjc->kic', factor1, sel1_panel), 'row')  64.4 us
    dot_general x13, matrix products, product(): return jnp.einsum(form, left, right, precision=HIGH)  33.4 us
    ppermute x4, starting transfers between devices, shifted(): lax.ppermute(shard, axis, [(i, (i + by) % length) for i in range(length)])  12.7 us
    all_to_all x1, starting transfers between devices, on_device(): lax.all_to_all(outgoing, 'own', split_axis=0, concat_axis=0, tiled=True)  12.1 us
    reshape x2, local copies, waits for them, and re-layouts, select_send(): blocks4 = sigma_local.reshape(rows_here, B, cols_here, B)  10.6 us
  transfers between devices with their start and end apart: 8, of which 4 were waited for; matrix products, arithmetic and copies ran while one was open for 5% of the time, Pallas kernels for 0%

commit v1 on v0

--- a/solution.py
+++ b/solution.py
@@ -24,15 +24,12 @@
     row_here = lax.axis_index("row")
     rows_here = sigma_local.shape[0] // B
     cols_here = sigma_local.shape[1] // B
-    total = row_blocks.shape[0]
-    source = jnp.arange(total, dtype=jnp.int32) % total
-    rowlist = row_blocks[source].reshape(own_count, slots, -1)
+    rowlist = row_blocks.reshape(own_count, slots, -1)
     group = own_here * cols_here // rows_here
     want_col = lax.dynamic_index_in_dim(rowlist, group, 2, keepdims=False)
     local_col = want_col - own_here * cols_here
     match = ((local_col >= 0) & (local_col < cols_here)).astype(jnp.int32)
     which = jnp.sum(match * jnp.arange(slots, dtype=jnp.int32)[None, :], axis=1)
-    present = jnp.sum(match, axis=1).astype(jnp.float32)
     chosen = rowlist[jnp.arange(own_count, dtype=jnp.int32), which]
     chosen_row = (
         lax.dynamic_index_in_dim(chosen, row_here, 1, keepdims=False) - row_here * rows_here
@@ -43,13 +40,12 @@
         cols_here - 1,
     )
     blocks4 = sigma_local.reshape(rows_here, B, cols_here, B)
-    return blocks4[chosen_row, :, chosen_col, :] * present[:, None, None]
+    return blocks4[chosen_row, :, chosen_col, :]
 
 
 def select_take(received, row_blocks, slots, cols_here):
-    total = row_blocks.shape[0]
     mine = lax.axis_index("own") * slots + jnp.arange(slots, dtype=jnp.int32)
-    rowlist = row_blocks[mine % total]
+    rowlist = row_blocks[mine]
     sender = rowlist // cols_here
     return received[sender]
 
@@ -59,6 +55,11 @@
 ):
     slots = panel1.shape[0]
     cols_here = sigma_anc.shape[1] // B
+    keep_own2 = mask2.astype(jnp.float32)
+    up_parent = product("kij,kjc->kic", parent_block2, diag_inv2)
+    factor2_own = keep_own2[:, :, None] * product("kij,kjc->kic", panel2, diag_inv2)
+    factor2_child = shifted(factor2_own, "own", -1)
+
     outgoing = select_send(sigma_anc, row_blocks, slots)
     received = lax.all_to_all(outgoing, "own", split_axis=0, concat_axis=0, tiled=True)
     blocks1 = select_take(received, row_blocks, slots, cols_here)
@@ -68,20 +69,22 @@
     sel1_panel = -keep1[:, :, None] * product("kmij,kmjc->kic", blocks1, factors1)
     gram1 = product("kji,kjc->kic", diag_inv1, diag_inv1)
     sel1_diag = gram1 - lax.psum(product("kji,kjc->kic", factor1, sel1_panel), "row")
-    par_panel, par_diag, par_keep, blocks2 = shifted(
-        (sel1_panel, sel1_diag, keep1, blocks1), "own", 1
+
+    factor2 = keep1[:, :, None] * factor2_child
+    factors2 = lax.all_gather(factor2, "row", axis=1, tiled=True).reshape(slots, -1, B, B)
+    anc2 = keep1[:, :, None] * product("kmij,kmjc->kic", blocks1, factors2)
+
+    par_panel = shifted(sel1_panel, "own", 1)
+    par_anc = shifted(anc2, "own", 1)
+    par_diag = shifted(sel1_diag, "own", 1)
+
+    sel2_panel = -keep_own2[:, :, None] * (
+        product("kij,kjc->kic", par_panel, up_parent) + par_anc
     )
-    keep2 = mask2.astype(jnp.float32) * par_keep
-    up_parent = product("kij,kjc->kic", parent_block2, diag_inv2)
-    factor2 = keep2[:, :, None] * product("kij,kjc->kic", panel2, diag_inv2)
-    factors2 = lax.all_gather(factor2, "row", axis=1, tiled=True).reshape(slots, -1, B, B)
-    sel2_panel = -keep2[:, :, None] * (
-        product("kij,kjc->kic", par_panel, up_parent) + product("kmij,kmjc->kic", blocks2, factors2)
-    )
-    cross, back = lax.psum(
-        (product("kji,kjc->kic", par_panel, factor2), product("kji,kjc->kic", factor2, sel2_panel)),
-        "row",
-    )
+    cross = product("kji,kjc->kic", par_panel, factor2_own)
+    back = product("kji,kjc->kic", factor2_own, sel2_panel)
+    par_diag, cross, back = lax.optimization_barrier((par_diag, cross, back))
+    cross, back = lax.psum((cross, back), "row")
     sel2_parent = -(product("kij,kjc->kic", par_diag, up_parent) + cross)
     gram2 = product("kji,kjc->kic", diag_inv2, diag_inv2)
     sel2_diag = gram2 - product("kji,kjc->kic", up_parent, sel2_parent) - back

time: 461 us -> 445 us (0.965)
  other arithmetic: 8.18 us -> 2.14 us
  waiting for transfers between devices: 352 us -> 346 us
    ppermute x4, waiting for transfers between devices: 288 us -> 198 us  [shifted(): lax.ppermute(shard, axis, [(i, (i + by) % length) for i in range(length)])]
    psum x0 -> x1, waiting for transfers between devices: none -> 66.7 us  [on_device(): cross, back = lax.psum((cross, back), 'row')]
    all_gather x1, waiting for transfers between devices: 0.01 us -> 19.7 us  [on_device(): lax.all_gather(factor2, 'row', axis=1, tiled=True).reshape(slots, -1, B, B)]
    mul x1 -> x2, other arithmetic: 7.78 us -> 0.9 us  [the longest x1 0.9 us: on_device(): factor2 = keep1[:, :, None] * factor2_child]
  transfers between devices with their start and end apart: 8 -> 9, of which waited for: 4 -> 5; matrix products, arithmetic and copies ran while one was open for 5% -> 9% of each run, Pallas kernels for 0% -> 0%
where the time goes in v1:
time: 445 us; the launch traced here: 444 us
  waiting for transfers between devices  346 us (78%)
  matrix products  34.3 us (8%)
  local copies, waits for them, and re-layouts  25.7 us (6%)
  starting transfers between devices  21.9 us (5%)
  between operations  14 us (3%)
    ppermute x4, waiting for transfers between devices, shifted(): lax.ppermute(shard, axis, [(i, (i + by) % length) for i in range(length)])  198 us
    psum x1, waiting for transfers between devices, on_device(): cross, back = lax.psum((cross, back), 'row')  66.7 us
    psum x1, waiting for transfers between devices, on_device(): lax.psum(product('kji,kjc->kic', factor1, sel1_panel), 'row')  61.3 us
    dot_general x13, matrix products, product(): return jnp.einsum(form, left, right, precision=HIGH)  34.3 us
    all_gather x1, waiting for transfers between devices, on_device(): lax.all_gather(factor2, 'row', axis=1, tiled=True).reshape(slots, -1, B, B)  19.7 us
    all_to_all x1, starting transfers between devices, on_device(): lax.all_to_all(outgoing, 'own', split_axis=0, concat_axis=0, tiled=True)  12.1 us
    reshape x2, local copies, waits for them, and re-layouts, select_send(): blocks4 = sigma_local.reshape(rows_here, B, cols_here, B)  10.6 us
    ppermute x4, starting transfers between devices, shifted(): lax.ppermute(shard, axis, [(i, (i + by) % length) for i in range(length)])  9.62 us
  transfers between devices with their start and end apart: 9, of which 5 were waited for; matrix products, arithmetic and copies ran while one was open for 9% of the time, Pallas kernels for 0%

profile of v1, /device:TPU:1, one launch (start us, length us, event | category | flops | bytes accessed | tf_op | source)
XLA Modules:
  0.0 443.8 jit_solution(6164868798614665549)
XLA Ops:
  7.2 0.0 copy-start
  7.2 0.8 copy.67
  8.0 0.1 constant_dynamic-slice_fusion
  8.1 0.1 copy.90
  8.2 0.1 copy.69
  8.3 0.1 fusion.7
  8.5 0.7 gather_fusion
  9.1 5.9 %reshape.167 = f32[8,256,2,256]{3,2,1,0:T(2,128)} reshape(f32[2048,512]{1,0:T(8,128)} %param.9) | data formatting | bytes 8388608 | tf_op jit(solution)/shard_map/reshape | solution.py:42
  15.1 4.7 %copy.72 = f32[8,256,2,256]{3,1,2,0:T(8,128)} copy(f32[8,256,2,256]{3,2,1,0:T(2,128)} %reshape.167) | data formatting | bytes 8388608 | tf_op jit(solution)/shard_map/reshape | solution.py:42
  19.7 0.2 fusion.11
  19.9 6.5 %gather_fusion.1 = f32[32,256,256]{2,1,0:T(8,128)} fusion(f32[8,256,2,256]{3,1,2,0:T(8,128)} %copy.72, s32[32]{0:T(128)S(1)} %fusion.11), kind=kCustom, calls=%fused_computation.1 | custom fusion | bytes 16777472 | tf_op jit(solution)/shard_map/gather | solution.py:43
  26.4 0.0 copy-start.8
  26.5 12.1 %all-to-all-start = ((f32[32,256,256]{2,1,0:T(8,128)}), f32[32,256,256]{2,1,0:T(8,128)}, u32[]{:S(2)}, u32[]{:S(2)}) async-start(f32[32,256,256]{2,1,0:T(8,128)} %gather_fusion.1), calls=%async_computation | async-start | bytes 16777216 | tf_op jit(solution)/shard_map/all_to_all | solution.py:64
  38.6 0.0 all-gather.3.cloned.1.call-start
  38.6 0.0 copy-done.9
  38.7 0.0 copy-done.2
  38.7 0.0 copy-done.7
  38.7 1.5 convolution_multiply_fusion.1
  40.1 0.0 all-gather.3.cloned.1.call-update
  40.2 0.0 all-gather.5.cloned.1.call-start
  40.2 0.0 copy-done.10
  40.2 0.0 copy-done
  40.2 0.0 copy-done.8
  40.3 0.7 convolution_multiply_fusion
  40.9 4.6 %collective-permute-start.2 = (f32[2,256,256]{2,1,0:T(8,128)S(1)}, f32[2,256,256]{2,1,0:T(8,128)S(1)}, u32[]{:S(2)}, u32[]{:S(2)}) collective-permute-start(f32[2,256,256]{2,1,0:T(8,128)S(1)} %convolution_multiply_fusion), channel_id=1, source_target_pairs={{0,248},{8,0},{16,8},{24,16},{32,24},{40,32},{48,40},{56,48},{64,5... | collective-permute-start | bytes 1572872 | tf_op jit(solution)/shard_map/ppermute | solution.py:14
  45.6 189.5 %collective-permute-done.2 = f32[2,256,256]{2,1,0:T(8,128)S(1)} collective-permute-done((f32[2,256,256]{2,1,0:T(8,128)S(1)}, f32[2,256,256]{2,1,0:T(8,128)S(1)}, u32[]{:S(2)}, u32[]{:S(2)}) %collective-permute-start.2) | collective-permute-done | bytes 524320 | tf_op jit(solution)/shard_map/ppermute | solution.py:14
  235.1 0.9 broadcast_multiply_fusion
  236.0 0.0 all-gather.5.cloned.1.call-update
  236.0 0.0 all-reduce.4.cloned.1.call-start
  236.1 0.6 gather_fusion.2
  236.6 0.1 reshape.158
  236.7 0.0 all-to-all-done
  236.7 6.2 %gather_fusion.3 = f32[16,256,256]{2,1,0:T(8,128)} fusion(f32[32,256,256]{2,1,0:T(8,128)} %all-to-all-done, s32[1024]{0:T(1024)S(1)} %pad_clamp_fusion), kind=kCustom, calls=%fused_computation.3 | custom fusion | bytes 8388672 | tf_op jit(solution)/shard_map/gather | solution.py:50
  242.9 8.1 %fusion.3 = f32[2,256,256]{2,1,0:T(8,128)S(1)} fusion(f32[2,8,256,256]{3,2,1,0:T(8,128)} %bitcast.67, f32[2,8,256,256]{3,2,1,0:T(8,128)} %bitcast.69, f32[2]{0:T(128)S(1)} %fusion.16), kind=kOutput, calls=%fused_computation.14 | convolution fusion | flops 3221356544 | bytes 8912904 | tf_op jit(solution)/shard_map/kmij,kmjc->kic/dot_general | solution.py:18
  251.1 0.0 copy-start.3
  251.1 2.4 collective-permute-start.1
  253.5 0.0 copy-done.1
  253.5 1.9 fusion.18
  255.4 19.7 %all-gather.5.cloned.1.call-done = f32[2,2048,256]{2,1,0:T(8,128)} async-done(((f32[2,256,256]{2,1,0:T(8,128)}), f32[2,2048,256]{2,1,0:T(8,128)}) %all-gather.5.cloned.1.call-update) | async-done | bytes 4194320 | tf_op jit(solution)/shard_map/all_gather | solution.py:74
  275.1 8.2 %fusion.1 = f32[2,256,256]{2,1,0:T(8,128)} fusion(f32[2,8,256,256]{3,2,1,0:T(8,128)} %bitcast.68, f32[2,8,256,256]{3,2,1,0:T(8,128)} %bitcast.70, f32[2]{0:T(128)S(1)} %convert_bitcast_fusion.1), kind=kOutput, calls=%fused_computation.8 | convolution fusion | flops 3221356544 | bytes 8912904 | tf_op jit(solution)/shard_map/kmij,kmjc->kic/dot_general | solution.py:18
  283.3 0.0 copy-done.3
  283.3 1.3 collective-permute-start.3
  284.6 0.0 all-reduce.4.cloned.1.call-update
  284.6 0.0 all-reduce.6.cloned.1.call-start
  284.7 1.7 fusion.20
  286.4 61.3 %all-reduce.4.cloned.1.call-done = f32[2,256,256]{2,1,0:T(8,128)} async-done(((f32[2,256,256]{2,1,0:T(8,128)}), f32[2,256,256]{2,1,0:T(8,128)}) %all-reduce.4.cloned.1.call-update) | async-done | bytes 524304 | tf_op jit(solution)/shard_map/psum | solution.py:71
  347.7 2.9 convolution_subtract_fusion.1
  350.6 1.3 collective-permute-start
  351.9 0.0 collective-permute-done.3
  351.9 0.0 collective-permute-done.1
  351.9 1.7 fusion.2
  353.6 0.0 copy-start.4
  353.6 1.8 fusion.21
  355.4 1.8 fusion.19
  357.3 8.3 %collective-permute-done = f32[2,256,256]{2,1,0:T(8,128)} collective-permute-done((f32[2,256,256]{2,1,0:T(8,128)}, f32[2,256,256]{2,1,0:T(8,128)}, u32[]{:S(2)}, u32[]{:S(2)}) %collective-permute-start) | collective-permute-done | bytes 524320 | tf_op jit(solution)/shard_map/ppermute | solution.py:14
  365.6 0.0 all-reduce.6.cloned.1.call-update
  365.6 1.1 fusion.22
  366.7 66.7 %all-reduce.6.cloned.1.call-done = (f32[2,256,256]{2,1,0:T(8,128)}, f32[2,256,256]{2,1,0:T(8,128)}) async-done(((f32[2,256,256]{2,1,0:T(8,128)}, f32[2,256,256]{2,1,0:T(8,128)}), (f32[2,256,256]{2,1,0:T(8,128)}, f32[2,256,256]{2,1,0:T(8,128)})) %all-reduce.6.cloned.1.call-update) | async-done | bytes 1048592 | tf_op jit(solution)/shard_map/psum | solution.py:87
  433.4 1.9 fusion
  435.3 0.0 copy-start.5
  435.3 1.0 convolution_subtract_fusion
  436.4 0.0 copy-done.4
  436.4 0.0 copy-done.6
  436.4 0.9 sub.48
  (17 shorter events, 0.1 us)
Async XLA Ops:
  7.2 33.1 %copy-start = (f32[2,256,256]{2,1,0:T(8,128)S(1)}, f32[2,256,256]{2,1,0:T(8,128)}, u32[]{:S(2)}) copy-start(f32[2,256,256]{2,1,0:T(8,128)} %param.16) | copy-start | bytes 1572868
  26.4 12.2 %copy-start.9 = (s32[2,1]{0,1:T(1,128)S(1)}, s32[2,1]{0,1:T(1,128)}, u32[]{:S(2)}) copy-start(s32[2,1]{0,1:T(1,128)} %param.13) | copy-start | bytes 28
  26.4 12.2 %copy-start.2 = (f32[2,256,256]{2,1,0:T(8,128)S(1)}, f32[2,256,256]{2,1,0:T(8,128)}, u32[]{:S(2)}) copy-start(f32[2,256,256]{2,1,0:T(8,128)} %param.12) | copy-start | bytes 1572868
  26.4 12.2 %copy-start.7 = (f32[2,256,256]{2,1,0:T(8,128)S(1)}, f32[2,256,256]{2,1,0:T(8,128)}, u32[]{:S(2)}) copy-start(f32[2,256,256]{2,1,0:T(8,128)} %param.11) | copy-start | bytes 1572868
  26.4 13.8 %copy-start.10 = (s32[2,1]{0,1:T(1,128)S(1)}, s32[2,1]{0,1:T(1,128)}, u32[]{:S(2)}) copy-start(s32[2,1]{0,1:T(1,128)} %param.17) | copy-start | bytes 28
  26.4 13.8 %copy-start.8 = (f32[2,256,256]{2,1,0:T(8,128)S(1)}, f32[2,256,256]{2,1,0:T(8,128)}, u32[]{:S(2)}) copy-start(f32[2,256,256]{2,1,0:T(8,128)} %param.15) | copy-start | bytes 1572868
  26.5 210.3 %all-to-all-start = ((f32[32,256,256]{2,1,0:T(8,128)}), f32[32,256,256]{2,1,0:T(8,128)}, u32[]{:S(2)}, u32[]{:S(2)}) async-start(f32[32,256,256]{2,1,0:T(8,128)} %gather_fusion.1), calls=%async_computation | async-start | bytes 16777216 | tf_op jit(solution)/shard_map/all_to_all | solution.py:64
  38.6 204.3 %all-gather.3.cloned.1.call-start = ((), (), s32[]{:S(2)}) async-start(), calls=%async_computation.1 | async-start | bytes 4718592 | tf_op jit(solution)/shard_map/all_gather | solution.py:68
  40.2 234.9 %all-gather.5.cloned.1.call-start = ((), (), s32[]{:S(2)}) async-start(), calls=%async_computation.3 | async-start | bytes 4718592 | tf_op jit(solution)/shard_map/all_gather | solution.py:74
  40.9 194.1 %collective-permute-start.2 = (f32[2,256,256]{2,1,0:T(8,128)S(1)}, f32[2,256,256]{2,1,0:T(8,128)S(1)}, u32[]{:S(2)}, u32[]{:S(2)}) collective-permute-start(f32[2,256,256]{2,1,0:T(8,128)S(1)} %convolution_multiply_fusion), channel_id=1, source_target_pairs={{0,248},{8,0},{16,8},{24,16},{32,24},{40,32},{48,40},{56,48},{64,5... | collective-permute-start | bytes 1572872 | tf_op jit(solution)/shard_map/ppermute | solution.py:14
  236.0 111.7 %all-reduce.4.cloned.1.call-start = ((), (), s32[]{:S(2)}) async-start(), calls=%async_computation.2 | async-start | bytes 1048576 | tf_op jit(solution)/shard_map/psum | solution.py:71
  242.9 10.6 %copy-start.1 = (f32[2,256,256]{2,1,0:T(8,128)S(1)}, f32[2,256,256]{2,1,0:T(8,128)}, u32[]{:S(2)}) copy-start(f32[2,256,256]{2,1,0:T(8,128)} %convolution_multiply_fusion.1) | copy-start | bytes 1572868
  251.1 32.2 %copy-start.3 = (f32[2,256,256]{2,1,0:T(8,128)}, f32[2,256,256]{2,1,0:T(8,128)S(1)}, u32[]{:S(2)}) copy-start(f32[2,256,256]{2,1,0:T(8,128)S(1)} %fusion.3) | copy-start | bytes 1572868
  251.1 100.8 %collective-permute-start.1 = (f32[2,256,256]{2,1,0:T(8,128)S(1)}, f32[2,256,256]{2,1,0:T(8,128)S(1)}, u32[]{:S(2)}, u32[]{:S(2)}) collective-permute-start(f32[2,256,256]{2,1,0:T(8,128)S(1)} %fusion.3), channel_id=1, source_target_pairs={{0,8},{8,16},{16,24},{24,32},{32,40},{40,48},{48,56},{56,64},{64,7... | collective-permute-start | bytes 1572872 | tf_op jit(solution)/shard_map/ppermute | solution.py:14
  283.3 68.6 %collective-permute-start.3 = (f32[2,256,256]{2,1,0:T(8,128)}, f32[2,256,256]{2,1,0:T(8,128)}, u32[]{:S(2)}, u32[]{:S(2)}) collective-permute-start(f32[2,256,256]{2,1,0:T(8,128)} %fusion.1), channel_id=1, source_target_pairs={{0,8},{8,16},{16,24},{24,32},{32,40},{40,48},{48,56},{56,64},{64,7... | collective-permute-start | bytes 1572872 | tf_op jit(solution)/shard_map/ppermute | solution.py:14
  284.6 148.8 %all-reduce.6.cloned.1.call-start = ((), (), s32[]{:S(2)}) async-start(), calls=%async_computation.4 | async-start | bytes 2097152 | tf_op jit(solution)/shard_map/psum | solution.py:87
  350.6 15.0 %collective-permute-start = (f32[2,256,256]{2,1,0:T(8,128)}, f32[2,256,256]{2,1,0:T(8,128)}, u32[]{:S(2)}, u32[]{:S(2)}) collective-permute-start(f32[2,256,256]{2,1,0:T(8,128)} %convolution_subtract_fusion.1), channel_id=1, source_target_pairs={{0,8},{8,16},{16,24},{24,32},{32,40},{40,48},{48,56},{56,64},{64,7... | collective-permute-start | bytes 1572872 | tf_op jit(solution)/shard_map/ppermute | solution.py:14
  353.6 82.8 %copy-start.4 = (f32[2,256,256]{2,1,0:T(8,128)}, f32[2,256,256]{2,1,0:T(8,128)S(1)}, u32[]{:S(2)}) copy-start(f32[2,256,256]{2,1,0:T(8,128)S(1)} %fusion.2) | copy-start | bytes 1572868
  433.4 3.0 copy-start.6
  435.3 2.0 copy-start.5
Sparse Core Ops, SparseCore 0:
  41.8 36.7 all-gather.2
  236.1 38.9 all-gather.4
  284.7 62.9 all-reduce.3
  365.7 67.5 all-reduce.5

commit v2 on v1

--- a/solution.py
+++ b/solution.py
@@ -1,6 +1,8 @@
 import jax
 import jax.numpy as jnp
 from jax import lax
+from jax.experimental import pallas as pl
+from jax.experimental.pallas import tpu as pltpu
 from jax.sharding import PartitionSpec as P
 
 B = 256
@@ -14,8 +16,39 @@
     return lax.ppermute(shard, axis, [(i, (i + by) % length) for i in range(length)])
 
 
+def row_sum(x):
+    length = lax.axis_size("row")
+    step = 1
+    while step < length:
+        x = x + lax.ppermute(x, "row", [(i, i ^ step) for i in range(length)])
+        step *= 2
+    return x
+
+
 def product(form, left, right):
     return jnp.einsum(form, left, right, precision=HIGH)
+
+
+def _copy_block(rows_ref, cols_ref, src_ref, out_ref):
+    out_ref[0] = src_ref[...]
+
+
+def gather_blocks(src, rows, cols):
+    count = rows.shape[0]
+    grid_spec = pltpu.PrefetchScalarGridSpec(
+        num_scalar_prefetch=2,
+        grid=(count,),
+        in_specs=[pl.BlockSpec((B, B), lambda i, r, c: (r[i], c[i]))],
+        out_specs=pl.BlockSpec((1, B, B), lambda i, r, c: (i, 0, 0)),
+    )
+    return pl.pallas_call(
+        _copy_block,
+        out_shape=jax.ShapeDtypeStruct((count, B, B), src.dtype),
+        grid_spec=grid_spec,
+        cost_estimate=pl.CostEstimate(
+            flops=0, bytes_accessed=2 * count * B * B * 4, transcendentals=0
+        ),
+    )(rows, cols, src)
 
 
 def select_send(sigma_local, row_blocks, slots):
@@ -31,16 +64,17 @@
     match = ((local_col >= 0) & (local_col < cols_here)).astype(jnp.int32)
     which = jnp.sum(match * jnp.arange(slots, dtype=jnp.int32)[None, :], axis=1)
     chosen = rowlist[jnp.arange(own_count, dtype=jnp.int32), which]
-    chosen_row = (
-        lax.dynamic_index_in_dim(chosen, row_here, 1, keepdims=False) - row_here * rows_here
+    chosen_row = jnp.clip(
+        lax.dynamic_index_in_dim(chosen, row_here, 1, keepdims=False) - row_here * rows_here,
+        0,
+        rows_here - 1,
     )
     chosen_col = jnp.clip(
         lax.dynamic_index_in_dim(chosen, group, 1, keepdims=False) - own_here * cols_here,
         0,
         cols_here - 1,
     )
-    blocks4 = sigma_local.reshape(rows_here, B, cols_here, B)
-    return blocks4[chosen_row, :, chosen_col, :]
+    return gather_blocks(sigma_local, chosen_row, chosen_col)
 
 
 def select_take(received, row_blocks, slots, cols_here):
@@ -56,35 +90,39 @@
     slots = panel1.shape[0]
     cols_here = sigma_anc.shape[1] // B
     keep_own2 = mask2.astype(jnp.float32)
-    up_parent = product("kij,kjc->kic", parent_block2, diag_inv2)
     factor2_own = keep_own2[:, :, None] * product("kij,kjc->kic", panel2, diag_inv2)
     factor2_child = shifted(factor2_own, "own", -1)
 
     outgoing = select_send(sigma_anc, row_blocks, slots)
+    factor2_child, outgoing = lax.optimization_barrier((factor2_child, outgoing))
     received = lax.all_to_all(outgoing, "own", split_axis=0, concat_axis=0, tiled=True)
-    blocks1 = select_take(received, row_blocks, slots, cols_here)
+
     keep1 = mask1.astype(jnp.float32)
     factor1 = keep1[:, :, None] * product("kij,kjc->kic", panel1, diag_inv1)
-    factors1 = lax.all_gather(factor1, "row", axis=1, tiled=True).reshape(slots, -1, B, B)
-    sel1_panel = -keep1[:, :, None] * product("kmij,kmjc->kic", blocks1, factors1)
+    factor2 = keep1[:, :, None] * factor2_child
+    both = jnp.concatenate([factor1, factor2], axis=-1)
+    boths = lax.all_gather(both, "row", axis=1, tiled=True).reshape(slots, -1, B, 2 * B)
+
+    blocks1 = select_take(received, row_blocks, slots, cols_here)
+    kept = keep1[:, :, None] * product("kmij,kmjc->kic", blocks1, boths)
+    sel1_panel = -kept[:, :, :B]
     gram1 = product("kji,kjc->kic", diag_inv1, diag_inv1)
-    sel1_diag = gram1 - lax.psum(product("kji,kjc->kic", factor1, sel1_panel), "row")
+    sel1_diag = gram1 - row_sum(product("kji,kjc->kic", factor1, sel1_panel))
 
-    factor2 = keep1[:, :, None] * factor2_child
-    factors2 = lax.all_gather(factor2, "row", axis=1, tiled=True).reshape(slots, -1, B, B)
-    anc2 = keep1[:, :, None] * product("kmij,kmjc->kic", blocks1, factors2)
+    par_kept = shifted(kept, "own", 1)
+    par_diag = shifted(sel1_diag, "own", 1)
+    par_panel = -par_kept[:, :, :B]
+    par_anc = par_kept[:, :, B:]
 
-    par_panel = shifted(sel1_panel, "own", 1)
-    par_anc = shifted(anc2, "own", 1)
-    par_diag = shifted(sel1_diag, "own", 1)
-
+    up_parent = product("kij,kjc->kic", parent_block2, diag_inv2)
     sel2_panel = -keep_own2[:, :, None] * (
         product("kij,kjc->kic", par_panel, up_parent) + par_anc
     )
     cross = product("kji,kjc->kic", par_panel, factor2_own)
     back = product("kji,kjc->kic", factor2_own, sel2_panel)
-    par_diag, cross, back = lax.optimization_barrier((par_diag, cross, back))
-    cross, back = lax.psum((cross, back), "row")
+    summed = row_sum(jnp.concatenate([cross, back], axis=-1))
+    cross = summed[:, :, :B]
+    back = summed[:, :, B:]
     sel2_parent = -(product("kij,kjc->kic", par_diag, up_parent) + cross)
     gram2 = product("kji,kjc->kic", diag_inv2, diag_inv2)
     sel2_diag = gram2 - product("kji,kjc->kic", up_parent, sel2_parent) - back

time: 445 us -> 374 us (0.84)
  waiting for transfers between devices: 346 us -> 270 us
  Pallas kernels: 0 us -> 19.9 us
  local copies, waits for them, and re-layouts: 25.7 us -> 8.88 us
  matrix products: 34.3 us -> 21.8 us
  starting transfers between devices: 21.9 us -> 30.2 us
    all_to_all x1, waiting for transfers between devices: 0.01 us -> 185 us  [on_device(): lax.all_to_all(outgoing, 'own', split_axis=0, concat_axis=0, tiled=True)]
    ppermute x4 -> x3, waiting for transfers between devices: 198 us -> 20.3 us  [shifted(): lax.ppermute(shard, axis, [(i, (i + by) % length) for i in range(length)])]
    psum x2 -> x0, waiting for transfers between devices: 128 us -> none  [the longest x1 66.7 us: on_device(): cross, back = lax.psum((cross, back), 'row')]
    ppermute x0 -> x6, waiting for transfers between devices: none -> 64 us  [row_sum(): x = x + lax.ppermute(x, 'row', [(i, i ^ step) for i in range(length)])]
    pallas_call x0 -> x1, Pallas kernels: none -> 19.9 us  [gather_blocks(): pl.pallas_call(_copy_block, out_shape=jax.ShapeDtypeStruct((count, B, B),...]
    all_gather x2 -> x1, waiting for transfers between devices: 19.7 us -> 0.01 us  [on_device(): lax.all_gather(both, 'row', axis=1, tiled=True).reshape(slots, -1, B, 2 * B)]
    dot_general x13 -> x12, matrix products: 34.3 us -> 21.8 us  [product(): return jnp.einsum(form, left, right, precision=HIGH)]
    reshape x2 -> x0, local copies, waits for them, and re-layouts: 10.6 us -> none  [select_send(): blocks4 = sigma_local.reshape(rows_here, B, cols_here, B)]
  transfers between devices with their start and end apart: 9 -> 11, of which waited for: 5 -> 7; matrix products, arithmetic and copies ran while one was open for 9% -> 4% of each run, Pallas kernels for 0% -> 5%
where the time goes in v2:
time: 374 us; the launch traced here: 369 us
  waiting for transfers between devices  270 us (72%)
  starting transfers between devices  30.2 us (8%)
  matrix products  21.8 us (6%)
  Pallas kernels  19.9 us (5%)
  between operations  14.3 us (4%)
  local copies, waits for them, and re-layouts  8.88 us (2%)
  other arithmetic  3.94 us (1%)
    all_to_all x1, waiting for transfers between devices, on_device(): lax.all_to_all(outgoing, 'own', split_axis=0, concat_axis=0, tiled=True)  185 us
    ppermute x6, waiting for transfers between devices, row_sum(): x = x + lax.ppermute(x, 'row', [(i, i ^ step) for i in range(length)])  64 us
    dot_general x12, matrix products, product(): return jnp.einsum(form, left, right, precision=HIGH)  21.8 us
    ppermute x3, waiting for transfers between devices, shifted(): lax.ppermute(shard, axis, [(i, (i + by) % length) for i in range(length)])  20.3 us
    pallas_call x1, Pallas kernels, gather_blocks(): pl.pallas_call(_copy_block, out_shape=jax.ShapeDtypeStruct((count, B, B),...  19.9 us
    ppermute x3, starting transfers between devices, shifted(): lax.ppermute(shard, axis, [(i, (i + by) % length) for i in range(length)])  18.1 us
  transfers between devices with their start and end apart: 11, of which 7 were waited for; matrix products, arithmetic and copies ran while one was open for 4% of the time, Pallas kernels for 5%

profile of v2, /device:TPU:1, one launch (start us, length us, event | category | flops | bytes accessed | tf_op | source)
XLA Modules:
  0.0 368.6 jit_solution(5635075497474936140)
XLA Ops:
  7.2 0.0 copy-start
  7.2 0.7 convert_bitcast_fusion
  7.9 0.3 copy-done
  8.2 1.7 convolution_multiply_fusion.1
  9.9 8.7 %collective-permute-start = (f32[2,256,256]{2,1,0:T(8,128)S(1)}, f32[2,256,256]{2,1,0:T(8,128)S(1)}, u32[]{:S(2)}, u32[]{:S(2)}) collective-permute-start(f32[2,256,256]{2,1,0:T(8,128)S(1)} %convolution_multiply_fusion.1), channel_id=1, source_target_pairs={{0,248},{8,0},{16,8},{24,16},{32,24},{40,32},{48,40},{56,48},{64,5... | collective-permute-start | bytes 1572872 | tf_op jit(solution)/shard_map/ppermute | solution.py:16
  18.6 0.8 copy.61
  19.4 0.1 constant_dynamic-slice_fusion
  19.5 0.1 copy.88
  19.6 0.1 copy.63
  19.7 0.1 fusion.8
  19.8 0.7 gather_fusion
  20.5 0.7 clamp_reduce_fusion
  21.2 19.9 %shard_map.128 = f32[32,256,256]{2,1,0:T(8,128)} custom-call(s32[32]{0:T(128)} %get-tuple-element.10.rows_ref, s32[32]{0:T(128)} %get-tuple-element.9.cols_ref, f32[2048,512]{1,0:T(8,128)} %src_ref.1), custom_call_target="tpu_custom_call" | custom-call | bytes 16777216 | tf_op jit(solution)/shard_map/pallas_call | solution.py:44
  41.1 0.0 collective-permute-done
  41.1 5.1 %all-to-all-start = ((f32[32,256,256]{2,1,0:T(8,128)}), f32[32,256,256]{2,1,0:T(8,128)}, u32[]{:S(2)}, u32[]{:S(2)}) async-start(f32[32,256,256]{2,1,0:T(8,128)} %shard_map.128), calls=%async_computation | async-start | bytes 16777216 | tf_op jit(solution)/shard_map/all_to_all | solution.py:98
  46.2 0.0 all-gather.2.cloned.1.call-start
  46.3 0.7 convolution_multiply_fusion
  47.0 0.1 broadcast_multiply_fusion
  47.1 1.2 pad_maximum_fusion
  48.3 0.0 all-gather.2.cloned.1.call-update
  48.4 0.6 gather_fusion.1
  48.9 0.1 reshape.147
  49.0 185.2 %all-to-all-done = f32[32,256,256]{2,1,0:T(8,128)} async-done(((f32[32,256,256]{2,1,0:T(8,128)}), f32[32,256,256]{2,1,0:T(8,128)}, u32[]{:S(2)}, u32[]{:S(2)}) %all-to-all-start) | async-done | bytes 8388640 | tf_op jit(solution)/shard_map/all_to_all | solution.py:98
  234.3 6.1 %gather_fusion.2 = f32[16,256,256]{2,1,0:T(8,128)} fusion(f32[32,256,256]{2,1,0:T(8,128)} %all-to-all-done, s32[1024]{0:T(1024)S(1)} %pad_clamp_fusion), kind=kCustom, calls=%fused_computation.2 | custom fusion | bytes 8388672 | tf_op jit(solution)/shard_map/gather | solution.py:84
  240.4 10.3 %fusion = f32[2,256,512]{2,1,0:T(8,128)S(1)} fusion(f32[2,8,256,256]{3,2,1,0:T(8,128)} %bitcast.55, f32[2,8,256,512]{3,2,1,0:T(8,128)} %bitcast.56, f32[2]{0:T(128)S(1)} %convert_bitcast_fusion.1), kind=kOutput, calls=%fused_computation.4 | convolution fusion | flops 6442713088 | bytes 13631496 | tf_op jit(solution)/shard_map/kmij,kmjc->kic/dot_general | solution.py:29
  250.7 7.1 %collective-permute-start.5 = (f32[2,256,512]{2,1,0:T(8,128)S(1)}, f32[2,256,512]{2,1,0:T(8,128)S(1)}, u32[]{:S(2)}, u32[]{:S(2)}) collective-permute-start(f32[2,256,512]{2,1,0:T(8,128)S(1)} %fusion), channel_id=1, source_target_pairs={{0,8},{8,16},{16,24},{24,32},{32,40},{40,48},{48,56},{56,64},{64,7... | collective-permute-start | bytes 3145736 | tf_op jit(solution)/shard_map/ppermute | solution.py:16
  257.8 0.7 fusion.15
  258.5 20.3 %collective-permute-done.5 = f32[2,256,512]{2,1,0:T(8,128)S(1)} collective-permute-done((f32[2,256,512]{2,1,0:T(8,128)S(1)}, f32[2,256,512]{2,1,0:T(8,128)S(1)}, u32[]{:S(2)}, u32[]{:S(2)}) %collective-permute-start.5) | collective-permute-done | bytes 1048608 | tf_op jit(solution)/shard_map/ppermute | solution.py:16
  278.8 0.7 fusion.2
  279.5 0.0 copy-start.2
  279.5 1.1 fusion.16
  280.6 1.1 fusion.4
  281.7 0.1 pad_maximum_fusion.1
  281.8 2.6 collective-permute-start.6
  284.4 0.1 slice_negate_fusion.1
  284.5 0.0 copy-start.3
  284.5 1.1 fusion.14
  285.6 0.1 collective-permute-start.1
  285.7 1.1 collective-permute-done.6
  286.7 0.2 fusion.12
  286.9 0.0 copy-done.2
  286.9 0.1 collective-permute-start.7
  287.0 0.6 collective-permute-done.1
  287.6 0.1 add.98
  287.6 1.0 collective-permute-start.2
  288.6 34.0 %collective-permute-done.2 = f32[2,256,256]{2,1,0:T(8,128)S(1)} collective-permute-done((f32[2,256,256]{2,1,0:T(8,128)S(1)}, f32[2,256,256]{2,1,0:T(8,128)S(1)}, u32[]{:S(2)}, u32[]{:S(2)}) %collective-permute-start.2) | collective-permute-done | bytes 524320 | tf_op jit(solution)/shard_map/ppermute | solution.py:23
  322.6 0.1 add.99
  322.7 0.7 collective-permute-start.3
  323.4 0.0 collective-permute-done.7
  323.4 0.2 add.103
  323.6 2.4 collective-permute-start.8
  326.0 1.1 fusion.13
  327.1 9.4 %collective-permute-done.3 = f32[2,256,256]{2,1,0:T(8,128)S(1)} collective-permute-done((f32[2,256,256]{2,1,0:T(8,128)S(1)}, f32[2,256,256]{2,1,0:T(8,128)S(1)}, u32[]{:S(2)}, u32[]{:S(2)}) %collective-permute-start.3) | collective-permute-done | bytes 524320 | tf_op jit(solution)/shard_map/ppermute | solution.py:23
  336.5 0.1 add_subtract_fusion
  336.6 0.0 copy-start.7
  336.6 2.3 collective-permute-start.4
  338.9 1.1 fusion.17
  339.9 19.0 %collective-permute-done.8 = f32[2,256,512]{2,1,0:T(8,128)S(1)} collective-permute-done((f32[2,256,512]{2,1,0:T(8,128)S(1)}, f32[2,256,512]{2,1,0:T(8,128)S(1)}, u32[]{:S(2)}, u32[]{:S(2)}) %collective-permute-start.8) | collective-permute-done | bytes 1048608 | tf_op jit(solution)/shard_map/ppermute | solution.py:23
  358.9 0.2 add.104
  359.2 0.0 collective-permute-done.4
  359.2 0.7 fusion.3
  359.8 0.0 copy-start.4
  359.9 1.9 fusion.1
  361.7 0.0 copy-done.4
  (20 shorter events, 0.1 us)
Async XLA Ops:
  7.2 1.1 copy-start
  9.9 31.2 %collective-permute-start = (f32[2,256,256]{2,1,0:T(8,128)S(1)}, f32[2,256,256]{2,1,0:T(8,128)S(1)}, u32[]{:S(2)}, u32[]{:S(2)}) collective-permute-start(f32[2,256,256]{2,1,0:T(8,128)S(1)} %convolution_multiply_fusion.1), channel_id=1, source_target_pairs={{0,248},{8,0},{16,8},{24,16},{32,24},{40,32},{48,40},{56,48},{64,5... | collective-permute-start | bytes 1572872 | tf_op jit(solution)/shard_map/ppermute | solution.py:16
  41.1 5.2 %copy-start.8 = (s32[2,1]{0,1:T(1,128)S(1)}, s32[2,1]{0,1:T(1,128)}, u32[]{:S(2)}) copy-start(s32[2,1]{0,1:T(1,128)} %param.13) | copy-start | bytes 28
  41.1 5.2 %copy-start.1 = (f32[2,256,256]{2,1,0:T(8,128)S(1)}, f32[2,256,256]{2,1,0:T(8,128)}, u32[]{:S(2)}) copy-start(f32[2,256,256]{2,1,0:T(8,128)} %param.12) | copy-start | bytes 1572868
  41.1 5.2 %copy-start.6 = (f32[2,256,256]{2,1,0:T(8,128)S(1)}, f32[2,256,256]{2,1,0:T(8,128)}, u32[]{:S(2)}) copy-start(f32[2,256,256]{2,1,0:T(8,128)} %param.11) | copy-start | bytes 1572868
  41.1 193.2 %all-to-all-start = ((f32[32,256,256]{2,1,0:T(8,128)}), f32[32,256,256]{2,1,0:T(8,128)}, u32[]{:S(2)}, u32[]{:S(2)}) async-start(f32[32,256,256]{2,1,0:T(8,128)} %shard_map.128), calls=%async_computation | async-start | bytes 16777216 | tf_op jit(solution)/shard_map/all_to_all | solution.py:98
  46.2 194.2 %all-gather.2.cloned.1.call-start = ((), (), s32[]{:S(2)}) async-start(), calls=%async_computation.1 | async-start | bytes 9437184 | tf_op jit(solution)/shard_map/all_gather | solution.py:104
  240.4 17.4 %copy-start.9 = (s32[2,1]{0,1:T(1,128)S(1)}, s32[2,1]{0,1:T(1,128)}, u32[]{:S(2)}) copy-start(s32[2,1]{0,1:T(1,128)} %param.17) | copy-start | bytes 28
  240.4 17.4 %copy-start.5 = (f32[2,256,256]{2,1,0:T(8,128)S(1)}, f32[2,256,256]{2,1,0:T(8,128)}, u32[]{:S(2)}) copy-start(f32[2,256,256]{2,1,0:T(8,128)} %param.14) | copy-start | bytes 1572868
  250.7 28.1 %collective-permute-start.5 = (f32[2,256,512]{2,1,0:T(8,128)S(1)}, f32[2,256,512]{2,1,0:T(8,128)S(1)}, u32[]{:S(2)}, u32[]{:S(2)}) collective-permute-start(f32[2,256,512]{2,1,0:T(8,128)S(1)} %fusion), channel_id=1, source_target_pairs={{0,8},{8,16},{16,24},{24,32},{32,40},{40,48},{48,56},{56,64},{64,7... | collective-permute-start | bytes 3145736 | tf_op jit(solution)/shard_map/ppermute | solution.py:16
  279.5 7.4 %copy-start.2 = (f32[2,256,256]{2,1,0:T(8,128)}, f32[2,256,256]{2,1,0:T(8,128)S(1)}, u32[]{:S(2)}) copy-start(f32[2,256,256]{2,1,0:T(8,128)S(1)} %fusion.2) | copy-start | bytes 1572868
  281.8 4.9 %collective-permute-start.6 = (f32[2,256,512]{2,1,0:T(8,128)S(1)}, f32[2,256,512]{2,1,0:T(8,128)S(1)}, u32[]{:S(2)}, u32[]{:S(2)}) collective-permute-start(f32[2,256,512]{2,1,0:T(8,128)S(1)} %pad_maximum_fusion.1), channel_id=1, source_target_pairs={{0,1},{1,0},{2,3},{3,2},{4,5},{5,4},{6,7},{7,6},{8,9},{9,8},{10,11... | collective-permute-start | bytes 3145736 | tf_op jit(solution)/shard_map/ppermute | solution.py:23
  284.5 39.1 %copy-start.3 = (f32[2,256,256]{2,1,0:T(8,128)}, f32[2,256,256]{2,1,0:T(8,128)S(1)}, u32[]{:S(2)}) copy-start(f32[2,256,256]{2,1,0:T(8,128)S(1)} %slice_negate_fusion.1) | copy-start | bytes 1572868
  285.6 2.0 collective-permute-start.1
  286.9 36.5 %collective-permute-start.7 = (f32[2,256,512]{2,1,0:T(8,128)S(1)}, f32[2,256,512]{2,1,0:T(8,128)S(1)}, u32[]{:S(2)}, u32[]{:S(2)}) collective-permute-start(f32[2,256,512]{2,1,0:T(8,128)S(1)} %fusion.12), channel_id=1, source_target_pairs={{0,2},{1,3},{2,0},{3,1},{4,6},{5,7},{6,4},{7,5},{8,10},{9,11},{10,... | collective-permute-start | bytes 3145736 | tf_op jit(solution)/shard_map/ppermute | solution.py:23
  287.6 35.0 %collective-permute-start.2 = (f32[2,256,256]{2,1,0:T(8,128)S(1)}, f32[2,256,256]{2,1,0:T(8,128)S(1)}, u32[]{:S(2)}, u32[]{:S(2)}) collective-permute-start(f32[2,256,256]{2,1,0:T(8,128)S(1)} %add.98), channel_id=1, source_target_pairs={{0,2},{1,3},{2,0},{3,1},{4,6},{5,7},{6,4},{7,5},{8,10},{9,11},{10,... | collective-permute-start | bytes 1572872 | tf_op jit(solution)/shard_map/ppermute | solution.py:23
  322.7 13.8 %collective-permute-start.3 = (f32[2,256,256]{2,1,0:T(8,128)S(1)}, f32[2,256,256]{2,1,0:T(8,128)S(1)}, u32[]{:S(2)}, u32[]{:S(2)}) collective-permute-start(f32[2,256,256]{2,1,0:T(8,128)S(1)} %add.99), channel_id=1, source_target_pairs={{0,4},{1,5},{2,6},{3,7},{4,0},{5,1},{6,2},{7,3},{8,12},{9,13},{10,... | collective-permute-start | bytes 1572872 | tf_op jit(solution)/shard_map/ppermute | solution.py:23
  323.6 35.3 %collective-permute-start.8 = (f32[2,256,512]{2,1,0:T(8,128)S(1)}, f32[2,256,512]{2,1,0:T(8,128)S(1)}, u32[]{:S(2)}, u32[]{:S(2)}) collective-permute-start(f32[2,256,512]{2,1,0:T(8,128)S(1)} %add.103), channel_id=1, source_target_pairs={{0,4},{1,5},{2,6},{3,7},{4,0},{5,1},{6,2},{7,3},{8,12},{9,13},{10,... | collective-permute-start | bytes 3145736 | tf_op jit(solution)/shard_map/ppermute | solution.py:23
  336.6 25.1 %copy-start.7 = (f32[2,256,256]{2,1,0:T(8,128)}, f32[2,256,256]{2,1,0:T(8,128)S(1)}, u32[]{:S(2)}) copy-start(f32[2,256,256]{2,1,0:T(8,128)S(1)} %add_subtract_fusion) | copy-start | bytes 1572868
  336.6 22.6 %collective-permute-start.4 = (f32[2,256,256]{2,1,0:T(8,128)S(1)}, f32[2,256,256]{2,1,0:T(8,128)S(1)}, u32[]{:S(2)}, u32[]{:S(2)}) collective-permute-start(f32[2,256,256]{2,1,0:T(8,128)S(1)} %add_subtract_fusion), channel_id=1, source_target_pairs={{0,8},{8,16},{16,24},{24,32},{32,40},{40,48},{48,56},{56,64},{64,7... | collective-permute-start | bytes 1572872 | tf_op jit(solution)/shard_map/ppermute | solution.py:16
  359.8 1.9 copy-start.4
Sparse Core Ops, SparseCore 0:
  48.9 54.3 all-gather.1

commit v3 on v2

--- a/solution.py
+++ b/solution.py
@@ -18,35 +18,64 @@
 
 def row_sum(x):
     length = lax.axis_size("row")
-    step = 1
+    core = lax.axis_index("row") % 2
+    half = x.shape[1] // 2
+    lo, hi = x[:, :half], x[:, half:]
+    mine = jnp.where(core == 0, lo, hi)
+    other = jnp.where(core == 0, hi, lo)
+    partner = [(i, i ^ 1) for i in range(length)]
+    part = mine + lax.ppermute(other, "row", partner)
+    step = 2
     while step < length:
-        x = x + lax.ppermute(x, "row", [(i, i ^ step) for i in range(length)])
+        part = part + lax.ppermute(part, "row", [(i, i ^ step) for i in range(length)])
         step *= 2
-    return x
+    got = lax.ppermute(part, "row", partner)
+    return jnp.where(
+        core == 0, jnp.concatenate([part, got], axis=1), jnp.concatenate([got, part], axis=1)
+    )
 
 
 def product(form, left, right):
     return jnp.einsum(form, left, right, precision=HIGH)
 
 
-def _copy_block(rows_ref, cols_ref, src_ref, out_ref):
-    out_ref[0] = src_ref[...]
+def _copy_blocks(rows_ref, cols_ref, src_ref, out_ref, staged, sem_in, sems_out):
+    load = pltpu.make_async_copy(src_ref, staged, sem_in)
+    load.start()
+    load.wait()
+    count = out_ref.shape[0]
+    copies = []
+    for i in range(count):
+        copy = pltpu.make_async_copy(
+            staged.at[pl.ds(rows_ref[i] * B, B), pl.ds(pl.multiple_of(cols_ref[i] * B, B), B)],
+            out_ref.at[i],
+            sems_out.at[i],
+        )
+        copy.start()
+        copies.append(copy)
+    for copy in copies:
+        copy.wait()
 
 
 def gather_blocks(src, rows, cols):
     count = rows.shape[0]
     grid_spec = pltpu.PrefetchScalarGridSpec(
         num_scalar_prefetch=2,
-        grid=(count,),
-        in_specs=[pl.BlockSpec((B, B), lambda i, r, c: (r[i], c[i]))],
-        out_specs=pl.BlockSpec((1, B, B), lambda i, r, c: (i, 0, 0)),
+        grid=(),
+        in_specs=[pl.BlockSpec(memory_space=pl.ANY)],
+        out_specs=pl.BlockSpec(memory_space=pl.ANY),
+        scratch_shapes=[
+            pltpu.VMEM(src.shape, src.dtype),
+            pltpu.SemaphoreType.DMA(()),
+            pltpu.SemaphoreType.DMA((count,)),
+        ],
     )
     return pl.pallas_call(
-        _copy_block,
+        _copy_blocks,
         out_shape=jax.ShapeDtypeStruct((count, B, B), src.dtype),
         grid_spec=grid_spec,
         cost_estimate=pl.CostEstimate(
-            flops=0, bytes_accessed=2 * count * B * B * 4, transcendentals=0
+            flops=0, bytes_accessed=(src.size + count * B * B) * 4, transcendentals=0
         ),
     )(rows, cols, src)
 

time: 374 us -> 346 us (0.925); the launches traced: 369 us -> 345 us
  Pallas kernels: 19.9 us -> 6.37 us
  waiting for transfers between devices: 270 us -> 259 us
    ppermute x6 -> x8, waiting for transfers between devices: 64 us -> 34.1 us  [the longest x4 32.9 us: row_sum(): lax.ppermute(part, 'row', [(i, i ^ step) for i in range(length)])]
    ppermute x3, waiting for transfers between devices: 20.3 us -> 46 us  [shifted(): lax.ppermute(shard, axis, [(i, (i + by) % length) for i in range(length)])]
    pallas_call x1, Pallas kernels: 19.9 us -> 6.37 us  [gather_blocks(): pl.pallas_call(_copy_blocks, out_shape=jax.ShapeDtypeStruct((count, B, B)...]
    ppermute x3, starting transfers between devices: 18.1 us -> 11.2 us  [shifted(): lax.ppermute(shard, axis, [(i, (i + by) % length) for i in range(length)])]
    all_to_all x1, waiting for transfers between devices: 185 us -> 179 us  [on_device(): lax.all_to_all(outgoing, 'own', split_axis=0, concat_axis=0, tiled=True)]
    ppermute x6 -> x8, starting transfers between devices: 6.96 us -> 9.07 us  [the longest x4 5.35 us: row_sum(): lax.ppermute(part, 'row', [(i, i ^ step) for i in range(length)])]
  transfers between devices with their start and end apart: 11 -> 13, of which waited for: 7 -> 8; matrix products, arithmetic and copies ran while one was open for 4% -> 5% of each run, Pallas kernels for 5% -> 2%
where the time goes in v3:
time: 346 us; the launch traced here: 345 us
  waiting for transfers between devices  259 us (75%)
  starting transfers between devices  27.6 us (8%)
  matrix products  25 us (7%)
  between operations  14.4 us (4%)
  local copies, waits for them, and re-layouts  8.89 us (3%)
  Pallas kernels  6.37 us (2%)
  other arithmetic  3.59 us (1%)
    all_to_all x1, waiting for transfers between devices, on_device(): lax.all_to_all(outgoing, 'own', split_axis=0, concat_axis=0, tiled=True)  179 us
    ppermute x3, waiting for transfers between devices, shifted(): lax.ppermute(shard, axis, [(i, (i + by) % length) for i in range(length)])  46 us
    ppermute x4, waiting for transfers between devices, row_sum(): lax.ppermute(part, 'row', [(i, i ^ step) for i in range(length)])  32.9 us
    dot_general x12, matrix products, product(): return jnp.einsum(form, left, right, precision=HIGH)  25 us
    ppermute x3, starting transfers between devices, shifted(): lax.ppermute(shard, axis, [(i, (i + by) % length) for i in range(length)])  11.2 us
    all_to_all x1, starting transfers between devices, on_device(): lax.all_to_all(outgoing, 'own', split_axis=0, concat_axis=0, tiled=True)  7.32 us
  transfers between devices with their start and end apart: 13, of which 8 were waited for; matrix products, arithmetic and copies ran while one was open for 5% of the time, Pallas kernels for 2%

profile of v3, /device:TPU:1, one launch (start us, length us, event | category | flops | bytes accessed | tf_op | source)
XLA Modules:
  0.0 345.2 jit_solution(15951450371168322979)
XLA Ops:
  7.2 0.0 copy-start
  7.2 0.7 convert_bitcast_fusion
  7.9 0.3 copy-done
  8.2 1.7 convolution_multiply_fusion.1
  9.9 8.7 %collective-permute-start = (f32[2,256,256]{2,1,0:T(8,128)S(1)}, f32[2,256,256]{2,1,0:T(8,128)S(1)}, u32[]{:S(2)}, u32[]{:S(2)}) collective-permute-start(f32[2,256,256]{2,1,0:T(8,128)S(1)} %convolution_multiply_fusion.1), channel_id=1, source_target_pairs={{0,248},{8,0},{16,8},{24,16},{32,24},{40,32},{48,40},{56,48},{64,5... | collective-permute-start | bytes 1572872 | tf_op jit(solution)/shard_map/ppermute | solution.py:16
  18.6 0.8 copy.61
  19.4 0.1 constant_dynamic-slice_fusion
  19.5 0.1 copy.88
  19.6 0.1 copy.63
  19.7 0.1 fusion.9
  19.8 0.7 gather_fusion
  20.5 0.7 clamp_reduce_fusion
  21.2 6.4 %shard_map.128 = f32[32,256,256]{2,1,0:T(8,128)} custom-call(s32[32]{0:T(128)} %get-tuple-element.10.rows_ref, s32[32]{0:T(128)} %get-tuple-element.9.cols_ref, f32[2048,512]{1,0:T(8,128)} %src_ref.1), custom_call_target="tpu_custom_call" | custom-call | bytes 12582912 | tf_op jit(solution)/shard_map/pallas_call | solution.py:73
  27.6 0.0 copy-start.7
  27.6 0.0 copy-start.1
  27.6 0.0 copy-start.6
  27.6 1.6 collective-permute-done
  29.2 7.3 %all-to-all-start = ((f32[32,256,256]{2,1,0:T(8,128)}), f32[32,256,256]{2,1,0:T(8,128)}, u32[]{:S(2)}, u32[]{:S(2)}) async-start(f32[32,256,256]{2,1,0:T(8,128)} %shard_map.128), calls=%async_computation | async-start | bytes 16777216 | tf_op jit(solution)/shard_map/all_to_all | solution.py:127
  36.5 0.0 all-gather.2.cloned.1.call-start
  36.6 0.7 convolution_multiply_fusion
  37.3 0.1 broadcast_multiply_fusion
  37.4 1.2 pad_maximum_fusion
  38.6 0.0 all-gather.2.cloned.1.call-update
  38.7 0.6 gather_fusion.1
  39.2 0.1 reshape.147
  39.3 179.3 %all-to-all-done = f32[32,256,256]{2,1,0:T(8,128)} async-done(((f32[32,256,256]{2,1,0:T(8,128)}), f32[32,256,256]{2,1,0:T(8,128)}, u32[]{:S(2)}, u32[]{:S(2)}) %all-to-all-start) | async-done | bytes 8388640 | tf_op jit(solution)/shard_map/all_to_all | solution.py:127
  218.6 6.1 %gather_fusion.2 = f32[16,256,256]{2,1,0:T(8,128)} fusion(f32[32,256,256]{2,1,0:T(8,128)} %all-to-all-done, s32[1024]{0:T(1024)S(1)} %pad_clamp_fusion), kind=kCustom, calls=%fused_computation.2 | custom fusion | bytes 8388672 | tf_op jit(solution)/shard_map/gather | solution.py:113
  224.7 10.2 %fusion = f32[2,256,512]{2,1,0:T(8,128)S(1)} fusion(f32[2,8,256,256]{3,2,1,0:T(8,128)} %bitcast.55, f32[2,8,256,512]{3,2,1,0:T(8,128)} %bitcast.56, f32[2]{0:T(128)S(1)} %convert_bitcast_fusion.1), kind=kOutput, calls=%fused_computation.4 | convolution fusion | flops 6442713088 | bytes 13631496 | tf_op jit(solution)/shard_map/kmij,kmjc->kic/dot_general | solution.py:39
  235.0 2.5 collective-permute-start.6
  237.4 1.7 fusion.14
  239.1 29.2 %collective-permute-done.6 = f32[2,256,512]{2,1,0:T(8,128)} collective-permute-done((f32[2,256,512]{2,1,0:T(8,128)S(1)}, f32[2,256,512]{2,1,0:T(8,128)}, u32[]{:S(2)}, u32[]{:S(2)}) %collective-permute-start.6) | collective-permute-done | bytes 1048608 | tf_op jit(solution)/shard_map/ppermute | solution.py:16
  268.3 1.9 fusion.1
  270.2 0.0 copy-start.2
  270.2 1.0 fusion.15
  271.3 2.1 fusion.5
  273.4 0.1 broadcast_select_fusion
  273.4 1.3 collective-permute-start.7
  274.7 0.1 slice_negate_fusion.1
  274.8 0.0 copy-start.3
  274.8 1.0 fusion.13
  275.9 0.1 collective-permute-start.1
  276.0 0.3 collective-permute-done.7
  276.3 0.1 select_add_fusion
  276.4 1.2 collective-permute-start.8
  277.5 0.1 select_add_fusion.1
  277.6 1.1 collective-permute-start.2
  278.7 16.5 %collective-permute-done.2 = f32[2,128,256]{2,1,0:T(8,128)S(1)} collective-permute-done((f32[2,128,256]{2,1,0:T(8,128)S(1)}, f32[2,128,256]{2,1,0:T(8,128)S(1)}, u32[]{:S(2)}, u32[]{:S(2)}) %collective-permute-start.2) | collective-permute-done | bytes 262176 | tf_op jit(solution)/shard_map/ppermute | solution.py:30
  295.3 0.1 add.109
  295.3 2.8 collective-permute-start.9
  298.1 0.3 collective-permute-start.3
  298.4 16.4 %collective-permute-done.3 = f32[2,128,256]{2,1,0:T(8,128)S(1)} collective-permute-done((f32[2,128,256]{2,1,0:T(8,128)S(1)}, f32[2,128,256]{2,1,0:T(8,128)S(1)}, u32[]{:S(2)}, u32[]{:S(2)}) %collective-permute-start.3) | collective-permute-done | bytes 262176 | tf_op jit(solution)/shard_map/ppermute | solution.py:30
  314.8 2.2 collective-permute-start.4
  317.0 0.1 add.110
  317.1 0.1 collective-permute-start.10
  317.2 1.0 collective-permute-done.4
  318.2 1.1 fusion.4
  319.3 0.0 copy-start.5
  319.3 0.1 collective-permute-start.5
  319.4 1.1 fusion.16
  320.4 0.1 maximum_select_fusion
  320.6 15.2 %collective-permute-done.5 = f32[2,256,256]{2,1,0:T(8,128)S(1)} collective-permute-done((f32[2,256,256]{2,1,0:T(8,128)S(1)}, f32[2,256,256]{2,1,0:T(8,128)S(1)}, u32[]{:S(2)}, u32[]{:S(2)}) %collective-permute-start.5) | collective-permute-done | bytes 524320 | tf_op jit(solution)/shard_map/ppermute | solution.py:16
  335.8 0.7 fusion.2
  336.5 0.0 copy-start.4
  336.5 1.9 slice_subtract_fusion
  (24 shorter events, 0.2 us)
Async XLA Ops:
  7.2 1.1 copy-start
  9.9 19.3 %collective-permute-start = (f32[2,256,256]{2,1,0:T(8,128)S(1)}, f32[2,256,256]{2,1,0:T(8,128)S(1)}, u32[]{:S(2)}, u32[]{:S(2)}) collective-permute-start(f32[2,256,256]{2,1,0:T(8,128)S(1)} %convolution_multiply_fusion.1), channel_id=1, source_target_pairs={{0,248},{8,0},{16,8},{24,16},{32,24},{40,32},{48,40},{56,48},{64,5... | collective-permute-start | bytes 1572872 | tf_op jit(solution)/shard_map/ppermute | solution.py:16
  27.6 9.0 %copy-start.7 = (s32[2,1]{0,1:T(1,128)S(1)}, s32[2,1]{0,1:T(1,128)}, u32[]{:S(2)}) copy-start(s32[2,1]{0,1:T(1,128)} %param.13) | copy-start | bytes 28
  27.6 9.0 %copy-start.1 = (f32[2,256,256]{2,1,0:T(8,128)S(1)}, f32[2,256,256]{2,1,0:T(8,128)}, u32[]{:S(2)}) copy-start(f32[2,256,256]{2,1,0:T(8,128)} %param.12) | copy-start | bytes 1572868
  27.6 9.0 %copy-start.6 = (f32[2,256,256]{2,1,0:T(8,128)S(1)}, f32[2,256,256]{2,1,0:T(8,128)}, u32[]{:S(2)}) copy-start(f32[2,256,256]{2,1,0:T(8,128)} %param.11) | copy-start | bytes 1572868
  29.2 189.4 %all-to-all-start = ((f32[32,256,256]{2,1,0:T(8,128)}), f32[32,256,256]{2,1,0:T(8,128)}, u32[]{:S(2)}, u32[]{:S(2)}) async-start(f32[32,256,256]{2,1,0:T(8,128)} %shard_map.128), calls=%async_computation | async-start | bytes 16777216 | tf_op jit(solution)/shard_map/all_to_all | solution.py:127
  36.5 188.2 %all-gather.2.cloned.1.call-start = ((), (), s32[]{:S(2)}) async-start(), calls=%async_computation.1 | async-start | bytes 9437184 | tf_op jit(solution)/shard_map/all_gather | solution.py:133
  224.7 12.7 %copy-start.8 = (s32[2,1]{0,1:T(1,128)S(1)}, s32[2,1]{0,1:T(1,128)}, u32[]{:S(2)}) copy-start(s32[2,1]{0,1:T(1,128)} %param.17) | copy-start | bytes 28
  235.0 33.4 %collective-permute-start.6 = (f32[2,256,512]{2,1,0:T(8,128)S(1)}, f32[2,256,512]{2,1,0:T(8,128)}, u32[]{:S(2)}, u32[]{:S(2)}) collective-permute-start(f32[2,256,512]{2,1,0:T(8,128)S(1)} %fusion), channel_id=1, source_target_pairs={{0,8},{8,16},{16,24},{24,32},{32,40},{40,48},{48,56},{56,64},{64,7... | collective-permute-start | bytes 3145736 | tf_op jit(solution)/shard_map/ppermute | solution.py:16
  270.2 6.2 %copy-start.2 = (f32[2,256,256]{2,1,0:T(8,128)}, f32[2,256,256]{2,1,0:T(8,128)S(1)}, u32[]{:S(2)}) copy-start(f32[2,256,256]{2,1,0:T(8,128)S(1)} %fusion.1) | copy-start | bytes 1572868
  273.4 2.8 collective-permute-start.7
  274.8 40.0 %copy-start.3 = (f32[2,256,256]{2,1,0:T(8,128)}, f32[2,256,256]{2,1,0:T(8,128)S(1)}, u32[]{:S(2)}) copy-start(f32[2,256,256]{2,1,0:T(8,128)S(1)} %slice_negate_fusion.1) | copy-start | bytes 1572868
  275.9 1.6 collective-permute-start.1
  276.4 18.9 %collective-permute-start.8 = (f32[2,128,512]{2,1,0:T(8,128)S(1)}, f32[2,128,512]{2,1,0:T(8,128)S(1)}, u32[]{:S(2)}, u32[]{:S(2)}) collective-permute-start(f32[2,128,512]{2,1,0:T(8,128)S(1)} %select_add_fusion), channel_id=1, source_target_pairs={{0,2},{1,3},{2,0},{3,1},{4,6},{5,7},{6,4},{7,5},{8,10},{9,11},{10,... | collective-permute-start | bytes 1572872 | tf_op jit(solution)/shard_map/ppermute | solution.py:30
  277.6 17.6 %collective-permute-start.2 = (f32[2,128,256]{2,1,0:T(8,128)S(1)}, f32[2,128,256]{2,1,0:T(8,128)S(1)}, u32[]{:S(2)}, u32[]{:S(2)}) collective-permute-start(f32[2,128,256]{2,1,0:T(8,128)S(1)} %select_add_fusion.1), channel_id=1, source_target_pairs={{0,2},{1,3},{2,0},{3,1},{4,6},{5,7},{6,4},{7,5},{8,10},{9,11},{10,... | collective-permute-start | bytes 786440 | tf_op jit(solution)/shard_map/ppermute | solution.py:30
  295.3 21.7 %collective-permute-start.9 = (f32[2,128,512]{2,1,0:T(8,128)S(1)}, f32[2,128,512]{2,1,0:T(8,128)S(1)}, u32[]{:S(2)}, u32[]{:S(2)}) collective-permute-start(f32[2,128,512]{2,1,0:T(8,128)S(1)} %add.109), channel_id=1, source_target_pairs={{0,4},{1,5},{2,6},{3,7},{4,0},{5,1},{6,2},{7,3},{8,12},{9,13},{10,... | collective-permute-start | bytes 1572872 | tf_op jit(solution)/shard_map/ppermute | solution.py:30
  298.1 16.6 %collective-permute-start.3 = (f32[2,128,256]{2,1,0:T(8,128)S(1)}, f32[2,128,256]{2,1,0:T(8,128)S(1)}, u32[]{:S(2)}, u32[]{:S(2)}) collective-permute-start(f32[2,128,256]{2,1,0:T(8,128)S(1)} %add.105), channel_id=1, source_target_pairs={{0,4},{1,5},{2,6},{3,7},{4,0},{5,1},{6,2},{7,3},{8,12},{9,13},{10,... | collective-permute-start | bytes 786440 | tf_op jit(solution)/shard_map/ppermute | solution.py:30
  314.8 3.4 collective-permute-start.4
  317.1 3.3 collective-permute-start.10
  319.3 19.1 %copy-start.5 = (f32[2,256,256]{2,1,0:T(8,128)}, f32[2,256,256]{2,1,0:T(8,128)S(1)}, u32[]{:S(2)}) copy-start(f32[2,256,256]{2,1,0:T(8,128)S(1)} %fusion.4) | copy-start | bytes 1572868
  319.3 16.5 %collective-permute-start.5 = (f32[2,256,256]{2,1,0:T(8,128)S(1)}, f32[2,256,256]{2,1,0:T(8,128)S(1)}, u32[]{:S(2)}, u32[]{:S(2)}) collective-permute-start(f32[2,256,256]{2,1,0:T(8,128)S(1)} %fusion.4), channel_id=1, source_target_pairs={{0,8},{8,16},{16,24},{24,32},{32,40},{40,48},{48,56},{56,64},{64,7... | collective-permute-start | bytes 1572872 | tf_op jit(solution)/shard_map/ppermute | solution.py:16
  336.5 1.9 copy-start.4
Sparse Core Ops, SparseCore 0:
  39.2 55.2 all-gather.1

commit v4 on v3

--- a/solution.py
+++ b/solution.py
@@ -118,44 +118,56 @@
 ):
     slots = panel1.shape[0]
     cols_here = sigma_anc.shape[1] // B
+    row_count = lax.axis_size("row")
+    row_here = lax.axis_index("row")
+    core = row_here % 2
     keep_own2 = mask2.astype(jnp.float32)
     factor2_own = keep_own2[:, :, None] * product("kij,kjc->kic", panel2, diag_inv2)
-    factor2_child = shifted(factor2_own, "own", -1)
+    piece = B // row_count
+    up_own = lax.dynamic_slice_in_dim(parent_block2, row_here * piece, piece, axis=1)
+    up_own = product("kij,kjc->kic", up_own, diag_inv2)
+    payload = shifted(jnp.concatenate([factor2_own, up_own], axis=1), "own", -1)
 
     outgoing = select_send(sigma_anc, row_blocks, slots)
-    factor2_child, outgoing = lax.optimization_barrier((factor2_child, outgoing))
+    payload, outgoing = lax.optimization_barrier((payload, outgoing))
     received = lax.all_to_all(outgoing, "own", split_axis=0, concat_axis=0, tiled=True)
 
     keep1 = mask1.astype(jnp.float32)
     factor1 = keep1[:, :, None] * product("kij,kjc->kic", panel1, diag_inv1)
-    factor2 = keep1[:, :, None] * factor2_child
+    factor2 = keep1[:, :, None] * payload[:, :B]
     both = jnp.concatenate([factor1, factor2], axis=-1)
     boths = lax.all_gather(both, "row", axis=1, tiled=True).reshape(slots, -1, B, 2 * B)
+    up_parent = lax.all_gather(payload[:, B:], "row", axis=1, tiled=True)
 
     blocks1 = select_take(received, row_blocks, slots, cols_here)
     kept = keep1[:, :, None] * product("kmij,kmjc->kic", blocks1, boths)
     sel1_panel = -kept[:, :, :B]
+    pre2 = -(product("kij,kjc->kic", sel1_panel, up_parent) + kept[:, :, B:])
+    pre2_child = shifted(pre2, "own", 1)
+    terms = jnp.concatenate(
+        [
+            product("kji,kjc->kic", factor1, sel1_panel),
+            product("kji,kjc->kic", sel1_panel, factor2),
+            product("kji,kjc->kic", factor2, pre2),
+        ],
+        axis=-1,
+    )
+    summed = row_sum(terms)
     gram1 = product("kji,kjc->kic", diag_inv1, diag_inv1)
-    sel1_diag = gram1 - row_sum(product("kji,kjc->kic", factor1, sel1_panel))
+    sel1_diag = gram1 - summed[:, :, :B]
+    sel2_parent = -(product("kij,kjc->kic", sel1_diag, up_parent) + summed[:, :, B : 2 * B])
+    down = product("kji,kjc->kic", up_parent, sel2_parent) + summed[:, :, 2 * B :]
 
-    par_kept = shifted(kept, "own", 1)
-    par_diag = shifted(sel1_diag, "own", 1)
-    par_panel = -par_kept[:, :, :B]
-    par_anc = par_kept[:, :, B:]
+    partner = [(i, i ^ 1) for i in range(row_count)]
+    got = shifted(jnp.where(core == 0, sel2_parent, down), "own", 1)
+    other = lax.ppermute(got, "row", partner)
+    sel2_parent_child = jnp.where(core == 0, got, other)
+    down_child = jnp.where(core == 0, other, got)
 
-    up_parent = product("kij,kjc->kic", parent_block2, diag_inv2)
-    sel2_panel = -keep_own2[:, :, None] * (
-        product("kij,kjc->kic", par_panel, up_parent) + par_anc
-    )
-    cross = product("kji,kjc->kic", par_panel, factor2_own)
-    back = product("kji,kjc->kic", factor2_own, sel2_panel)
-    summed = row_sum(jnp.concatenate([cross, back], axis=-1))
-    cross = summed[:, :, :B]
-    back = summed[:, :, B:]
-    sel2_parent = -(product("kij,kjc->kic", par_diag, up_parent) + cross)
+    sel2_panel = keep_own2[:, :, None] * pre2_child
     gram2 = product("kji,kjc->kic", diag_inv2, diag_inv2)
-    sel2_diag = gram2 - product("kji,kjc->kic", up_parent, sel2_parent) - back
-    return (sel1_panel, sel1_diag, sel2_parent, sel2_panel, sel2_diag)
+    sel2_diag = gram2 - down_child
+    return (sel1_panel, sel1_diag, sel2_parent_child, sel2_panel, sel2_diag)
 
 
 def solution(mesh):

time: 346 us -> 333 us (0.962)
  waiting for transfers between devices: 259 us -> 229 us
  blocking collectives: 0 us -> 15.5 us
  starting transfers between devices: 27.6 us -> 32.1 us
    ppermute x3, waiting for transfers between devices: 46 us -> 27.1 us  [shifted(): lax.ppermute(shard, axis, [(i, (i + by) % length) for i in range(length)])]
    all_gather x0 -> x1, blocking collectives: none -> 15.5 us  [on_device(): up_parent = lax.all_gather(payload[:, B:], 'row', axis=1, tiled=True)]
    all_to_all x1, waiting for transfers between devices: 179 us -> 164 us  [on_device(): lax.all_to_all(outgoing, 'own', split_axis=0, concat_axis=0, tiled=True)]
    ppermute x2 -> x1, starting transfers between devices: 1.39 us -> 5.35 us  [row_sum(): part = mine + lax.ppermute(other, 'row', partner)]
    ppermute x4 -> x2, waiting for transfers between devices: 32.9 us -> 33.8 us  [row_sum(): lax.ppermute(part, 'row', [(i, i ^ step) for i in range(length)])]
  transfers between devices with their start and end apart: 13 -> 10, of which waited for: 8 -> 8; matrix products, arithmetic and copies ran while one was open for 5% -> 4% of each run, Pallas kernels for 2% -> 2%
where the time goes in v4:
time: 333 us
  waiting for transfers between devices  229 us (69%)
  starting transfers between devices  32.1 us (10%)
  matrix products  21.6 us (6%)
  blocking collectives  15.5 us (5%)
  between operations  14.3 us (4%)
  local copies, waits for them, and re-layouts  8.19 us (2%)
  Pallas kernels  6.37 us (2%)
  other arithmetic  5.63 us (2%)
    all_to_all x1, waiting for transfers between devices, on_device(): lax.all_to_all(outgoing, 'own', split_axis=0, concat_axis=0, tiled=True)  164 us
    ppermute x2, waiting for transfers between devices, row_sum(): lax.ppermute(part, 'row', [(i, i ^ step) for i in range(length)])  33.8 us
    ppermute x3, waiting for transfers between devices, shifted(): lax.ppermute(shard, axis, [(i, (i + by) % length) for i in range(length)])  27.1 us
    dot_general x12, matrix products, product(): return jnp.einsum(form, left, right, precision=HIGH)  21.6 us
    all_gather x1, blocking collectives, on_device(): up_parent = lax.all_gather(payload[:, B:], 'row', axis=1, tiled=True)  15.5 us
    ppermute x3, starting transfers between devices, shifted(): lax.ppermute(shard, axis, [(i, (i + by) % length) for i in range(length)])  10.8 us
    all_to_all x1, starting transfers between devices, on_device(): lax.all_to_all(outgoing, 'own', split_axis=0, concat_axis=0, tiled=True)  7.45 us
  transfers between devices with their start and end apart: 10, of which 8 were waited for; matrix products, arithmetic and copies ran while one was open for 4% of the time, Pallas kernels for 2%

profile of v4, /device:TPU:1, one launch (start us, length us, event | category | flops | bytes accessed | tf_op | source)
XLA Modules:
  0.0 332.5 jit_solution(3876077651129145644)
XLA Ops:
  7.2 0.0 copy-start
  7.2 0.7 convert_bitcast_fusion
  7.9 0.3 copy-done
  8.2 1.3 fusion.8
  9.5 1.7 convolution_multiply_fusion.1
  11.2 8.7 %collective-permute-start = (f32[2,288,256]{2,1,0:T(8,128)S(1)}, f32[2,288,256]{2,1,0:T(8,128)S(1)}, u32[]{:S(2)}, u32[]{:S(2)}) collective-permute-start(f32[2,288,256]{2,1,0:T(8,128)S(1)} %pad_maximum_fusion.2), channel_id=1, source_target_pairs={{0,248},{8,0},{16,8},{24,16},{32,24},{40,32},{48,40},{56,48},{64,5... | collective-permute-start | bytes 1769480 | tf_op jit(solution)/shard_map/ppermute | solution.py:16
  19.9 0.1 copy.61
  20.0 0.1 constant_dynamic-slice_fusion
  20.1 0.1 copy.88
  20.2 0.1 copy.63
  20.3 0.1 fusion.13
  20.4 0.7 gather_fusion
  21.1 0.7 clamp_reduce_fusion
  21.8 6.4 %shard_map.128 = f32[32,256,256]{2,1,0:T(8,128)} custom-call(s32[32]{0:T(128)} %get-tuple-element.10.rows_ref, s32[32]{0:T(128)} %get-tuple-element.9.cols_ref, f32[2048,512]{1,0:T(8,128)} %src_ref.1), custom_call_target="tpu_custom_call" | custom-call | bytes 12582912 | tf_op jit(solution)/shard_map/pallas_call | solution.py:73
  28.2 0.0 copy-start.6
  28.2 0.0 copy-start.2
  28.2 3.7 %collective-permute-done = f32[2,288,256]{2,1,0:T(8,128)S(1)} collective-permute-done((f32[2,288,256]{2,1,0:T(8,128)S(1)}, f32[2,288,256]{2,1,0:T(8,128)S(1)}, u32[]{:S(2)}, u32[]{:S(2)}) %collective-permute-start) | collective-permute-done | bytes 589856 | tf_op jit(solution)/shard_map/ppermute | solution.py:16
  31.9 7.4 %all-to-all-start = ((f32[32,256,256]{2,1,0:T(8,128)}), f32[32,256,256]{2,1,0:T(8,128)}, u32[]{:S(2)}, u32[]{:S(2)}) async-start(f32[32,256,256]{2,1,0:T(8,128)} %shard_map.128), calls=%async_computation | async-start | bytes 16777216 | tf_op jit(solution)/shard_map/all_to_all | solution.py:133
  39.4 0.0 all-gather.2.cloned.1.call-start
  39.4 0.0 copy-done.2
  39.5 0.0 copy-done.4
  39.5 0.7 convolution_multiply_fusion
  40.1 0.1 slice_multiply_fusion
  40.2 1.2 pad_maximum_fusion.1
  41.5 0.0 all-gather.2.cloned.1.call-update
  41.5 0.6 gather_fusion.1
  42.1 0.1 reshape.140
  42.2 15.5 %all_gather.7 = f32[2,256,256]{2,1,0:T(8,128)S(1)} all-gather(f32[2,32,256]{2,1,0:T(8,128)S(1)} %slice.29), channel_id=1, replica_groups=mesh['own'=32,'row'=8] {'row'}, dimensions={1}, use_global_device_ids=true | all-gather | bytes 589824 | tf_op jit(solution)/shard_map/all_gather | solution.py:140
  57.7 164.0 %all-to-all-done = f32[32,256,256]{2,1,0:T(8,128)} async-done(((f32[32,256,256]{2,1,0:T(8,128)}), f32[32,256,256]{2,1,0:T(8,128)}, u32[]{:S(2)}, u32[]{:S(2)}) %all-to-all-start) | async-done | bytes 8388640 | tf_op jit(solution)/shard_map/all_to_all | solution.py:133
  221.7 6.1 %gather_fusion.2 = f32[16,256,256]{2,1,0:T(8,128)} fusion(f32[32,256,256]{2,1,0:T(8,128)} %all-to-all-done, s32[1024]{0:T(1024)S(1)} %pad_clamp_fusion), kind=kCustom, calls=%fused_computation.2 | custom fusion | bytes 8388672 | tf_op jit(solution)/shard_map/gather | solution.py:113
  227.8 10.2 %fusion = f32[2,256,512]{2,1,0:T(8,128)S(1)} fusion(f32[2,8,256,256]{3,2,1,0:T(8,128)} %bitcast.53, f32[2,8,256,512]{3,2,1,0:T(8,128)} %bitcast.54, f32[2]{0:T(128)S(1)} %convert_bitcast_fusion.1), kind=kOutput, calls=%fused_computation.6 | convolution fusion | flops 6442713088 | bytes 13631496 | tf_op jit(solution)/shard_map/kmij,kmjc->kic/dot_general | solution.py:39
  238.1 0.1 slice_negate_fusion
  238.1 0.0 copy-start.1
  238.1 1.1 fusion.18
  239.2 1.1 fusion.17
  240.3 0.7 fusion.1
  241.0 1.1 fusion.19
  242.0 0.1 pad_maximum_fusion
  242.1 0.1 slice_select_fusion
  242.2 5.3 %collective-permute-start.1 = (f32[2,128,768]{2,1,0:T(8,128)S(1)}, f32[2,128,768]{2,1,0:T(8,128)S(1)}, u32[]{:S(2)}, u32[]{:S(2)}) collective-permute-start(f32[2,128,768]{2,1,0:T(8,128)S(1)} %slice_select_fusion), channel_id=1, source_target_pairs={{0,1},{1,0},{2,3},{3,2},{4,5},{5,4},{6,7},{7,6},{8,9},{9,8},{10,11... | collective-permute-start | bytes 2359304 | tf_op jit(solution)/shard_map/ppermute | solution.py:27
  247.6 1.9 collective-permute-done.1
  249.5 0.1 select_add_fusion
  249.7 1.4 collective-permute-start.2
  251.0 17.5 %collective-permute-done.2 = f32[2,128,768]{2,1,0:T(8,128)S(1)} collective-permute-done((f32[2,128,768]{2,1,0:T(8,128)S(1)}, f32[2,128,768]{2,1,0:T(8,128)S(1)}, u32[]{:S(2)}, u32[]{:S(2)}) %collective-permute-start.2) | collective-permute-done | bytes 786464 | tf_op jit(solution)/shard_map/ppermute | solution.py:30
  268.5 0.1 add.104
  268.6 3.1 collective-permute-start.3
  271.7 16.4 %collective-permute-done.3 = f32[2,128,768]{2,1,0:T(8,128)S(1)} collective-permute-done((f32[2,128,768]{2,1,0:T(8,128)S(1)}, f32[2,128,768]{2,1,0:T(8,128)S(1)}, u32[]{:S(2)}, u32[]{:S(2)}) %collective-permute-start.3) | collective-permute-done | bytes 786464 | tf_op jit(solution)/shard_map/ppermute | solution.py:30
  288.0 0.1 add.105
  288.1 2.4 collective-permute-start.4
  290.5 1.9 collective-permute-done.4
  292.5 0.1 maximum_select_fusion
  292.6 1.1 slice_subtract_fusion
  293.7 0.0 copy-start.3
  293.7 0.7 fusion.20
  294.3 1.1 fusion.2
  295.5 0.1 collective-permute-start.5
  295.6 2.1 collective-permute-start.7
  297.7 14.8 %collective-permute-done.5 = f32[2,256,256]{2,1,0:T(8,128)S(1)} collective-permute-done((f32[2,256,256]{2,1,0:T(8,128)S(1)}, f32[2,256,256]{2,1,0:T(8,128)S(1)}, u32[]{:S(2)}, u32[]{:S(2)}) %collective-permute-start.5) | collective-permute-done | bytes 524320 | tf_op jit(solution)/shard_map/ppermute | solution.py:16
  312.4 1.5 collective-permute-start.6
  314.0 1.1 fusion.21
  315.1 8.6 %collective-permute-done.7 = f32[2,256,256]{2,1,0:T(8,128)S(1)} collective-permute-done((f32[2,256,256]{2,1,0:T(8,128)S(1)}, f32[2,256,256]{2,1,0:T(8,128)S(1)}, u32[]{:S(2)}, u32[]{:S(2)}) %collective-permute-start.7) | collective-permute-done | bytes 524320 | tf_op jit(solution)/shard_map/ppermute | solution.py:16
  323.7 0.9 broadcast_multiply_fusion
  324.6 0.0 collective-permute-done.6
  324.6 1.1 select_subtract_fusion
  (15 shorter events, 0.1 us)
Async XLA Ops:
  7.2 1.1 copy-start
  8.2 11.7 %copy-start.5 = (s32[64,8]{0,1:T(8,128)S(1)}, s32[64,8]{0,1:T(8,128)}, u32[]{:S(2)}) copy-start(s32[64,8]{0,1:T(8,128)} %param.10) | copy-start | bytes 6148
  11.2 20.7 %collective-permute-start = (f32[2,288,256]{2,1,0:T(8,128)S(1)}, f32[2,288,256]{2,1,0:T(8,128)S(1)}, u32[]{:S(2)}, u32[]{:S(2)}) collective-permute-start(f32[2,288,256]{2,1,0:T(8,128)S(1)} %pad_maximum_fusion.2), channel_id=1, source_target_pairs={{0,248},{8,0},{16,8},{24,16},{32,24},{40,32},{48,40},{56,48},{64,5... | collective-permute-start | bytes 1769480 | tf_op jit(solution)/shard_map/ppermute | solution.py:16
  28.2 11.2 %copy-start.6 = (s32[2,1]{0,1:T(1,128)S(1)}, s32[2,1]{0,1:T(1,128)}, u32[]{:S(2)}) copy-start(s32[2,1]{0,1:T(1,128)} %param.13) | copy-start | bytes 28
  28.2 11.2 %copy-start.2 = (f32[2,256,256]{2,1,0:T(8,128)S(1)}, f32[2,256,256]{2,1,0:T(8,128)}, u32[]{:S(2)}) copy-start(f32[2,256,256]{2,1,0:T(8,128)} %param.12) | copy-start | bytes 1572868
  31.9 7.5 %copy-start.4 = (f32[2,256,256]{2,1,0:T(8,128)S(1)}, f32[2,256,256]{2,1,0:T(8,128)}, u32[]{:S(2)}) copy-start(f32[2,256,256]{2,1,0:T(8,128)} %param.11) | copy-start | bytes 1572868
  31.9 189.8 %all-to-all-start = ((f32[32,256,256]{2,1,0:T(8,128)}), f32[32,256,256]{2,1,0:T(8,128)}, u32[]{:S(2)}, u32[]{:S(2)}) async-start(f32[32,256,256]{2,1,0:T(8,128)} %shard_map.128), calls=%async_computation | async-start | bytes 16777216 | tf_op jit(solution)/shard_map/all_to_all | solution.py:133
  39.4 188.4 %all-gather.2.cloned.1.call-start = ((), (), s32[]{:S(2)}) async-start(), calls=%async_computation.1 | async-start | bytes 9437184 | tf_op jit(solution)/shard_map/all_gather | solution.py:139
  238.1 2.2 copy-start.1
  242.2 7.3 %collective-permute-start.1 = (f32[2,128,768]{2,1,0:T(8,128)S(1)}, f32[2,128,768]{2,1,0:T(8,128)S(1)}, u32[]{:S(2)}, u32[]{:S(2)}) collective-permute-start(f32[2,128,768]{2,1,0:T(8,128)S(1)} %slice_select_fusion), channel_id=1, source_target_pairs={{0,1},{1,0},{2,3},{3,2},{4,5},{5,4},{6,7},{7,6},{8,9},{9,8},{10,11... | collective-permute-start | bytes 2359304 | tf_op jit(solution)/shard_map/ppermute | solution.py:27
  249.7 18.8 %collective-permute-start.2 = (f32[2,128,768]{2,1,0:T(8,128)S(1)}, f32[2,128,768]{2,1,0:T(8,128)S(1)}, u32[]{:S(2)}, u32[]{:S(2)}) collective-permute-start(f32[2,128,768]{2,1,0:T(8,128)S(1)} %select_add_fusion), channel_id=1, source_target_pairs={{0,2},{1,3},{2,0},{3,1},{4,6},{5,7},{6,4},{7,5},{8,10},{9,11},{10,... | collective-permute-start | bytes 2359304 | tf_op jit(solution)/shard_map/ppermute | solution.py:30
  268.6 19.5 %collective-permute-start.3 = (f32[2,128,768]{2,1,0:T(8,128)S(1)}, f32[2,128,768]{2,1,0:T(8,128)S(1)}, u32[]{:S(2)}, u32[]{:S(2)}) collective-permute-start(f32[2,128,768]{2,1,0:T(8,128)S(1)} %add.104), channel_id=1, source_target_pairs={{0,4},{1,5},{2,6},{3,7},{4,0},{5,1},{6,2},{7,3},{8,12},{9,13},{10,... | collective-permute-start | bytes 2359304 | tf_op jit(solution)/shard_map/ppermute | solution.py:30
  288.1 4.3 %collective-permute-start.4 = (f32[2,128,768]{2,1,0:T(8,128)S(1)}, f32[2,128,768]{2,1,0:T(8,128)S(1)}, u32[]{:S(2)}, u32[]{:S(2)}) collective-permute-start(f32[2,128,768]{2,1,0:T(8,128)S(1)} %add.105), channel_id=1, source_target_pairs={{0,1},{1,0},{2,3},{3,2},{4,5},{5,4},{6,7},{7,6},{8,9},{9,8},{10,11... | collective-permute-start | bytes 2359304 | tf_op jit(solution)/shard_map/ppermute | solution.py:32
  293.7 1.8 copy-start.3
  295.5 17.0 %collective-permute-start.5 = (f32[2,256,256]{2,1,0:T(8,128)S(1)}, f32[2,256,256]{2,1,0:T(8,128)S(1)}, u32[]{:S(2)}, u32[]{:S(2)}) collective-permute-start(f32[2,256,256]{2,1,0:T(8,128)S(1)} %fusion.2), channel_id=1, source_target_pairs={{0,8},{8,16},{16,24},{24,32},{32,40},{40,48},{48,56},{56,64},{64,7... | collective-permute-start | bytes 1572872 | tf_op jit(solution)/shard_map/ppermute | solution.py:16
  295.6 28.1 %collective-permute-start.7 = (f32[2,256,256]{2,1,0:T(8,128)S(1)}, f32[2,256,256]{2,1,0:T(8,128)S(1)}, u32[]{:S(2)}, u32[]{:S(2)}) collective-permute-start(f32[2,256,256]{2,1,0:T(8,128)S(1)} %fusion.1), channel_id=1, source_target_pairs={{0,8},{8,16},{16,24},{24,32},{32,40},{40,48},{48,56},{56,64},{64,7... | collective-permute-start | bytes 1572872 | tf_op jit(solution)/shard_map/ppermute | solution.py:16
  312.4 12.1 %collective-permute-start.6 = (f32[2,256,256]{2,1,0:T(8,128)S(1)}, f32[2,256,256]{2,1,0:T(8,128)S(1)}, u32[]{:S(2)}, u32[]{:S(2)}) collective-permute-start(f32[2,256,256]{2,1,0:T(8,128)S(1)} %collective-permute-done.5), channel_id=1, source_target_pairs={{0,1},{1,0},{2,3},{3,2},{4,5},{5,4},{6,7},{7,6},{8,9},{9,8},{10,11... | collective-permute-start | bytes 1572872 | tf_op jit(solution)/shard_map/ppermute | solution.py:163
Sparse Core Ops, SparseCore 0:
  42.0 55.2 all-gather.1

commit v5 on v4

--- a/solution.py
+++ b/solution.py
@@ -16,7 +16,7 @@
     return lax.ppermute(shard, axis, [(i, (i + by) % length) for i in range(length)])
 
 
-def row_sum(x):
+def row_sum(x, arrive=None):
     length = lax.axis_size("row")
     core = lax.axis_index("row") % 2
     half = x.shape[1] // 2
@@ -29,10 +29,13 @@
     while step < length:
         part = part + lax.ppermute(part, "row", [(i, i ^ step) for i in range(length)])
         step *= 2
+    if arrive is not None:
+        arrive, part = lax.optimization_barrier((arrive, part))
     got = lax.ppermute(part, "row", partner)
-    return jnp.where(
+    full = jnp.where(
         core == 0, jnp.concatenate([part, got], axis=1), jnp.concatenate([got, part], axis=1)
     )
+    return full, arrive
 
 
 def product(form, left, right):
@@ -106,11 +109,45 @@
     return gather_blocks(sigma_local, chosen_row, chosen_col)
 
 
+def _take_blocks(which_ref, src_ref, out_ref, staged, sems_in, sem_out):
+    count = staged.shape[0]
+    copies = []
+    for i in range(count):
+        copy = pltpu.make_async_copy(src_ref.at[which_ref[i]], staged.at[i], sems_in.at[i])
+        copy.start()
+        copies.append(copy)
+    for copy in copies:
+        copy.wait()
+    store = pltpu.make_async_copy(staged, out_ref, sem_out)
+    store.start()
+    store.wait()
+
+
 def select_take(received, row_blocks, slots, cols_here):
     mine = lax.axis_index("own") * slots + jnp.arange(slots, dtype=jnp.int32)
     rowlist = row_blocks[mine]
-    sender = rowlist // cols_here
-    return received[sender]
+    sender = jnp.clip(rowlist // cols_here, 0, received.shape[0] - 1).reshape(-1)
+    count = sender.shape[0]
+    grid_spec = pltpu.PrefetchScalarGridSpec(
+        num_scalar_prefetch=1,
+        grid=(),
+        in_specs=[pl.BlockSpec(memory_space=pl.ANY)],
+        out_specs=pl.BlockSpec(memory_space=pl.ANY),
+        scratch_shapes=[
+            pltpu.VMEM((count, B, B), received.dtype),
+            pltpu.SemaphoreType.DMA((count,)),
+            pltpu.SemaphoreType.DMA(()),
+        ],
+    )
+    taken = pl.pallas_call(
+        _take_blocks,
+        out_shape=jax.ShapeDtypeStruct((count, B, B), received.dtype),
+        grid_spec=grid_spec,
+        cost_estimate=pl.CostEstimate(
+            flops=0, bytes_accessed=2 * count * B * B * 4, transcendentals=0
+        ),
+    )(sender, received)
+    return taken.reshape(slots, -1, B, B)
 
 
 def on_device(
@@ -152,7 +189,7 @@
         ],
         axis=-1,
     )
-    summed = row_sum(terms)
+    summed, pre2_child = row_sum(terms, pre2_child)
     gram1 = product("kji,kjc->kic", diag_inv1, diag_inv1)
     sel1_diag = gram1 - summed[:, :, :B]
     sel2_parent = -(product("kij,kjc->kic", sel1_diag, up_parent) + summed[:, :, B : 2 * B])

time: 333 us -> 322 us (0.967)
  waiting for transfers between devices: 229 us -> 222 us
  local copies, waits for them, and re-layouts: 8.19 us -> 2.05 us
  Pallas kernels: 6.37 us -> 11.3 us
    ppermute x3, waiting for transfers between devices: 27.1 us -> 20.6 us  [shifted(): lax.ppermute(shard, axis, [(i, (i + by) % length) for i in range(length)])]
    gather x1 -> x0, local copies, waits for them, and re-layouts: 6.14 us -> none  [select_take(): return received[sender]]
    pallas_call x0 -> x1, Pallas kernels: none -> 4.89 us  [select_take(): pl.pallas_call(_take_blocks, out_shape=jax.ShapeDtypeStruct((count, B, B)...]
  transfers between devices with their start and end apart: 10 -> 10, of which waited for: 8 -> 7; matrix products, arithmetic and copies ran while one was open for 4% -> 2% of each run, Pallas kernels for 2% -> 3%
where the time goes in v5:
time: 322 us
  waiting for transfers between devices  222 us (69%)
  starting transfers between devices  29.4 us (9%)
  matrix products  21.6 us (7%)
  blocking collectives  15.3 us (5%)
  between operations  14.4 us (4%)
  Pallas kernels  11.3 us (4%)
  other arithmetic  6.12 us (2%)
    all_to_all x1, waiting for transfers between devices, on_device(): lax.all_to_all(outgoing, 'own', split_axis=0, concat_axis=0, tiled=True)  164 us
    ppermute x2, waiting for transfers between devices, row_sum(): lax.ppermute(part, 'row', [(i, i ^ step) for i in range(length)])  33.8 us
    dot_general x12, matrix products, product(): return jnp.einsum(form, left, right, precision=HIGH)  21.6 us
    ppermute x3, waiting for transfers between devices, shifted(): lax.ppermute(shard, axis, [(i, (i + by) % length) for i in range(length)])  20.6 us
    all_gather x1, blocking collectives, on_device(): up_parent = lax.all_gather(payload[:, B:], 'row', axis=1, tiled=True)  15.3 us
    ppermute x3, starting transfers between devices, shifted(): lax.ppermute(shard, axis, [(i, (i + by) % length) for i in range(length)])  8.76 us
    all_to_all x1, starting transfers between devices, on_device(): lax.all_to_all(outgoing, 'own', split_axis=0, concat_axis=0, tiled=True)  7.45 us
  transfers between devices with their start and end apart: 10, of which 7 were waited for; matrix products, arithmetic and copies ran while one was open for 2% of the time, Pallas kernels for 3%

profile of v5, /device:TPU:1, one launch (start us, length us, event | category | flops | bytes accessed | tf_op | source)
XLA Modules:
  0.0 322.1 jit_solution(14987795692396113750)
XLA Ops:
  7.2 0.0 copy-start
  7.2 0.7 convert_bitcast_fusion
  7.9 0.3 copy-done
  8.2 1.3 fusion.8
  9.5 1.7 convolution_multiply_fusion.1
  11.2 8.7 %collective-permute-start = (f32[2,288,256]{2,1,0:T(8,128)S(1)}, f32[2,288,256]{2,1,0:T(8,128)S(1)}, u32[]{:S(2)}, u32[]{:S(2)}) collective-permute-start(f32[2,288,256]{2,1,0:T(8,128)S(1)} %pad_maximum_fusion.2), channel_id=1, source_target_pairs={{0,248},{8,0},{16,8},{24,16},{32,24},{40,32},{48,40},{56,48},{64,5... | collective-permute-start | bytes 1769480 | tf_op jit(solution)/shard_map/ppermute | solution.py:16
  19.9 0.1 copy.61
  20.0 0.1 constant_dynamic-slice_fusion
  20.1 0.1 copy.88
  20.2 0.1 copy.64
  20.3 0.1 fusion.13
  20.4 0.7 gather_fusion.1
  21.1 0.7 clamp_reduce_fusion
  21.8 6.4 %shard_map.128 = f32[32,256,256]{2,1,0:T(8,128)} custom-call(s32[32]{0:T(128)} %get-tuple-element.14.rows_ref, s32[32]{0:T(128)} %get-tuple-element.13.cols_ref, f32[2048,512]{1,0:T(8,128)} %src_ref.1), custom_call_target="tpu_custom_call" | custom-call | bytes 12582912 | tf_op jit(solution)/shard_map/pallas_call | solution.py:76
  28.2 0.0 copy-start.6
  28.2 0.0 copy-start.2
  28.2 3.7 %collective-permute-done = f32[2,288,256]{2,1,0:T(8,128)S(1)} collective-permute-done((f32[2,288,256]{2,1,0:T(8,128)S(1)}, f32[2,288,256]{2,1,0:T(8,128)S(1)}, u32[]{:S(2)}, u32[]{:S(2)}) %collective-permute-start) | collective-permute-done | bytes 589856 | tf_op jit(solution)/shard_map/ppermute | solution.py:16
  31.9 7.4 %all-to-all-start = ((f32[32,256,256]{2,1,0:T(8,128)}), f32[32,256,256]{2,1,0:T(8,128)}, u32[]{:S(2)}, u32[]{:S(2)}) async-start(f32[32,256,256]{2,1,0:T(8,128)} %shard_map.128), calls=%async_computation | async-start | bytes 16777216 | tf_op jit(solution)/shard_map/all_to_all | solution.py:170
  39.4 0.0 all-gather.2.cloned.1.call-start
  39.5 0.7 convolution_multiply_fusion
  40.1 0.1 slice_multiply_fusion
  40.2 1.2 pad_maximum_fusion.1
  41.5 0.0 all-gather.2.cloned.1.call-update
  41.5 0.6 gather_fusion
  42.1 0.1 gather.9
  42.2 0.5 fusion.17.which_ref
  42.7 15.3 %all_gather.7 = f32[2,256,256]{2,1,0:T(8,128)S(1)} all-gather(f32[2,32,256]{2,1,0:T(8,128)S(1)} %slice.29), channel_id=1, replica_groups=mesh['own'=32,'row'=8] {'row'}, dimensions={1}, use_global_device_ids=true | all-gather | bytes 589824 | tf_op jit(solution)/shard_map/all_gather | solution.py:177
  58.0 163.7 %all-to-all-done.src_ref = f32[32,256,256]{2,1,0:T(8,128)} async-done(((f32[32,256,256]{2,1,0:T(8,128)}), f32[32,256,256]{2,1,0:T(8,128)}, u32[]{:S(2)}, u32[]{:S(2)}) %all-to-all-start) | async-done | bytes 8388640 | tf_op jit(solution)/shard_map/all_to_all | solution.py:170
  221.7 4.9 %shard_map.129 = f32[16,256,256]{2,1,0:T(8,128)} custom-call(s32[16]{0:T(128)} %fusion.17.which_ref, f32[32,256,256]{2,1,0:T(8,128)} %all-to-all-done.src_ref), custom_call_target="tpu_custom_call" | custom-call | bytes 8388608 | tf_op jit(solution)/shard_map/pallas_call | solution.py:142
  226.6 0.0 all-gather.2.cloned.1.call-done
  226.6 10.2 %fusion = f32[2,256,512]{2,1,0:T(8,128)S(1)} fusion(f32[2,8,256,256]{3,2,1,0:T(8,128)} %bitcast.41, f32[2,8,256,512]{3,2,1,0:T(8,128)} %bitcast.42, f32[2]{0:T(128)S(1)} %convert_bitcast_fusion.1), kind=kOutput, calls=%fused_computation.5 | convolution fusion | flops 6442713088 | bytes 13631496 | tf_op jit(solution)/shard_map/kmij,kmjc->kic/dot_general | solution.py:42
  236.8 0.1 slice_negate_fusion
  236.9 0.0 copy-start.1
  236.9 1.1 fusion.19
  238.0 1.1 fusion.18
  239.1 0.7 fusion.1
  239.8 1.1 fusion.20
  240.8 0.1 pad_maximum_fusion
  240.9 0.1 slice_select_fusion
  241.0 5.5 %collective-permute-start.2 = (f32[2,128,768]{2,1,0:T(8,128)S(1)}, f32[2,128,768]{2,1,0:T(8,128)S(1)}, u32[]{:S(2)}, u32[]{:S(2)}) collective-permute-start(f32[2,128,768]{2,1,0:T(8,128)S(1)} %slice_select_fusion), channel_id=1, source_target_pairs={{0,1},{1,0},{2,3},{3,2},{4,5},{5,4},{6,7},{7,6},{8,9},{9,8},{10,11... | collective-permute-start | bytes 2359304 | tf_op jit(solution)/shard_map/ppermute | solution.py:27
  246.6 1.9 collective-permute-done.2
  248.5 0.1 select_add_fusion
  248.6 1.4 collective-permute-start.3
  250.0 17.5 %collective-permute-done.3 = f32[2,128,768]{2,1,0:T(8,128)S(1)} collective-permute-done((f32[2,128,768]{2,1,0:T(8,128)S(1)}, f32[2,128,768]{2,1,0:T(8,128)S(1)}, u32[]{:S(2)}, u32[]{:S(2)}) %collective-permute-start.3) | collective-permute-done | bytes 786464 | tf_op jit(solution)/shard_map/ppermute | solution.py:30
  267.5 0.1 add.87
  267.6 3.1 collective-permute-start.4
  270.6 0.0 collective-permute-start.1
  270.6 16.4 %collective-permute-done.4 = f32[2,128,768]{2,1,0:T(8,128)S(1)} collective-permute-done((f32[2,128,768]{2,1,0:T(8,128)S(1)}, f32[2,128,768]{2,1,0:T(8,128)S(1)}, u32[]{:S(2)}, u32[]{:S(2)}) %collective-permute-start.4) | collective-permute-done | bytes 786464 | tf_op jit(solution)/shard_map/ppermute | solution.py:30
  287.0 0.1 add.88
  287.1 0.0 collective-permute-done.1
  287.1 2.2 collective-permute-start.5
  289.3 1.9 collective-permute-done.5
  291.2 0.1 maximum_select_fusion
  291.3 1.1 slice_subtract_fusion
  292.4 0.0 copy-start.3
  292.4 0.7 fusion.21
  293.1 1.1 fusion.2
  294.2 0.1 collective-permute-start.6
  294.3 16.9 %collective-permute-done.6 = f32[2,256,256]{2,1,0:T(8,128)S(1)} collective-permute-done((f32[2,256,256]{2,1,0:T(8,128)S(1)}, f32[2,256,256]{2,1,0:T(8,128)S(1)}, u32[]{:S(2)}, u32[]{:S(2)}) %collective-permute-start.6) | collective-permute-done | bytes 524320 | tf_op jit(solution)/shard_map/ppermute | solution.py:16
  311.2 1.0 collective-permute-start.7
  312.2 1.1 fusion.22
  313.2 0.9 broadcast_multiply_fusion
  314.1 0.0 collective-permute-done.7
  314.1 1.1 select_subtract_fusion
  (14 shorter events, 0.1 us)
Async XLA Ops:
  7.2 1.1 copy-start
  8.2 11.7 %copy-start.5 = (s32[64,8]{0,1:T(8,128)S(1)}, s32[64,8]{0,1:T(8,128)}, u32[]{:S(2)}) copy-start(s32[64,8]{0,1:T(8,128)} %param.10) | copy-start | bytes 6148
  11.2 20.7 %collective-permute-start = (f32[2,288,256]{2,1,0:T(8,128)S(1)}, f32[2,288,256]{2,1,0:T(8,128)S(1)}, u32[]{:S(2)}, u32[]{:S(2)}) collective-permute-start(f32[2,288,256]{2,1,0:T(8,128)S(1)} %pad_maximum_fusion.2), channel_id=1, source_target_pairs={{0,248},{8,0},{16,8},{24,16},{32,24},{40,32},{48,40},{56,48},{64,5... | collective-permute-start | bytes 1769480 | tf_op jit(solution)/shard_map/ppermute | solution.py:16
  28.2 11.2 %copy-start.6 = (s32[2,1]{0,1:T(1,128)S(1)}, s32[2,1]{0,1:T(1,128)}, u32[]{:S(2)}) copy-start(s32[2,1]{0,1:T(1,128)} %param.13) | copy-start | bytes 28
  28.2 11.2 %copy-start.2 = (f32[2,256,256]{2,1,0:T(8,128)S(1)}, f32[2,256,256]{2,1,0:T(8,128)}, u32[]{:S(2)}) copy-start(f32[2,256,256]{2,1,0:T(8,128)} %param.12) | copy-start | bytes 1572868
  31.9 7.5 %copy-start.4 = (f32[2,256,256]{2,1,0:T(8,128)S(1)}, f32[2,256,256]{2,1,0:T(8,128)}, u32[]{:S(2)}) copy-start(f32[2,256,256]{2,1,0:T(8,128)} %param.11) | copy-start | bytes 1572868
  31.9 189.8 %all-to-all-start = ((f32[32,256,256]{2,1,0:T(8,128)}), f32[32,256,256]{2,1,0:T(8,128)}, u32[]{:S(2)}, u32[]{:S(2)}) async-start(f32[32,256,256]{2,1,0:T(8,128)} %shard_map.128), calls=%async_computation | async-start | bytes 16777216 | tf_op jit(solution)/shard_map/all_to_all | solution.py:170
  39.4 187.2 %all-gather.2.cloned.1.call-start = ((), (), s32[]{:S(2)}) async-start(), calls=%async_computation.1 | async-start | bytes 9437184 | tf_op jit(solution)/shard_map/all_gather | solution.py:176
  236.9 2.2 copy-start.1
  241.0 7.4 %collective-permute-start.2 = (f32[2,128,768]{2,1,0:T(8,128)S(1)}, f32[2,128,768]{2,1,0:T(8,128)S(1)}, u32[]{:S(2)}, u32[]{:S(2)}) collective-permute-start(f32[2,128,768]{2,1,0:T(8,128)S(1)} %slice_select_fusion), channel_id=1, source_target_pairs={{0,1},{1,0},{2,3},{3,2},{4,5},{5,4},{6,7},{7,6},{8,9},{9,8},{10,11... | collective-permute-start | bytes 2359304 | tf_op jit(solution)/shard_map/ppermute | solution.py:27
  248.6 18.8 %collective-permute-start.3 = (f32[2,128,768]{2,1,0:T(8,128)S(1)}, f32[2,128,768]{2,1,0:T(8,128)S(1)}, u32[]{:S(2)}, u32[]{:S(2)}) collective-permute-start(f32[2,128,768]{2,1,0:T(8,128)S(1)} %select_add_fusion), channel_id=1, source_target_pairs={{0,2},{1,3},{2,0},{3,1},{4,6},{5,7},{6,4},{7,5},{8,10},{9,11},{10,... | collective-permute-start | bytes 2359304 | tf_op jit(solution)/shard_map/ppermute | solution.py:30
  267.6 19.5 %collective-permute-start.4 = (f32[2,128,768]{2,1,0:T(8,128)S(1)}, f32[2,128,768]{2,1,0:T(8,128)S(1)}, u32[]{:S(2)}, u32[]{:S(2)}) collective-permute-start(f32[2,128,768]{2,1,0:T(8,128)S(1)} %add.87), channel_id=1, source_target_pairs={{0,4},{1,5},{2,6},{3,7},{4,0},{5,1},{6,2},{7,3},{8,12},{9,13},{10,... | collective-permute-start | bytes 2359304 | tf_op jit(solution)/shard_map/ppermute | solution.py:30
  270.6 16.5 %collective-permute-start.1 = (f32[2,256,256]{2,1,0:T(8,128)S(1)}, f32[2,256,256]{2,1,0:T(8,128)S(1)}, u32[]{:S(2)}, u32[]{:S(2)}) collective-permute-start(f32[2,256,256]{2,1,0:T(8,128)S(1)} %fusion.1), channel_id=1, source_target_pairs={{0,8},{8,16},{16,24},{24,32},{32,40},{40,48},{48,56},{56,64},{64,7... | collective-permute-start | bytes 1572872 | tf_op jit(solution)/shard_map/ppermute | solution.py:16
  287.1 4.1 %collective-permute-start.5 = (f32[2,128,768]{2,1,0:T(8,128)S(1)}, f32[2,128,768]{2,1,0:T(8,128)S(1)}, u32[]{:S(2)}, u32[]{:S(2)}) collective-permute-start(f32[2,128,768]{2,1,0:T(8,128)S(1)} %add.88), channel_id=1, source_target_pairs={{0,1},{1,0},{2,3},{3,2},{4,5},{5,4},{6,7},{7,6},{8,9},{9,8},{10,11... | collective-permute-start | bytes 2359304 | tf_op jit(solution)/shard_map/ppermute | solution.py:34
  292.4 1.8 copy-start.3
  294.2 17.0 %collective-permute-start.6 = (f32[2,256,256]{2,1,0:T(8,128)S(1)}, f32[2,256,256]{2,1,0:T(8,128)S(1)}, u32[]{:S(2)}, u32[]{:S(2)}) collective-permute-start(f32[2,256,256]{2,1,0:T(8,128)S(1)} %fusion.2), channel_id=1, source_target_pairs={{0,8},{8,16},{16,24},{24,32},{32,40},{40,48},{48,56},{56,64},{64,7... | collective-permute-start | bytes 1572872 | tf_op jit(solution)/shard_map/ppermute | solution.py:16
  311.2 2.9 collective-permute-start.7
Sparse Core Ops, SparseCore 0:
  42.0 55.2 all-gather.1

commit v6 on v5

--- a/solution.py
+++ b/solution.py
@@ -18,19 +18,31 @@
 
 def row_sum(x, arrive=None):
     length = lax.axis_size("row")
-    core = lax.axis_index("row") % 2
+    row_here = lax.axis_index("row")
+    core = row_here % 2
+    chip = row_here // 2
+    chips = length // 2
     half = x.shape[1] // 2
     lo, hi = x[:, :half], x[:, half:]
     mine = jnp.where(core == 0, lo, hi)
     other = jnp.where(core == 0, hi, lo)
     partner = [(i, i ^ 1) for i in range(length)]
     part = mine + lax.ppermute(other, "row", partner)
-    step = 2
-    while step < length:
-        part = part + lax.ppermute(part, "row", [(i, i ^ step) for i in range(length)])
-        step *= 2
+    quarter = half // chips
+
+    def towards(value, by):
+        return lax.ppermute(value, "row", [(i, (i + 2 * by) % length) for i in range(length)])
+
+    total = lax.dynamic_slice_in_dim(part, chip * quarter, quarter, axis=1)
+    for by in range(1, chips):
+        target = (chip + by) % chips
+        total = total + towards(lax.dynamic_slice_in_dim(part, target * quarter, quarter, axis=1), by)
     if arrive is not None:
-        arrive, part = lax.optimization_barrier((arrive, part))
+        arrive, total = lax.optimization_barrier((arrive, total))
+    pieces = [total] + [towards(total, by) for by in range(1, chips)]
+    stacked = jnp.stack(pieces)
+    order = (chip - jnp.arange(chips, dtype=jnp.int32)) % chips
+    part = stacked[order].transpose(1, 0, 2, 3).reshape(part.shape)
     got = lax.ppermute(part, "row", partner)
     full = jnp.where(
         core == 0, jnp.concatenate([part, got], axis=1), jnp.concatenate([got, part], axis=1)

time: 322 us -> 322 us (level)
  waiting for transfers between devices: 222 us -> 207 us
  local copies, waits for them, and re-layouts: 2.05 us -> 13.1 us
  other arithmetic: 6.12 us -> 9.78 us
    ppermute x2 -> x6, waiting for transfers between devices: 33.8 us -> 18.4 us  [towards(): lax.ppermute(value, 'row', [(i, (i + 2 * by) % length) for i in range(len...]
    dynamic_slice x0 -> x4, local copies, waits for them, and re-layouts: none -> 5.44 us  [row_sum(): lax.dynamic_slice_in_dim(part, target * quarter, quarter, axis=1)]
    ppermute x0 -> x3, local copies, waits for them, and re-layouts: none -> 4.46 us  [towards(): lax.ppermute(value, 'row', [(i, (i + 2 * by) % length) for i in range(len...]
  transfers between devices with their start and end apart: 10 -> 14, of which waited for: 7 -> 10; matrix products, arithmetic and copies ran while one was open for 2% -> 7% of each run, Pallas kernels for 3% -> 4%
where the time goes in v6:
time: 322 us
  waiting for transfers between devices  207 us (64%)
  starting transfers between devices  29.6 us (9%)
  matrix products  21.6 us (7%)
  blocking collectives  15.3 us (5%)
  between operations  14.5 us (5%)
  local copies, waits for them, and re-layouts  13.1 us (4%)
  Pallas kernels  11.3 us (4%)
  other arithmetic  9.78 us (3%)
    all_to_all x1, waiting for transfers between devices, on_device(): lax.all_to_all(outgoing, 'own', split_axis=0, concat_axis=0, tiled=True)  164 us
    dot_general x12, matrix products, product(): return jnp.einsum(form, left, right, precision=HIGH)  21.6 us
    ppermute x3, waiting for transfers between devices, shifted(): lax.ppermute(shard, axis, [(i, (i + by) % length) for i in range(length)])  20.5 us
    ppermute x6, waiting for transfers between devices, towards(): lax.ppermute(value, 'row', [(i, (i + 2 * by) % length) for i in range(len...  18.4 us
    all_gather x1, blocking collectives, on_device(): up_parent = lax.all_gather(payload[:, B:], 'row', axis=1, tiled=True)  15.3 us
    ppermute x3, starting transfers between devices, shifted(): lax.ppermute(shard, axis, [(i, (i + by) % length) for i in range(length)])  8.76 us
    all_to_all x1, starting transfers between devices, on_device(): lax.all_to_all(outgoing, 'own', split_axis=0, concat_axis=0, tiled=True)  7.31 us
  transfers between devices with their start and end apart: 14, of which 10 were waited for; matrix products, arithmetic and copies ran while one was open for 7% of the time, Pallas kernels for 4%

profile of v6, /device:TPU:1, one launch (start us, length us, event | category | flops | bytes accessed | tf_op | source)
XLA Modules:
  0.0 321.8 jit_solution(7210189659001540131)
XLA Ops:
  7.2 0.7 convert_bitcast_fusion
  7.9 0.3 copy-done
  8.2 1.3 fusion.8
  9.5 1.7 convolution_multiply_fusion.1
  11.2 8.7 %collective-permute-start = (f32[2,288,256]{2,1,0:T(8,128)S(1)}, f32[2,288,256]{2,1,0:T(8,128)S(1)}, u32[]{:S(2)}, u32[]{:S(2)}) collective-permute-start(f32[2,288,256]{2,1,0:T(8,128)S(1)} %pad_maximum_fusion.3), channel_id=1, source_target_pairs={{0,248},{8,0},{16,8},{24,16},{32,24},{40,32},{48,40},{56,48},{64,5... | collective-permute-start | bytes 1769480 | tf_op jit(solution)/shard_map/ppermute | solution.py:16
  19.9 0.1 copy.89
  20.0 0.1 constant_dynamic-slice_fusion.3
  20.1 0.1 copy.121
  20.2 0.1 copy.92
  20.3 0.1 fusion.13
  20.4 0.7 gather_fusion.1
  21.1 0.7 clamp_reduce_fusion
  21.8 6.4 %shard_map.128 = f32[32,256,256]{2,1,0:T(8,128)} custom-call(s32[32]{0:T(128)} %get-tuple-element.14.rows_ref, s32[32]{0:T(128)} %get-tuple-element.13.cols_ref, f32[2048,512]{1,0:T(8,128)} %src_ref.1), custom_call_target="tpu_custom_call" | custom-call | bytes 12582912 | tf_op jit(solution)/shard_map/pallas_call | solution.py:88
  28.3 3.7 %collective-permute-done = f32[2,288,256]{2,1,0:T(8,128)S(1)} collective-permute-done((f32[2,288,256]{2,1,0:T(8,128)S(1)}, f32[2,288,256]{2,1,0:T(8,128)S(1)}, u32[]{:S(2)}, u32[]{:S(2)}) %collective-permute-start) | collective-permute-done | bytes 589856 | tf_op jit(solution)/shard_map/ppermute | solution.py:16
  31.9 7.3 %all-to-all-start = ((f32[32,256,256]{2,1,0:T(8,128)}), f32[32,256,256]{2,1,0:T(8,128)}, u32[]{:S(2)}, u32[]{:S(2)}) async-start(f32[32,256,256]{2,1,0:T(8,128)} %shard_map.128), calls=%async_computation | async-start | bytes 16777216 | tf_op jit(solution)/shard_map/all_to_all | solution.py:182
  39.3 0.7 convolution_multiply_fusion
  40.0 0.1 slice_multiply_fusion
  40.1 1.2 pad_maximum_fusion.1
  41.4 0.6 gather_fusion
  42.0 0.5 fusion.19.which_ref
  42.5 15.3 %all_gather.7 = f32[2,256,256]{2,1,0:T(8,128)S(1)} all-gather(f32[2,32,256]{2,1,0:T(8,128)S(1)} %slice.29), channel_id=1, replica_groups=mesh['own'=32,'row'=8] {'row'}, dimensions={1}, use_global_device_ids=true | all-gather | bytes 589824 | tf_op jit(solution)/shard_map/all_gather | solution.py:189
  57.8 163.7 %all-to-all-done.src_ref = f32[32,256,256]{2,1,0:T(8,128)} async-done(((f32[32,256,256]{2,1,0:T(8,128)}), f32[32,256,256]{2,1,0:T(8,128)}, u32[]{:S(2)}, u32[]{:S(2)}) %all-to-all-start) | async-done | bytes 8388640 | tf_op jit(solution)/shard_map/all_to_all | solution.py:182
  221.5 4.9 %shard_map.129 = f32[16,256,256]{2,1,0:T(8,128)} custom-call(s32[16]{0:T(128)} %fusion.19.which_ref, f32[32,256,256]{2,1,0:T(8,128)} %all-to-all-done.src_ref), custom_call_target="tpu_custom_call" | custom-call | bytes 8388608 | tf_op jit(solution)/shard_map/pallas_call | solution.py:154
  226.5 10.2 %fusion = f32[2,256,512]{2,1,0:T(8,128)S(1)} fusion(f32[2,8,256,256]{3,2,1,0:T(8,128)} %bitcast.49, f32[2,8,256,512]{3,2,1,0:T(8,128)} %bitcast.50, f32[2]{0:T(128)S(1)} %convert_bitcast_fusion.1), kind=kOutput, calls=%fused_computation.6 | convolution fusion | flops 6442713088 | bytes 13631496 | tf_op jit(solution)/shard_map/kmij,kmjc->kic/dot_general | solution.py:54
  236.8 1.0 fusion.21
  237.8 1.0 fusion.20
  238.9 0.7 fusion.1
  239.6 1.0 fusion.22
  240.6 0.1 pad_maximum_fusion
  240.8 5.5 %collective-permute-start.2 = (f32[2,128,768]{1,2,0:T(8,128)S(1)}, f32[2,128,768]{1,2,0:T(8,128)}, u32[]{:S(2)}, u32[]{:S(2)}) collective-permute-start(f32[2,128,768]{1,2,0:T(8,128)S(1)} %slice_select_fusion), channel_id=1, source_target_pairs={{0,1},{1,0},{2,3},{3,2},{4,5},{5,4},{6,7},{7,6},{8,9},{9,8},{10,11... | collective-permute-start | bytes 2359304 | tf_op jit(solution)/shard_map/ppermute | solution.py:30
  246.4 2.0 collective-permute-done.2
  248.4 1.2 select_add_fusion
  249.7 1.6 constant_dynamic-slice_fusion.2
  251.2 2.1 copy.105
  253.3 2.8 collective-permute-start.5
  256.1 0.9 copy.103
  257.0 0.3 collective-permute-start.4
  257.3 0.9 copy.101
  258.2 0.8 collective-permute-start.3
  259.0 5.4 %collective-permute-done.5 = f32[2,32,768]{2,1,0:T(8,128)} collective-permute-done((f32[2,32,768]{2,1,0:T(8,128)}, f32[2,32,768]{2,1,0:T(8,128)}, u32[]{:S(2)}, u32[]{:S(2)}) %collective-permute-start.5) | collective-permute-done | bytes 196640 | tf_op jit(solution)/shard_map/ppermute | solution.py:34
  264.4 1.2 copy.106
  265.6 2.1 copy.104
  267.7 2.1 collective-permute-done.3
  269.7 1.2 copy.102
  270.9 1.6 add_add_fusion
  272.6 0.2 copy.107
  272.8 1.5 collective-permute-start.8
  274.4 0.7 collective-permute-start.6
  275.1 0.2 copy.110
  275.3 3.6 %collective-permute-done.8 = f32[2,32,768]{2,1,0:T(8,128)S(1)} collective-permute-done((f32[2,32,768]{2,1,0:T(8,128)S(1)}, f32[2,32,768]{2,1,0:T(8,128)S(1)}, u32[]{:S(2)}, u32[]{:S(2)}) %collective-permute-start.8) | collective-permute-done | bytes 196640 | tf_op jit(solution)/shard_map/ppermute | solution.py:34
  278.9 2.0 collective-permute-done.7
  280.9 5.4 %collective-permute-done.6 = f32[2,32,768]{2,1,0:T(8,128)S(1)} collective-permute-done((f32[2,32,768]{2,1,0:T(8,128)S(1)}, f32[2,32,768]{2,1,0:T(8,128)S(1)}, u32[]{:S(2)}, u32[]{:S(2)}) %collective-permute-start.6) | collective-permute-done | bytes 196640 | tf_op jit(solution)/shard_map/ppermute | solution.py:34
  286.3 0.6 gather_fusion.2
  287.0 0.9 collective-permute-start.9
  287.9 1.9 collective-permute-done.9
  289.9 0.1 maximum_select_fusion
  290.0 1.1 slice_subtract_fusion
  291.1 0.7 fusion.23
  291.8 1.1 fusion.2
  293.0 16.9 %collective-permute-done.10 = f32[2,256,256]{2,1,0:T(8,128)S(1)} collective-permute-done((f32[2,256,256]{2,1,0:T(8,128)S(1)}, f32[2,256,256]{2,1,0:T(8,128)S(1)}, u32[]{:S(2)}, u32[]{:S(2)}) %collective-permute-start.10) | collective-permute-done | bytes 524320 | tf_op jit(solution)/shard_map/ppermute | solution.py:16
  309.9 1.0 collective-permute-start.11
  310.9 1.1 fusion.24
  311.9 1.9 broadcast_multiply_fusion
  313.9 1.1 select_subtract_fusion
  (41 shorter events, 0.7 us)
Async XLA Ops:
  7.2 1.1 copy-start
  8.2 11.7 %copy-start.8 = (s32[64,8]{0,1:T(8,128)S(1)}, s32[64,8]{0,1:T(8,128)}, u32[]{:S(2)}) copy-start(s32[64,8]{0,1:T(8,128)} %param.10) | copy-start | bytes 6148
  11.2 20.7 %collective-permute-start = (f32[2,288,256]{2,1,0:T(8,128)S(1)}, f32[2,288,256]{2,1,0:T(8,128)S(1)}, u32[]{:S(2)}, u32[]{:S(2)}) collective-permute-start(f32[2,288,256]{2,1,0:T(8,128)S(1)} %pad_maximum_fusion.3), channel_id=1, source_target_pairs={{0,248},{8,0},{16,8},{24,16},{32,24},{40,32},{48,40},{56,48},{64,5... | collective-permute-start | bytes 1769480 | tf_op jit(solution)/shard_map/ppermute | solution.py:16
  28.2 11.1 %copy-start.9 = (s32[2,1]{0,1:T(1,128)S(1)}, s32[2,1]{0,1:T(1,128)}, u32[]{:S(2)}) copy-start(s32[2,1]{0,1:T(1,128)} %param.13) | copy-start | bytes 28
  28.2 11.1 %copy-start.4 = (f32[2,256,256]{2,1,0:T(8,128)S(1)}, f32[2,256,256]{2,1,0:T(8,128)}, u32[]{:S(2)}) copy-start(f32[2,256,256]{2,1,0:T(8,128)} %param.12) | copy-start | bytes 1572868
  28.2 11.1 %copy-start.7 = (f32[2,256,256]{2,1,0:T(8,128)S(1)}, f32[2,256,256]{2,1,0:T(8,128)}, u32[]{:S(2)}) copy-start(f32[2,256,256]{2,1,0:T(8,128)} %param.11) | copy-start | bytes 1572868
  31.9 189.6 %all-to-all-start = ((f32[32,256,256]{2,1,0:T(8,128)}), f32[32,256,256]{2,1,0:T(8,128)}, u32[]{:S(2)}, u32[]{:S(2)}) async-start(f32[32,256,256]{2,1,0:T(8,128)} %shard_map.128), calls=%async_computation | async-start | bytes 16777216 | tf_op jit(solution)/shard_map/all_to_all | solution.py:182
  39.2 187.2 %all-gather.2.cloned.1.call-start = ((), (), s32[]{:S(2)}) async-start(), calls=%async_computation.1 | async-start | bytes 9437184 | tf_op jit(solution)/shard_map/all_gather | solution.py:188
  57.8 181.1 %copy-start.2 = (f32[2,256,256]{2,1,0:T(8,128)}, f32[2,256,256]{2,1,0:T(8,128)S(1)}, u32[]{:S(2)}) copy-start(f32[2,256,256]{2,1,0:T(8,128)S(1)} %all_gather.7) | copy-start | bytes 1572868
  236.8 2.1 copy-start.1
  240.8 7.6 %collective-permute-start.2 = (f32[2,128,768]{1,2,0:T(8,128)S(1)}, f32[2,128,768]{1,2,0:T(8,128)}, u32[]{:S(2)}, u32[]{:S(2)}) collective-permute-start(f32[2,128,768]{1,2,0:T(8,128)S(1)} %slice_select_fusion), channel_id=1, source_target_pairs={{0,1},{1,0},{2,3},{3,2},{4,5},{5,4},{6,7},{7,6},{8,9},{9,8},{10,11... | collective-permute-start | bytes 2359304 | tf_op jit(solution)/shard_map/ppermute | solution.py:30
  246.4 26.2 %collective-permute-start.1 = (f32[2,256,256]{2,1,0:T(8,128)S(1)}, f32[2,256,256]{2,1,0:T(8,128)}, u32[]{:S(2)}, u32[]{:S(2)}) collective-permute-start(f32[2,256,256]{2,1,0:T(8,128)S(1)} %fusion.1), channel_id=1, source_target_pairs={{0,8},{8,16},{16,24},{24,32},{32,40},{40,48},{48,56},{56,64},{64,7... | collective-permute-start | bytes 1572872 | tf_op jit(solution)/shard_map/ppermute | solution.py:16
  253.3 11.1 %collective-permute-start.5 = (f32[2,32,768]{2,1,0:T(8,128)}, f32[2,32,768]{2,1,0:T(8,128)}, u32[]{:S(2)}, u32[]{:S(2)}) collective-permute-start(f32[2,32,768]{2,1,0:T(8,128)} %copy.105), channel_id=1, source_target_pairs={{0,6},{1,7},{2,0},{3,1},{4,2},{5,3},{6,4},{7,5},{8,14},{9,15},{10,... | collective-permute-start | bytes 589832 | tf_op jit(solution)/shard_map/ppermute | solution.py:34
  257.0 8.6 %collective-permute-start.4 = (f32[2,32,768]{2,1,0:T(8,128)}, f32[2,32,768]{2,1,0:T(8,128)}, u32[]{:S(2)}, u32[]{:S(2)}) collective-permute-start(f32[2,32,768]{2,1,0:T(8,128)} %copy.103), channel_id=1, source_target_pairs={{0,4},{1,5},{2,6},{3,7},{4,0},{5,1},{6,2},{7,3},{8,12},{9,13},{10,... | collective-permute-start | bytes 589832 | tf_op jit(solution)/shard_map/ppermute | solution.py:34
  258.2 11.6 %collective-permute-start.3 = (f32[2,32,768]{2,1,0:T(8,128)}, f32[2,32,768]{2,1,0:T(8,128)S(1)}, u32[]{:S(2)}, u32[]{:S(2)}) collective-permute-start(f32[2,32,768]{2,1,0:T(8,128)} %copy.101), channel_id=1, source_target_pairs={{0,2},{1,3},{2,4},{3,5},{4,6},{5,7},{6,0},{7,1},{8,10},{9,11},{10,... | collective-permute-start | bytes 589832 | tf_op jit(solution)/shard_map/ppermute | solution.py:34
  272.8 6.0 %collective-permute-start.8 = (f32[2,32,768]{2,1,0:T(8,128)S(1)}, f32[2,32,768]{2,1,0:T(8,128)S(1)}, u32[]{:S(2)}, u32[]{:S(2)}) collective-permute-start(f32[2,32,768]{2,1,0:T(8,128)S(1)} %copy.107), channel_id=1, source_target_pairs={{0,6},{1,7},{2,0},{3,1},{4,2},{5,3},{6,4},{7,5},{8,14},{9,15},{10,... | collective-permute-start | bytes 589832 | tf_op jit(solution)/shard_map/ppermute | solution.py:34
  274.4 6.5 %collective-permute-start.7 = (f32[2,32,768]{2,1,0:T(8,128)S(1)}, f32[2,32,768]{2,1,0:T(8,128)S(1)}, u32[]{:S(2)}, u32[]{:S(2)}) collective-permute-start(f32[2,32,768]{2,1,0:T(8,128)S(1)} %copy.107), channel_id=1, source_target_pairs={{0,4},{1,5},{2,6},{3,7},{4,0},{5,1},{6,2},{7,3},{8,12},{9,13},{10,... | collective-permute-start | bytes 589832 | tf_op jit(solution)/shard_map/ppermute | solution.py:34
  274.4 11.9 %collective-permute-start.6 = (f32[2,32,768]{2,1,0:T(8,128)S(1)}, f32[2,32,768]{2,1,0:T(8,128)S(1)}, u32[]{:S(2)}, u32[]{:S(2)}) collective-permute-start(f32[2,32,768]{2,1,0:T(8,128)S(1)} %copy.107), channel_id=1, source_target_pairs={{0,2},{1,3},{2,4},{3,5},{4,6},{5,7},{6,0},{7,1},{8,10},{9,11},{10,... | collective-permute-start | bytes 589832 | tf_op jit(solution)/shard_map/ppermute | solution.py:34
  287.0 3.0 copy-start.5
  287.0 2.8 collective-permute-start.9
  290.0 1.1 copy-start.3
  291.1 1.8 copy-start.6
  292.9 17.0 %collective-permute-start.10 = (f32[2,256,256]{2,1,0:T(8,128)S(1)}, f32[2,256,256]{2,1,0:T(8,128)S(1)}, u32[]{:S(2)}, u32[]{:S(2)}) collective-permute-start(f32[2,256,256]{2,1,0:T(8,128)S(1)} %fusion.2), channel_id=1, source_target_pairs={{0,8},{8,16},{16,24},{24,32},{32,40},{40,48},{48,56},{56,64},{64,7... | collective-permute-start | bytes 1572872 | tf_op jit(solution)/shard_map/ppermute | solution.py:16
  309.9 4.0 %collective-permute-start.11 = (f32[2,256,256]{2,1,0:T(8,128)S(1)}, f32[2,256,256]{2,1,0:T(8,128)S(1)}, u32[]{:S(2)}, u32[]{:S(2)}) collective-permute-start(f32[2,256,256]{2,1,0:T(8,128)S(1)} %collective-permute-done.10), channel_id=1, source_target_pairs={{0,1},{1,0},{2,3},{3,2},{4,5},{5,4},{6,7},{7,6},{8,9},{9,8},{10,11... | collective-permute-start | bytes 1572872 | tf_op jit(solution)/shard_map/ppermute | solution.py:212
Sparse Core Ops, SparseCore 0:
  41.9 55.2 all-gather.1

commit v7 on v6

--- a/solution.py
+++ b/solution.py
@@ -16,7 +16,12 @@
     return lax.ppermute(shard, axis, [(i, (i + by) % length) for i in range(length)])
 
 
-def row_sum(x, arrive=None):
+def _towards(value, by):
+    length = lax.axis_size("row")
+    return lax.ppermute(value, "row", [(i, (i + 2 * by) % length) for i in range(length)])
+
+
+def row_scatter(x):
     length = lax.axis_size("row")
     row_here = lax.axis_index("row")
     core = row_here % 2
@@ -26,28 +31,43 @@
     lo, hi = x[:, :half], x[:, half:]
     mine = jnp.where(core == 0, lo, hi)
     other = jnp.where(core == 0, hi, lo)
-    partner = [(i, i ^ 1) for i in range(length)]
-    part = mine + lax.ppermute(other, "row", partner)
+    part = mine + lax.ppermute(other, "row", [(i, i ^ 1) for i in range(length)])
     quarter = half // chips
-
-    def towards(value, by):
-        return lax.ppermute(value, "row", [(i, (i + 2 * by) % length) for i in range(length)])
-
     total = lax.dynamic_slice_in_dim(part, chip * quarter, quarter, axis=1)
     for by in range(1, chips):
         target = (chip + by) % chips
-        total = total + towards(lax.dynamic_slice_in_dim(part, target * quarter, quarter, axis=1), by)
-    if arrive is not None:
-        arrive, total = lax.optimization_barrier((arrive, total))
-    pieces = [total] + [towards(total, by) for by in range(1, chips)]
+        total = total + _towards(
+            lax.dynamic_slice_in_dim(part, target * quarter, quarter, axis=1), by
+        )
+    return total
+
+
+def row_rows(piece):
+    length = lax.axis_size("row")
+    row_here = lax.axis_index("row")
+    core = row_here % 2
+    chip = row_here // 2
+    chips = length // 2
+    pieces = [piece] + [_towards(piece, by) for by in range(1, chips)]
     stacked = jnp.stack(pieces)
     order = (chip - jnp.arange(chips, dtype=jnp.int32)) % chips
-    part = stacked[order].transpose(1, 0, 2, 3).reshape(part.shape)
-    got = lax.ppermute(part, "row", partner)
-    full = jnp.where(
+    part = stacked[order].transpose(1, 0, 2, 3).reshape(
+        piece.shape[0], chips * piece.shape[1], piece.shape[2]
+    )
+    got = lax.ppermute(part, "row", [(i, i ^ 1) for i in range(length)])
+    return jnp.where(
         core == 0, jnp.concatenate([part, got], axis=1), jnp.concatenate([got, part], axis=1)
     )
-    return full, arrive
+
+
+def held_rows(x):
+    length = lax.axis_size("row")
+    row_here = lax.axis_index("row")
+    chips = length // 2
+    half = x.shape[1] // 2
+    quarter = half // chips
+    first = (row_here % 2) * half + (row_here // 2) * quarter
+    return lax.dynamic_slice_in_dim(x, first, quarter, axis=1)
 
 
 def product(form, left, right):
@@ -169,7 +189,6 @@
     cols_here = sigma_anc.shape[1] // B
     row_count = lax.axis_size("row")
     row_here = lax.axis_index("row")
-    core = row_here % 2
     keep_own2 = mask2.astype(jnp.float32)
     factor2_own = keep_own2[:, :, None] * product("kij,kjc->kic", panel2, diag_inv2)
     piece = B // row_count
@@ -201,21 +220,21 @@
         ],
         axis=-1,
     )
-    summed, pre2_child = row_sum(terms, pre2_child)
+    summed = row_scatter(terms)
+    pre2_child, summed = lax.optimization_barrier((pre2_child, summed))
     gram1 = product("kji,kjc->kic", diag_inv1, diag_inv1)
-    sel1_diag = gram1 - summed[:, :, :B]
-    sel2_parent = -(product("kij,kjc->kic", sel1_diag, up_parent) + summed[:, :, B : 2 * B])
-    down = product("kji,kjc->kic", up_parent, sel2_parent) + summed[:, :, 2 * B :]
-
-    partner = [(i, i ^ 1) for i in range(row_count)]
-    got = shifted(jnp.where(core == 0, sel2_parent, down), "own", 1)
-    other = lax.ppermute(got, "row", partner)
-    sel2_parent_child = jnp.where(core == 0, got, other)
-    down_child = jnp.where(core == 0, other, got)
+    diag_piece = held_rows(gram1) - summed[:, :, :B]
+    parent_piece = -(product("kij,kjc->kic", diag_piece, up_parent) + summed[:, :, B : 2 * B])
+    sel1_diag = row_rows(diag_piece)
+    child = row_rows(
+        shifted(jnp.concatenate([parent_piece, summed[:, :, 2 * B :]], axis=-1), "own", 1)
+    )
+    sel2_parent_child = child[:, :, :B]
+    up_own_full = product("kij,kjc->kic", parent_block2, diag_inv2)
 
     sel2_panel = keep_own2[:, :, None] * pre2_child
     gram2 = product("kji,kjc->kic", diag_inv2, diag_inv2)
-    sel2_diag = gram2 - down_child
+    sel2_diag = gram2 - product("kji,kjc->kic", up_own_full, sel2_parent_child) - child[:, :, B:]
     return (sel1_panel, sel1_diag, sel2_parent_child, sel2_panel, sel2_diag)
 
 

time: 322 us -> 301 us (0.935)
  waiting for transfers between devices: 207 us -> 188 us
  local copies, waits for them, and re-layouts: 13.1 us -> 4.84 us
  starting transfers between devices: 29.6 us -> 33.3 us
    ppermute x3, waiting for transfers between devices: 20.5 us -> 7.76 us  [shifted(): lax.ppermute(shard, axis, [(i, (i + by) % length) for i in range(length)])]
    dynamic_slice x4 -> x1, local copies, waits for them, and re-layouts: 5.44 us -> 0.05 us  [row_scatter(): lax.dynamic_slice_in_dim(part, target * quarter, quarter, axis=1)]
    ppermute x9 -> x12, waiting for transfers between devices: 22.4 us -> 17.1 us  [the longest x9 14.9 us: _towards(): lax.ppermute(value, 'row', [(i, (i + 2 * by) % length) for i in range(len...]
    ppermute x3 -> x0, local copies, waits for them, and re-layouts: 4.46 us -> none  [towards(): lax.ppermute(value, 'row', [(i, (i + 2 * by) % length) for i in range(len...]
    ppermute x9 -> x12, starting transfers between devices: 13.5 us -> 17.2 us  [the longest x9 7.48 us: _towards(): lax.ppermute(value, 'row', [(i, (i + 2 * by) % length) for i in range(len...]
    dot_general x12 -> x13, matrix products: 21.6 us -> 22.7 us  [product(): return jnp.einsum(form, left, right, precision=HIGH)]
  transfers between devices with their start and end apart: 14 -> 17, of which waited for: 10 -> 8; matrix products, arithmetic and copies ran while one was open for 7% -> 5% of each run, Pallas kernels for 4% -> 4%
where the time goes in v7:
time: 301 us; the launch traced here: 299 us
  waiting for transfers between devices  188 us (62%)
  starting transfers between devices  33.3 us (11%)
  matrix products  22.7 us (8%)
  blocking collectives  15.3 us (5%)
  between operations  14.5 us (5%)
  Pallas kernels  11.3 us (4%)
  other arithmetic  8.9 us (3%)
  local copies, waits for them, and re-layouts  4.84 us (2%)
    all_to_all x1, waiting for transfers between devices, on_device(): lax.all_to_all(outgoing, 'own', split_axis=0, concat_axis=0, tiled=True)  163 us
    dot_general x13, matrix products, product(): return jnp.einsum(form, left, right, precision=HIGH)  22.7 us
    all_gather x1, blocking collectives, on_device(): up_parent = lax.all_gather(payload[:, B:], 'row', axis=1, tiled=True)  15.3 us
    ppermute x9, waiting for transfers between devices, _towards(): lax.ppermute(value, 'row', [(i, (i + 2 * by) % length) for i in range(len...  14.9 us
    ppermute x3, starting transfers between devices, shifted(): lax.ppermute(shard, axis, [(i, (i + by) % length) for i in range(length)])  8.76 us
    ppermute x3, waiting for transfers between devices, shifted(): lax.ppermute(shard, axis, [(i, (i + by) % length) for i in range(length)])  7.76 us
    ppermute x9, starting transfers between devices, _towards(): lax.ppermute(value, 'row', [(i, (i + 2 * by) % length) for i in range(len...  7.48 us
    all_to_all x1, starting transfers between devices, on_device(): lax.all_to_all(outgoing, 'own', split_axis=0, concat_axis=0, tiled=True)  7.32 us
  transfers between devices with their start and end apart: 17, of which 8 were waited for; matrix products, arithmetic and copies ran while one was open for 5% of the time, Pallas kernels for 4%

profile of v7, /device:TPU:1, one launch (start us, length us, event | category | flops | bytes accessed | tf_op | source)
XLA Modules:
  0.0 299.2 jit_solution(3207905032456212015)
XLA Ops:
  7.2 0.7 convert_bitcast_fusion
  7.9 0.3 copy-done
  8.2 1.2 fusion.3
  9.5 1.7 convolution_multiply_fusion.1
  11.2 8.7 %collective-permute-start = (f32[2,288,256]{2,1,0:T(8,128)S(1)}, f32[2,288,256]{2,1,0:T(8,128)S(1)}, u32[]{:S(2)}, u32[]{:S(2)}) collective-permute-start(f32[2,288,256]{2,1,0:T(8,128)S(1)} %pad_maximum_fusion.2), channel_id=1, source_target_pairs={{0,248},{8,0},{16,8},{24,16},{32,24},{40,32},{48,40},{56,48},{64,5... | collective-permute-start | bytes 1769480 | tf_op jit(solution)/shard_map/ppermute | solution.py:16
  19.9 0.8 copy.66
  20.7 0.1 constant_dynamic-slice_fusion.3
  20.8 0.1 copy.97
  20.9 0.1 copy.69
  21.0 0.1 fusion.8
  21.1 0.7 gather_fusion.1
  21.8 0.7 clamp_reduce_fusion
  22.5 6.4 %shard_map.128 = f32[32,256,256]{2,1,0:T(8,128)} custom-call(s32[32]{0:T(128)} %get-tuple-element.14.rows_ref, s32[32]{0:T(128)} %get-tuple-element.13.cols_ref, f32[2048,512]{1,0:T(8,128)} %src_ref.1), custom_call_target="tpu_custom_call" | custom-call | bytes 12582912 | tf_op jit(solution)/shard_map/pallas_call | solution.py:108
  28.9 3.0 collective-permute-done
  31.9 7.3 %all-to-all-start = ((f32[32,256,256]{2,1,0:T(8,128)}), f32[32,256,256]{2,1,0:T(8,128)}, u32[]{:S(2)}, u32[]{:S(2)}) async-start(f32[32,256,256]{2,1,0:T(8,128)} %shard_map.128), calls=%async_computation | async-start | bytes 16777216 | tf_op jit(solution)/shard_map/all_to_all | solution.py:201
  39.3 0.7 convolution_multiply_fusion
  40.0 0.1 slice_multiply_fusion
  40.1 1.2 pad_maximum_fusion.1
  41.3 0.6 gather_fusion
  41.9 0.1 gather.15
  42.0 0.5 fusion.14.which_ref
  42.5 15.3 %all_gather.7 = f32[2,256,256]{2,1,0:T(8,128)S(1)} all-gather(f32[2,32,256]{2,1,0:T(8,128)S(1)} %slice.35), channel_id=1, replica_groups=mesh['own'=32,'row'=8] {'row'}, dimensions={1}, use_global_device_ids=true | all-gather | bytes 589824 | tf_op jit(solution)/shard_map/all_gather | solution.py:208
  57.8 163.5 %all-to-all-done.src_ref = f32[32,256,256]{2,1,0:T(8,128)} async-done(((f32[32,256,256]{2,1,0:T(8,128)}), f32[32,256,256]{2,1,0:T(8,128)}, u32[]{:S(2)}, u32[]{:S(2)}) %all-to-all-start) | async-done | bytes 8388640 | tf_op jit(solution)/shard_map/all_to_all | solution.py:201
  221.3 4.9 %shard_map.129 = f32[16,256,256]{2,1,0:T(8,128)} custom-call(s32[16]{0:T(128)} %fusion.14.which_ref, f32[32,256,256]{2,1,0:T(8,128)} %all-to-all-done.src_ref), custom_call_target="tpu_custom_call" | custom-call | bytes 8388608 | tf_op jit(solution)/shard_map/pallas_call | solution.py:174
  226.2 10.2 %fusion = f32[2,256,512]{2,1,0:T(8,128)S(1)} fusion(f32[2,8,256,256]{3,2,1,0:T(8,128)} %bitcast.58, f32[2,8,256,512]{3,2,1,0:T(8,128)} %bitcast.59, f32[2]{0:T(128)S(1)} %convert_bitcast_fusion.1), kind=kOutput, calls=%fused_computation.6 | convolution fusion | flops 6442713088 | bytes 13631496 | tf_op jit(solution)/shard_map/kmij,kmjc->kic/dot_general | solution.py:74
  236.4 0.1 slice_negate_fusion
  236.5 1.1 fusion.17
  237.6 1.1 fusion.16
  238.7 0.7 fusion.2
  239.3 0.8 copy-done.6
  240.1 1.0 fusion.18
  241.2 0.1 pad_maximum_fusion
  241.3 1.0 slice_select_fusion
  242.3 5.6 %collective-permute-start.2 = (f32[2,128,768]{2,1,0:T(8,128)}, f32[2,128,768]{2,1,0:T(8,128)}, u32[]{:S(2)}, u32[]{:S(2)}) collective-permute-start(f32[2,128,768]{2,1,0:T(8,128)} %slice_select_fusion), channel_id=1, source_target_pairs={{0,1},{1,0},{2,3},{3,2},{4,5},{5,4},{6,7},{7,6},{8,9},{9,8},{10,11... | collective-permute-start | bytes 2359304 | tf_op jit(solution)/shard_map/ppermute | solution.py:34
  247.9 2.3 collective-permute-done.2
  250.1 1.3 select_add_fusion
  251.5 2.7 collective-permute-start.5
  254.2 0.3 collective-permute-start.4
  254.6 0.7 collective-permute-start.3
  255.2 1.1 fusion.15
  256.3 5.9 %collective-permute-done.5 = f32[2,32,768]{2,1,0:T(8,128)S(1)} collective-permute-done((f32[2,32,768]{2,1,0:T(8,128)S(1)}, f32[2,32,768]{2,1,0:T(8,128)S(1)}, u32[]{:S(2)}, u32[]{:S(2)}) %collective-permute-start.5) | collective-permute-done | bytes 196640 | tf_op jit(solution)/shard_map/ppermute | solution.py:21
  262.2 4.6 %collective-permute-done.3 = f32[2,32,768]{2,1,0:T(8,128)S(1)} collective-permute-done((f32[2,32,768]{2,1,0:T(8,128)S(1)}, f32[2,32,768]{2,1,0:T(8,128)S(1)}, u32[]{:S(2)}, u32[]{:S(2)}) %collective-permute-start.3) | collective-permute-done | bytes 196640 | tf_op jit(solution)/shard_map/ppermute | solution.py:21
  266.7 0.1 add_add_fusion
  266.9 0.4 add_negate_fusion
  267.3 0.1 collective-permute-start.10
  267.4 1.1 fusion.19
  268.4 1.0 collective-permute-start.8
  269.4 0.4 collective-permute-start.7
  269.9 0.7 collective-permute-start.6
  270.6 4.8 %collective-permute-done.10 = f32[2,32,512]{2,1,0:T(8,128)S(1)} collective-permute-done((f32[2,32,512]{2,1,0:T(8,128)S(1)}, f32[2,32,512]{2,1,0:T(8,128)S(1)}, u32[]{:S(2)}, u32[]{:S(2)}) %collective-permute-start.10) | collective-permute-done | bytes 131104 | tf_op jit(solution)/shard_map/ppermute | solution.py:16
  275.4 0.5 collective-permute-start.13
  275.9 0.3 collective-permute-start.12
  276.3 0.7 collective-permute-start.11
  277.0 0.6 gather_fusion.2
  277.6 2.5 collective-permute-start.9
  280.2 1.2 collective-permute-done.12
  281.3 3.3 %collective-permute-done.11 = f32[2,32,512]{2,1,0:T(8,128)S(1)} collective-permute-done((f32[2,32,512]{2,1,0:T(8,128)S(1)}, f32[2,32,512]{2,1,0:T(8,128)S(1)}, u32[]{:S(2)}, u32[]{:S(2)}) %collective-permute-start.11) | collective-permute-done | bytes 131104 | tf_op jit(solution)/shard_map/ppermute | solution.py:21
  284.6 0.6 gather_fusion.3
  285.3 1.6 collective-permute-start.14
  286.9 1.0 fusion.20
  288.0 0.9 broadcast_multiply_fusion
  288.9 1.9 maximum_select_fusion.1
  290.7 0.1 maximum_select_fusion
  290.9 1.5 fusion.1
  (50 shorter events, 0.5 us)
Async XLA Ops:
  7.2 1.1 copy-start
  11.2 20.7 %collective-permute-start = (f32[2,288,256]{2,1,0:T(8,128)S(1)}, f32[2,288,256]{2,1,0:T(8,128)S(1)}, u32[]{:S(2)}, u32[]{:S(2)}) collective-permute-start(f32[2,288,256]{2,1,0:T(8,128)S(1)} %pad_maximum_fusion.2), channel_id=1, source_target_pairs={{0,248},{8,0},{16,8},{24,16},{32,24},{40,32},{48,40},{56,48},{64,5... | collective-permute-start | bytes 1769480 | tf_op jit(solution)/shard_map/ppermute | solution.py:16
  28.9 10.4 %copy-start.11 = (s32[2,1]{0,1:T(1,128)S(1)}, s32[2,1]{0,1:T(1,128)}, u32[]{:S(2)}) copy-start(s32[2,1]{0,1:T(1,128)} %param.13) | copy-start | bytes 28
  28.9 10.4 %copy-start.2 = (f32[2,256,256]{2,1,0:T(8,128)S(1)}, f32[2,256,256]{2,1,0:T(8,128)}, u32[]{:S(2)}) copy-start(f32[2,256,256]{2,1,0:T(8,128)} %param.12) | copy-start | bytes 1572868
  28.9 10.4 %copy-start.8 = (f32[2,256,256]{2,1,0:T(8,128)S(1)}, f32[2,256,256]{2,1,0:T(8,128)}, u32[]{:S(2)}) copy-start(f32[2,256,256]{2,1,0:T(8,128)} %param.11) | copy-start | bytes 1572868
  31.9 189.4 %all-to-all-start = ((f32[32,256,256]{2,1,0:T(8,128)}), f32[32,256,256]{2,1,0:T(8,128)}, u32[]{:S(2)}, u32[]{:S(2)}) async-start(f32[32,256,256]{2,1,0:T(8,128)} %shard_map.128), calls=%async_computation | async-start | bytes 16777216 | tf_op jit(solution)/shard_map/all_to_all | solution.py:201
  39.2 187.0 %all-gather.2.cloned.1.call-start = ((), (), s32[]{:S(2)}) async-start(), calls=%async_computation.1 | async-start | bytes 9437184 | tf_op jit(solution)/shard_map/all_gather | solution.py:207
  57.8 180.9 %copy-start.3 = (f32[2,256,256]{2,1,0:T(8,128)}, f32[2,256,256]{2,1,0:T(8,128)S(1)}, u32[]{:S(2)}) copy-start(f32[2,256,256]{2,1,0:T(8,128)S(1)} %all_gather.7) | copy-start | bytes 1572868
  236.5 4.8 %copy-start.1 = (f32[2,256,256]{2,1,0:T(8,128)}, f32[2,256,256]{2,1,0:T(8,128)S(1)}, u32[]{:S(2)}) copy-start(f32[2,256,256]{2,1,0:T(8,128)S(1)} %slice_negate_fusion) | copy-start | bytes 1572868
  239.3 0.8 copy-start.6
  242.3 24.6 %copy-start.4 = (f32[2,256,256]{2,1,0:T(8,128)S(1)}, f32[2,256,256]{2,1,0:T(8,128)}, u32[]{:S(2)}) copy-start(f32[2,256,256]{2,1,0:T(8,128)} %copy-done.3) | copy-start | bytes 1572868
  242.3 7.8 %collective-permute-start.2 = (f32[2,128,768]{2,1,0:T(8,128)}, f32[2,128,768]{2,1,0:T(8,128)}, u32[]{:S(2)}, u32[]{:S(2)}) collective-permute-start(f32[2,128,768]{2,1,0:T(8,128)} %slice_select_fusion), channel_id=1, source_target_pairs={{0,1},{1,0},{2,3},{3,2},{4,5},{5,4},{6,7},{7,6},{8,9},{9,8},{10,11... | collective-permute-start | bytes 2359304 | tf_op jit(solution)/shard_map/ppermute | solution.py:34
  247.9 18.9 %collective-permute-start.1 = (f32[2,256,256]{2,1,0:T(8,128)}, f32[2,256,256]{2,1,0:T(8,128)S(1)}, u32[]{:S(2)}, u32[]{:S(2)}) collective-permute-start(f32[2,256,256]{2,1,0:T(8,128)} %copy-done.6), channel_id=1, source_target_pairs={{0,8},{8,16},{16,24},{24,32},{32,40},{40,48},{48,56},{56,64},{64,7... | collective-permute-start | bytes 1572872 | tf_op jit(solution)/shard_map/ppermute | solution.py:16
  251.5 10.7 %collective-permute-start.5 = (f32[2,32,768]{2,1,0:T(8,128)S(1)}, f32[2,32,768]{2,1,0:T(8,128)S(1)}, u32[]{:S(2)}, u32[]{:S(2)}) collective-permute-start(f32[2,32,768]{2,1,0:T(8,128)S(1)} %get-tuple-element.16), channel_id=1, source_target_pairs={{0,6},{1,7},{2,0},{3,1},{4,2},{5,3},{6,4},{7,5},{8,14},{9,15},{10,... | collective-permute-start | bytes 589832 | tf_op jit(solution)/shard_map/ppermute | solution.py:21
  254.2 8.0 %collective-permute-start.4 = (f32[2,32,768]{2,1,0:T(8,128)S(1)}, f32[2,32,768]{2,1,0:T(8,128)S(1)}, u32[]{:S(2)}, u32[]{:S(2)}) collective-permute-start(f32[2,32,768]{2,1,0:T(8,128)S(1)} %get-tuple-element.17), channel_id=1, source_target_pairs={{0,4},{1,5},{2,6},{3,7},{4,0},{5,1},{6,2},{7,3},{8,12},{9,13},{10,... | collective-permute-start | bytes 589832 | tf_op jit(solution)/shard_map/ppermute | solution.py:21
  254.6 12.2 %collective-permute-start.3 = (f32[2,32,768]{2,1,0:T(8,128)S(1)}, f32[2,32,768]{2,1,0:T(8,128)S(1)}, u32[]{:S(2)}, u32[]{:S(2)}) collective-permute-start(f32[2,32,768]{2,1,0:T(8,128)S(1)} %get-tuple-element.15), channel_id=1, source_target_pairs={{0,2},{1,3},{2,4},{3,5},{4,6},{5,7},{6,0},{7,1},{8,10},{9,11},{10,... | collective-permute-start | bytes 589832 | tf_op jit(solution)/shard_map/ppermute | solution.py:21
  256.3 30.6 %copy-start.7 = (f32[2,256,256]{2,1,0:T(8,128)S(1)}, f32[2,256,256]{2,1,0:T(8,128)}, u32[]{:S(2)}) copy-start(f32[2,256,256]{2,1,0:T(8,128)} %param.14) | copy-start | bytes 1572868
  266.8 10.2 %copy-start.9 = (f32[2,256,256]{2,1,0:T(8,128)}, f32[2,256,256]{2,1,0:T(8,128)S(1)}, u32[]{:S(2)}) copy-start(f32[2,256,256]{2,1,0:T(8,128)S(1)} %collective-permute-done.1) | copy-start | bytes 1572868
  267.3 8.1 %collective-permute-start.10 = (f32[2,32,512]{2,1,0:T(8,128)S(1)}, f32[2,32,512]{2,1,0:T(8,128)S(1)}, u32[]{:S(2)}, u32[]{:S(2)}) collective-permute-start(f32[2,32,512]{2,1,0:T(8,128)S(1)} %pad_maximum_fusion.5), channel_id=1, source_target_pairs={{0,8},{8,16},{16,24},{24,32},{32,40},{40,48},{48,56},{56,64},{64,7... | collective-permute-start | bytes 393224 | tf_op jit(solution)/shard_map/ppermute | solution.py:16
  268.4 7.8 %collective-permute-start.8 = (f32[2,32,256]{2,1,0:T(8,128)S(1)}, f32[2,32,256]{2,1,0:T(8,128)S(1)}, u32[]{:S(2)}, u32[]{:S(2)}) collective-permute-start(f32[2,32,256]{2,1,0:T(8,128)S(1)} %slice_subtract_fusion), channel_id=1, source_target_pairs={{0,6},{1,7},{2,0},{3,1},{4,2},{5,3},{6,4},{7,5},{8,14},{9,15},{10,... | collective-permute-start | bytes 196616 | tf_op jit(solution)/shard_map/ppermute | solution.py:21
  269.4 7.5 %collective-permute-start.7 = (f32[2,32,256]{2,1,0:T(8,128)S(1)}, f32[2,32,256]{2,1,0:T(8,128)S(1)}, u32[]{:S(2)}, u32[]{:S(2)}) collective-permute-start(f32[2,32,256]{2,1,0:T(8,128)S(1)} %slice_subtract_fusion), channel_id=1, source_target_pairs={{0,4},{1,5},{2,6},{3,7},{4,0},{5,1},{6,2},{7,3},{8,12},{9,13},{10,... | collective-permute-start | bytes 196616 | tf_op jit(solution)/shard_map/ppermute | solution.py:21
  269.9 7.1 %collective-permute-start.6 = (f32[2,32,256]{2,1,0:T(8,128)S(1)}, f32[2,32,256]{2,1,0:T(8,128)S(1)}, u32[]{:S(2)}, u32[]{:S(2)}) collective-permute-start(f32[2,32,256]{2,1,0:T(8,128)S(1)} %slice_subtract_fusion), channel_id=1, source_target_pairs={{0,2},{1,3},{2,4},{3,5},{4,6},{5,7},{6,0},{7,1},{8,10},{9,11},{10,... | collective-permute-start | bytes 196616 | tf_op jit(solution)/shard_map/ppermute | solution.py:21
  275.4 4.8 %collective-permute-start.13 = (f32[2,32,512]{2,1,0:T(8,128)S(1)}, f32[2,32,512]{2,1,0:T(8,128)S(1)}, u32[]{:S(2)}, u32[]{:S(2)}) collective-permute-start(f32[2,32,512]{2,1,0:T(8,128)S(1)} %collective-permute-done.10), channel_id=1, source_target_pairs={{0,6},{1,7},{2,0},{3,1},{4,2},{5,3},{6,4},{7,5},{8,14},{9,15},{10,... | collective-permute-start | bytes 393224 | tf_op jit(solution)/shard_map/ppermute | solution.py:21
  275.9 5.4 %collective-permute-start.12 = (f32[2,32,512]{2,1,0:T(8,128)S(1)}, f32[2,32,512]{2,1,0:T(8,128)S(1)}, u32[]{:S(2)}, u32[]{:S(2)}) collective-permute-start(f32[2,32,512]{2,1,0:T(8,128)S(1)} %collective-permute-done.10), channel_id=1, source_target_pairs={{0,4},{1,5},{2,6},{3,7},{4,0},{5,1},{6,2},{7,3},{8,12},{9,13},{10,... | collective-permute-start | bytes 393224 | tf_op jit(solution)/shard_map/ppermute | solution.py:21
  276.3 8.3 %collective-permute-start.11 = (f32[2,32,512]{2,1,0:T(8,128)S(1)}, f32[2,32,512]{2,1,0:T(8,128)S(1)}, u32[]{:S(2)}, u32[]{:S(2)}) collective-permute-start(f32[2,32,512]{2,1,0:T(8,128)S(1)} %collective-permute-done.10), channel_id=1, source_target_pairs={{0,2},{1,3},{2,4},{3,5},{4,6},{5,7},{6,0},{7,1},{8,10},{9,11},{10,... | collective-permute-start | bytes 393224 | tf_op jit(solution)/shard_map/ppermute | solution.py:21
  277.0 10.9 %copy-start.10 = (f32[2,256,256]{2,1,0:T(8,128)S(1)}, f32[2,256,256]{2,1,0:T(8,128)}, u32[]{:S(2)}) copy-start(f32[2,256,256]{2,1,0:T(8,128)} %copy-done.9) | copy-start | bytes 1572868
  277.6 11.2 %collective-permute-start.9 = (f32[2,128,256]{2,1,0:T(8,128)S(1)}, f32[2,128,256]{2,1,0:T(8,128)}, u32[]{:S(2)}, u32[]{:S(2)}) collective-permute-start(f32[2,128,256]{2,1,0:T(8,128)S(1)} %bitcast.66), channel_id=1, source_target_pairs={{0,1},{1,0},{2,3},{3,2},{4,5},{5,4},{6,7},{7,6},{8,9},{9,8},{10,11... | collective-permute-start | bytes 786440 | tf_op jit(solution)/shard_map/ppermute | solution.py:57
  285.3 5.5 %collective-permute-start.14 = (f32[2,128,512]{2,1,0:T(8,128)S(1)}, f32[2,128,512]{2,1,0:T(8,128)S(1)}, u32[]{:S(2)}, u32[]{:S(2)}) collective-permute-start(f32[2,128,512]{2,1,0:T(8,128)S(1)} %bitcast.60), channel_id=1, source_target_pairs={{0,1},{1,0},{2,3},{3,2},{4,5},{5,4},{6,7},{7,6},{8,9},{9,8},{10,11... | collective-permute-start | bytes 1572872 | tf_op jit(solution)/shard_map/ppermute | solution.py:57
  290.9 1.5 copy-start.5
Sparse Core Ops, SparseCore 0:
  41.9 55.2 all-gather.1

commit v8 on v7

--- a/solution.py
+++ b/solution.py
@@ -58,6 +58,19 @@
     return jnp.where(
         core == 0, jnp.concatenate([part, got], axis=1), jnp.concatenate([got, part], axis=1)
     )
+
+
+def row_gather(x):
+    length = lax.axis_size("row")
+    row_here = lax.axis_index("row")
+    core = row_here % 2
+    chip = row_here // 2
+    chips = length // 2
+    got = lax.ppermute(x, "row", [(i, i ^ 1) for i in range(length)])
+    pair = jnp.where(core == 0, jnp.stack([x, got]), jnp.stack([got, x]))
+    stacked = jnp.stack([pair] + [_towards(pair, by) for by in range(1, chips)])
+    order = (chip - jnp.arange(chips, dtype=jnp.int32)) % chips
+    return stacked[order].reshape((length,) + x.shape)
 
 
 def held_rows(x):
@@ -204,11 +217,12 @@
     factor1 = keep1[:, :, None] * product("kij,kjc->kic", panel1, diag_inv1)
     factor2 = keep1[:, :, None] * payload[:, :B]
     both = jnp.concatenate([factor1, factor2], axis=-1)
-    boths = lax.all_gather(both, "row", axis=1, tiled=True).reshape(slots, -1, B, 2 * B)
-    up_parent = lax.all_gather(payload[:, B:], "row", axis=1, tiled=True)
+    boths = row_gather(both)
+    up_parent = row_gather(payload[:, B:])
+    up_parent = up_parent.transpose(1, 0, 2, 3).reshape(slots, B, B)
 
     blocks1 = select_take(received, row_blocks, slots, cols_here)
-    kept = keep1[:, :, None] * product("kmij,kmjc->kic", blocks1, boths)
+    kept = keep1[:, :, None] * product("kmij,mkjc->kic", blocks1, boths)
     sel1_panel = -kept[:, :, :B]
     pre2 = -(product("kij,kjc->kic", sel1_panel, up_parent) + kept[:, :, B:])
     pre2_child = shifted(pre2, "own", 1)

time: 301 us -> 286 us (0.950)
  waiting for transfers between devices: 188 us -> 172 us
  blocking collectives: 15.3 us -> 0 us
  between operations: 14.5 us -> 1.18 us
  other arithmetic: 8.9 us -> 21.4 us
  starting transfers between devices: 33.3 us -> 44 us
  local copies, waits for them, and re-layouts: 4.84 us -> 12.5 us
    all_to_all x1, waiting for transfers between devices: 163 us -> 50.5 us  [on_device(): lax.all_to_all(outgoing, 'own', split_axis=0, concat_axis=0, tiled=True)]
    ppermute x9 -> x15, waiting for transfers between devices: 14.9 us -> 106 us  [_towards(): lax.ppermute(value, 'row', [(i, (i + 2 * by) % length) for i in range(len...]
    all_gather x1 -> x0, blocking collectives: 15.3 us -> none  [on_device(): up_parent = lax.all_gather(payload[:, B:], 'row', axis=1, tiled=True)]
    gather x0 -> x2, local copies, waits for them, and re-layouts: none -> 8.28 us  [row_gather(): return stacked[order].reshape((length,) + x.shape)]
    another operation x0 -> x3, other arithmetic: none -> 7.58 us  [the longest x2 5.83 us: row_gather(): stacked = jnp.stack([pair] + [_towards(pair, by) for by in range(1, chips)])]
    ppermute x9 -> x15, starting transfers between devices: 7.48 us -> 14.5 us  [_towards(): lax.ppermute(value, 'row', [(i, (i + 2 * by) % length) for i in range(len...]
    select_n x1 -> x5, other arithmetic: 0.01 us -> 6.11 us  [the longest x4 6.1 us: row_gather(): pair = jnp.where(core == 0, jnp.stack([x, got]), jnp.stack([got, x]))]
    ppermute x0 -> x2, starting transfers between devices: none -> 3.13 us  [row_gather(): got = lax.ppermute(x, 'row', [(i, i ^ 1) for i in range(length)])]
  transfers between devices with their start and end apart: 17 -> 24, of which waited for: 8 -> 13; matrix products, arithmetic and copies ran while one was open for 5% -> 12% of each run, Pallas kernels for 4% -> 2%
where the time goes in v8:
time: 286 us; the launch traced here: 285 us
  waiting for transfers between devices  172 us (60%)
  starting transfers between devices  44 us (15%)
  matrix products  22.7 us (8%)
  other arithmetic  21.4 us (7%)
  local copies, waits for them, and re-layouts  12.5 us (4%)
  Pallas kernels  11.3 us (4%)
    ppermute x15, waiting for transfers between devices, _towards(): lax.ppermute(value, 'row', [(i, (i + 2 * by) % length) for i in range(len...  106 us
    all_to_all x1, waiting for transfers between devices, on_device(): lax.all_to_all(outgoing, 'own', split_axis=0, concat_axis=0, tiled=True)  50.5 us
    dot_general x13, matrix products, product(): return jnp.einsum(form, left, right, precision=HIGH)  22.7 us
    ppermute x15, starting transfers between devices, _towards(): lax.ppermute(value, 'row', [(i, (i + 2 * by) % length) for i in range(len...  14.5 us
    ppermute x3, waiting for transfers between devices, shifted(): lax.ppermute(shard, axis, [(i, (i + by) % length) for i in range(length)])  9.88 us
    ppermute x3, starting transfers between devices, shifted(): lax.ppermute(shard, axis, [(i, (i + by) % length) for i in range(length)])  8.76 us
    gather x2, local copies, waits for them, and re-layouts, row_gather(): return stacked[order].reshape((length,) + x.shape)  8.28 us
    all_to_all x1, starting transfers between devices, on_device(): lax.all_to_all(outgoing, 'own', split_axis=0, concat_axis=0, tiled=True)  7.45 us
  transfers between devices with their start and end apart: 24, of which 13 were waited for; matrix products, arithmetic and copies ran while one was open for 12% of the time, Pallas kernels for 2%

profile of v8, /device:TPU:1, one launch (start us, length us, event | category | flops | bytes accessed | tf_op | source)
XLA Modules:
  0.0 285.0 jit_solution(5382505761425649606)
XLA Ops:
  0.7 0.7 convert_bitcast_fusion
  1.7 1.2 fusion.10
  2.9 1.7 convolution_multiply_fusion.1
  4.7 8.7 %collective-permute-start = (f32[2,288,256]{2,1,0:T(8,128)S(1)}, f32[2,288,256]{2,1,0:T(8,128)S(1)}, u32[]{:S(2)}, u32[]{:S(2)}) collective-permute-start(f32[2,288,256]{2,1,0:T(8,128)S(1)} %pad_maximum_fusion.3), channel_id=1, source_target_pairs={{0,248},{8,0},{16,8},{24,16},{32,24},{40,32},{48,40},{56,48},{64,5... | collective-permute-start | bytes 1769480 | tf_op jit(solution)/shard_map/ppermute | solution.py:16
  13.9 0.7 gather_fusion.1
  14.6 0.7 clamp_reduce_fusion
  15.3 6.4 %shard_map.128 = f32[32,256,256]{2,1,0:T(8,128)} custom-call(s32[32]{0:T(128)} %get-tuple-element.14.rows_ref, s32[32]{0:T(128)} %get-tuple-element.13.cols_ref, f32[2048,512]{1,0:T(8,128)} %src_ref.1), custom_call_target="tpu_custom_call" | custom-call | bytes 12582912 | tf_op jit(solution)/shard_map/pallas_call | solution.py:121
  21.7 3.7 %collective-permute-done = f32[2,288,256]{2,1,0:T(8,128)S(1)} collective-permute-done((f32[2,288,256]{2,1,0:T(8,128)S(1)}, f32[2,288,256]{2,1,0:T(8,128)S(1)}, u32[]{:S(2)}, u32[]{:S(2)}) %collective-permute-start) | collective-permute-done | bytes 589856 | tf_op jit(solution)/shard_map/ppermute | solution.py:16
  25.4 7.4 %all-to-all-start = ((f32[32,256,256]{2,1,0:T(8,128)}), f32[32,256,256]{2,1,0:T(8,128)}, u32[]{:S(2)}, u32[]{:S(2)}) async-start(f32[32,256,256]{2,1,0:T(8,128)} %shard_map.128), calls=%async_computation | async-start | bytes 16777216 | tf_op jit(solution)/shard_map/all_to_all | solution.py:214
  32.9 0.7 convolution_multiply_fusion
  33.6 1.8 fusion.23
  35.4 1.8 collective-permute-start.1
  37.2 2.6 collective-permute-done.1
  39.9 3.2 %maximum_select_fusion.1 = f32[2,2,256,512]{3,2,1,0:T(8,128)} fusion(f32[1,2,256,512]{3,2,1,0:T(8,128)} %bitcast.10, f32[1,2,256,512]{3,2,1,0:T(8,128)S(1)} %get-tuple-element.16, pred[]{:T(512)S(6)} %eq.23), kind=kLoop, calls=%fused_computation.10 | loop fusion | flops 1572864 | bytes 4194305 | tf_op jit(solution)/shard_map/jit(_where)/select_n | solution.py:70
  43.1 2.7 collective-permute-start.4
  45.8 0.3 collective-permute-start.3
  46.2 0.7 collective-permute-start.2
  46.9 0.9 slice_bitcast_fusion.1
  47.7 1.3 collective-permute-start.5
  49.0 0.6 gather_fusion
  49.9 2.1 collective-permute-start.8
  52.0 0.5 fusion.21.which_ref
  52.5 1.5 collective-permute-start.7
  54.0 87.1 %collective-permute-done.8 = f32[2,2,32,256]{3,2,1,0:T(8,128)S(1)} collective-permute-done((f32[2,2,32,256]{3,2,1,0:T(8,128)S(1)}, f32[2,2,32,256]{3,2,1,0:T(8,128)S(1)}, u32[]{:S(2)}, u32[]{:S(2)}) %collective-permute-start.8) | collective-permute-done | bytes 131104 | tf_op jit(solution)/shard_map/ppermute | solution.py:21
  141.1 0.8 collective-permute-done.7
  142.0 5.6 %collective-permute-done.6 = f32[2,2,32,256]{3,2,1,0:T(8,128)S(1)} collective-permute-done((f32[2,2,32,256]{3,2,1,0:T(8,128)S(1)}, f32[2,2,32,256]{3,2,1,0:T(8,128)S(1)}, u32[]{:S(2)}, u32[]{:S(2)}) %collective-permute-start.6) | collective-permute-done | bytes 131104 | tf_op jit(solution)/shard_map/ppermute | solution.py:21
  147.6 0.6 gather_fusion.3
  148.3 2.8 maximum_select_fusion
  151.2 5.8 %pad_maximum_fusion = f32[4,2,2,256,512]{4,3,2,1,0:T(8,128)} fusion(f32[1,2,2,256,512]{4,3,2,1,0:T(8,128)} %bitcast.13, f32[1,2,2,256,512]{4,3,2,1,0:T(8,128)} %bitcast.12, f32[1,2,2,256,512]{4,3,2,1,0:T(8,128)} %bitcast.11, f32[1,2,2,256,512]{4,3,2,1,0:T(8,128)S(1)} %maximum_select_fusion), kind=kLoop, calls=%fused_computation.6 | loop fusion | flops 6291456 | bytes 16777216 | tf_op jit(solution)/shard_map/stack | solution.py:71
  157.0 7.7 %gather_fusion.2 = f32[4,2,2,256,512]{4,3,2,1,0:T(8,128)} fusion(f32[4,2,2,256,512]{4,3,2,1,0:T(8,128)} %pad_maximum_fusion, s32[1024]{0:T(1024)S(1)} %pad_clamp_fusion), kind=kCustom, calls=%fused_computation.2 | custom fusion | bytes 16777232 | tf_op jit(solution)/shard_map/gather | solution.py:73
  164.7 50.5 %all-to-all-done.src_ref = f32[32,256,256]{2,1,0:T(8,128)} async-done(((f32[32,256,256]{2,1,0:T(8,128)}), f32[32,256,256]{2,1,0:T(8,128)}, u32[]{:S(2)}, u32[]{:S(2)}) %all-to-all-start) | async-done | bytes 8388640 | tf_op jit(solution)/shard_map/all_to_all | solution.py:214
  215.1 4.9 %shard_map.129 = f32[16,256,256]{2,1,0:T(8,128)} custom-call(s32[16]{0:T(128)} %fusion.21.which_ref, f32[32,256,256]{2,1,0:T(8,128)} %all-to-all-done.src_ref), custom_call_target="tpu_custom_call" | custom-call | bytes 8388608 | tf_op jit(solution)/shard_map/pallas_call | solution.py:187
  220.1 10.2 %fusion.5 = f32[2,256,512]{2,1,0:T(8,128)S(1)} fusion(f32[2,8,256,256]{3,2,1,0:T(8,128)} %bitcast.80, f32[8,2,256,512]{3,2,1,0:T(8,128)} %bitcast.79, f32[2]{0:T(128)S(1)} %convert_bitcast_fusion.1), kind=kOutput, calls=%fused_computation.13 | convolution fusion | flops 6442713088 | bytes 13631496 | tf_op jit(solution)/shard_map/kmij,mkjc->kic/dot_general | solution.py:87
  230.4 1.0 fusion.26
  231.5 1.0 fusion.25
  232.5 0.7 fusion.9
  233.2 1.0 fusion.27
  234.4 1.0 slice_select_fusion
  235.4 5.3 %collective-permute-start.10 = (f32[2,128,768]{2,1,0:T(8,128)}, f32[2,128,768]{2,1,0:T(8,128)}, u32[]{:S(2)}, u32[]{:S(2)}) collective-permute-start(f32[2,128,768]{2,1,0:T(8,128)} %slice_select_fusion), channel_id=1, source_target_pairs={{0,1},{1,0},{2,3},{3,2},{4,5},{5,4},{6,7},{7,6},{8,9},{9,8},{10,11... | collective-permute-start | bytes 2359304 | tf_op jit(solution)/shard_map/ppermute | solution.py:34
  240.6 2.3 collective-permute-done.10
  242.9 1.3 select_add_fusion
  244.2 2.8 collective-permute-start.13
  247.0 0.4 collective-permute-start.12
  247.5 0.6 collective-permute-start.11
  248.1 1.1 fusion.24
  249.1 5.9 %collective-permute-done.13 = f32[2,32,768]{2,1,0:T(8,128)S(1)} collective-permute-done((f32[2,32,768]{2,1,0:T(8,128)S(1)}, f32[2,32,768]{2,1,0:T(8,128)S(1)}, u32[]{:S(2)}, u32[]{:S(2)}) %collective-permute-start.13) | collective-permute-done | bytes 196640 | tf_op jit(solution)/shard_map/ppermute | solution.py:21
  255.0 4.6 %collective-permute-done.11 = f32[2,32,768]{2,1,0:T(8,128)S(1)} collective-permute-done((f32[2,32,768]{2,1,0:T(8,128)S(1)}, f32[2,32,768]{2,1,0:T(8,128)S(1)}, u32[]{:S(2)}, u32[]{:S(2)}) %collective-permute-start.11) | collective-permute-done | bytes 196640 | tf_op jit(solution)/shard_map/ppermute | solution.py:21
  259.7 0.4 add_negate_fusion
  260.2 0.8 collective-permute-start.16
  261.0 0.6 collective-permute-start.15
  261.6 0.4 collective-permute-start.14
  262.0 6.2 %collective-permute-done.18 = f32[2,32,512]{2,1,0:T(8,128)S(1)} collective-permute-done((f32[2,32,512]{2,1,0:T(8,128)S(1)}, f32[2,32,512]{2,1,0:T(8,128)S(1)}, u32[]{:S(2)}, u32[]{:S(2)}) %collective-permute-start.18) | collective-permute-done | bytes 131104 | tf_op jit(solution)/shard_map/ppermute | solution.py:16
  268.5 0.7 collective-permute-start.20
  269.2 0.4 collective-permute-start.19
  269.7 1.1 fusion.28
  270.8 0.6 gather_fusion.4
  271.4 2.4 collective-permute-start.17
  273.9 2.4 collective-permute-done.19
  276.3 0.6 gather_fusion.5
  277.0 2.5 collective-permute-start.22
  279.5 1.0 fusion.29
  280.6 0.9 broadcast_multiply_fusion
  281.5 1.9 maximum_select_fusion.3
  283.5 1.5 fusion.8
  (73 shorter events, 2.6 us)
Async XLA Ops:
  0.6 1.1 copy-start
  0.6 12.7 %copy-start.11 = (s32[64,8]{0,1:T(8,128)S(1)}, s32[64,8]{0,1:T(8,128)}, u32[]{:S(2)}) copy-start(s32[64,8]{0,1:T(8,128)} %param.10) | copy-start | bytes 6148
  4.7 20.7 %collective-permute-start = (f32[2,288,256]{2,1,0:T(8,128)S(1)}, f32[2,288,256]{2,1,0:T(8,128)S(1)}, u32[]{:S(2)}, u32[]{:S(2)}) collective-permute-start(f32[2,288,256]{2,1,0:T(8,128)S(1)} %pad_maximum_fusion.3), channel_id=1, source_target_pairs={{0,248},{8,0},{16,8},{24,16},{32,24},{40,32},{48,40},{56,48},{64,5... | collective-permute-start | bytes 1769480 | tf_op jit(solution)/shard_map/ppermute | solution.py:16
  21.7 11.2 %copy-start.12 = (s32[2,1]{0,1:T(1,128)S(1)}, s32[2,1]{0,1:T(1,128)}, u32[]{:S(2)}) copy-start(s32[2,1]{0,1:T(1,128)} %param.13) | copy-start | bytes 28
  21.7 11.2 %copy-start.2 = (f32[2,256,256]{2,1,0:T(8,128)S(1)}, f32[2,256,256]{2,1,0:T(8,128)}, u32[]{:S(2)}) copy-start(f32[2,256,256]{2,1,0:T(8,128)} %param.12) | copy-start | bytes 1572868
  25.4 8.2 %copy-start.7 = (f32[2,288,256]{2,1,0:T(8,128)}, f32[2,288,256]{2,1,0:T(8,128)S(1)}, u32[]{:S(2)}) copy-start(f32[2,288,256]{2,1,0:T(8,128)S(1)} %collective-permute-done) | copy-start | bytes 1769476
  25.4 7.5 %copy-start.8 = (f32[2,256,256]{2,1,0:T(8,128)S(1)}, f32[2,256,256]{2,1,0:T(8,128)}, u32[]{:S(2)}) copy-start(f32[2,256,256]{2,1,0:T(8,128)} %param.11) | copy-start | bytes 1572868
  25.4 189.8 %all-to-all-start = ((f32[32,256,256]{2,1,0:T(8,128)}), f32[32,256,256]{2,1,0:T(8,128)}, u32[]{:S(2)}, u32[]{:S(2)}) async-start(f32[32,256,256]{2,1,0:T(8,128)} %shard_map.128), calls=%async_computation | async-start | bytes 16777216 | tf_op jit(solution)/shard_map/all_to_all | solution.py:214
  35.4 4.5 %collective-permute-start.1 = (f32[2,256,512]{2,1,0:T(8,128)}, f32[2,256,512]{2,1,0:T(8,128)}, u32[]{:S(2)}, u32[]{:S(2)}) collective-permute-start(f32[2,256,512]{2,1,0:T(8,128)} %get-tuple-element.17), channel_id=1, source_target_pairs={{0,1},{1,0},{2,3},{3,2},{4,5},{5,4},{6,7},{7,6},{8,9},{9,8},{10,11... | collective-permute-start | bytes 3145736 | tf_op jit(solution)/shard_map/ppermute | solution.py:69
  43.1 108.0 %collective-permute-start.4 = (f32[2,2,256,512]{3,2,1,0:T(8,128)}, f32[2,2,256,512]{3,2,1,0:T(8,128)}, u32[]{:S(2)}, u32[]{:S(2)}) collective-permute-start(f32[2,2,256,512]{3,2,1,0:T(8,128)} %maximum_select_fusion.1), channel_id=1, source_target_pairs={{0,6},{1,7},{2,0},{3,1},{4,2},{5,3},{6,4},{7,5},{8,14},{9,15},{10,... | collective-permute-start | bytes 6291464 | tf_op jit(solution)/shard_map/ppermute | solution.py:21
  45.8 105.3 %collective-permute-start.3 = (f32[2,2,256,512]{3,2,1,0:T(8,128)}, f32[2,2,256,512]{3,2,1,0:T(8,128)}, u32[]{:S(2)}, u32[]{:S(2)}) collective-permute-start(f32[2,2,256,512]{3,2,1,0:T(8,128)} %maximum_select_fusion.1), channel_id=1, source_target_pairs={{0,4},{1,5},{2,6},{3,7},{4,0},{5,1},{6,2},{7,3},{8,12},{9,13},{10,... | collective-permute-start | bytes 6291464 | tf_op jit(solution)/shard_map/ppermute | solution.py:21
  46.2 105.0 %collective-permute-start.2 = (f32[2,2,256,512]{3,2,1,0:T(8,128)}, f32[2,2,256,512]{3,2,1,0:T(8,128)}, u32[]{:S(2)}, u32[]{:S(2)}) collective-permute-start(f32[2,2,256,512]{3,2,1,0:T(8,128)} %maximum_select_fusion.1), channel_id=1, source_target_pairs={{0,2},{1,3},{2,4},{3,5},{4,6},{5,7},{6,0},{7,1},{8,10},{9,11},{10,... | collective-permute-start | bytes 6291464 | tf_op jit(solution)/shard_map/ppermute | solution.py:21
  47.7 2.2 collective-permute-start.5
  49.9 91.1 %collective-permute-start.8 = (f32[2,2,32,256]{3,2,1,0:T(8,128)S(1)}, f32[2,2,32,256]{3,2,1,0:T(8,128)S(1)}, u32[]{:S(2)}, u32[]{:S(2)}) collective-permute-start(f32[2,2,32,256]{3,2,1,0:T(8,128)S(1)} %maximum_select_fusion.5), channel_id=1, source_target_pairs={{0,6},{1,7},{2,0},{3,1},{4,2},{5,3},{6,4},{7,5},{8,14},{9,15},{10,... | collective-permute-start | bytes 393224 | tf_op jit(solution)/shard_map/ppermute | solution.py:21
  52.5 89.4 %collective-permute-start.7 = (f32[2,2,32,256]{3,2,1,0:T(8,128)S(1)}, f32[2,2,32,256]{3,2,1,0:T(8,128)S(1)}, u32[]{:S(2)}, u32[]{:S(2)}) collective-permute-start(f32[2,2,32,256]{3,2,1,0:T(8,128)S(1)} %maximum_select_fusion.5), channel_id=1, source_target_pairs={{0,4},{1,5},{2,6},{3,7},{4,0},{5,1},{6,2},{7,3},{8,12},{9,13},{10,... | collective-permute-start | bytes 393224 | tf_op jit(solution)/shard_map/ppermute | solution.py:21
  141.1 6.5 %collective-permute-start.6 = (f32[2,2,32,256]{3,2,1,0:T(8,128)S(1)}, f32[2,2,32,256]{3,2,1,0:T(8,128)S(1)}, u32[]{:S(2)}, u32[]{:S(2)}) collective-permute-start(f32[2,2,32,256]{3,2,1,0:T(8,128)S(1)} %maximum_select_fusion.5), channel_id=1, source_target_pairs={{0,2},{1,3},{2,4},{3,5},{4,6},{5,7},{6,0},{7,1},{8,10},{9,11},{10,... | collective-permute-start | bytes 393224 | tf_op jit(solution)/shard_map/ppermute | solution.py:21
  148.3 84.2 %copy-start.3 = (f32[2,8,32,256]{3,2,1,0:T(8,128)}, f32[2,8,32,256]{3,2,1,0:T(8,128)S(1)}, u32[]{:S(2)}) copy-start(f32[2,8,32,256]{3,2,1,0:T(8,128)S(1)} %copy.82) | copy-start | bytes 1572868
  230.4 2.8 copy-start.1
  235.4 7.5 %collective-permute-start.10 = (f32[2,128,768]{2,1,0:T(8,128)}, f32[2,128,768]{2,1,0:T(8,128)}, u32[]{:S(2)}, u32[]{:S(2)}) collective-permute-start(f32[2,128,768]{2,1,0:T(8,128)} %slice_select_fusion), channel_id=1, source_target_pairs={{0,1},{1,0},{2,3},{3,2},{4,5},{5,4},{6,7},{7,6},{8,9},{9,8},{10,11... | collective-permute-start | bytes 2359304 | tf_op jit(solution)/shard_map/ppermute | solution.py:34
  240.6 19.0 %collective-permute-start.9 = (f32[2,256,256]{2,1,0:T(8,128)S(1)}, f32[2,256,256]{2,1,0:T(8,128)S(1)}, u32[]{:S(2)}, u32[]{:S(2)}) collective-permute-start(f32[2,256,256]{2,1,0:T(8,128)S(1)} %fusion.9), channel_id=1, source_target_pairs={{0,8},{8,16},{16,24},{24,32},{32,40},{40,48},{48,56},{56,64},{64,7... | collective-permute-start | bytes 1572872 | tf_op jit(solution)/shard_map/ppermute | solution.py:16
  244.1 15.5 %copy-start.4 = (f32[2,8,32,256]{3,2,1,0:T(8,128)S(1)}, f32[2,8,32,256]{3,2,1,0:T(8,128)}, u32[]{:S(2)}) copy-start(f32[2,8,32,256]{3,2,1,0:T(8,128)} %copy-done.3) | copy-start | bytes 1572868
  244.2 10.8 %collective-permute-start.13 = (f32[2,32,768]{2,1,0:T(8,128)S(1)}, f32[2,32,768]{2,1,0:T(8,128)S(1)}, u32[]{:S(2)}, u32[]{:S(2)}) collective-permute-start(f32[2,32,768]{2,1,0:T(8,128)S(1)} %get-tuple-element.19), channel_id=1, source_target_pairs={{0,6},{1,7},{2,0},{3,1},{4,2},{5,3},{6,4},{7,5},{8,14},{9,15},{10,... | collective-permute-start | bytes 589832 | tf_op jit(solution)/shard_map/ppermute | solution.py:21
  247.0 8.0 %collective-permute-start.12 = (f32[2,32,768]{2,1,0:T(8,128)S(1)}, f32[2,32,768]{2,1,0:T(8,128)S(1)}, u32[]{:S(2)}, u32[]{:S(2)}) collective-permute-start(f32[2,32,768]{2,1,0:T(8,128)S(1)} %get-tuple-element.20), channel_id=1, source_target_pairs={{0,4},{1,5},{2,6},{3,7},{4,0},{5,1},{6,2},{7,3},{8,12},{9,13},{10,... | collective-permute-start | bytes 589832 | tf_op jit(solution)/shard_map/ppermute | solution.py:21
  247.5 12.1 %collective-permute-start.11 = (f32[2,32,768]{2,1,0:T(8,128)S(1)}, f32[2,32,768]{2,1,0:T(8,128)S(1)}, u32[]{:S(2)}, u32[]{:S(2)}) collective-permute-start(f32[2,32,768]{2,1,0:T(8,128)S(1)} %get-tuple-element.18), channel_id=1, source_target_pairs={{0,2},{1,3},{2,4},{3,5},{4,6},{5,7},{6,0},{7,1},{8,10},{9,11},{10,... | collective-permute-start | bytes 589832 | tf_op jit(solution)/shard_map/ppermute | solution.py:21
  259.6 11.1 %copy-start.9 = (f32[2,256,256]{2,1,0:T(8,128)}, f32[2,256,256]{2,1,0:T(8,128)S(1)}, u32[]{:S(2)}) copy-start(f32[2,256,256]{2,1,0:T(8,128)S(1)} %collective-permute-done.9) | copy-start | bytes 1572868
  260.1 8.1 %collective-permute-start.18 = (f32[2,32,512]{2,1,0:T(8,128)S(1)}, f32[2,32,512]{2,1,0:T(8,128)S(1)}, u32[]{:S(2)}, u32[]{:S(2)}) collective-permute-start(f32[2,32,512]{2,1,0:T(8,128)S(1)} %pad_maximum_fusion.7), channel_id=1, source_target_pairs={{0,8},{8,16},{16,24},{24,32},{32,40},{40,48},{48,56},{56,64},{64,7... | collective-permute-start | bytes 393224 | tf_op jit(solution)/shard_map/ppermute | solution.py:16
  260.2 9.0 %collective-permute-start.16 = (f32[2,32,256]{2,1,0:T(8,128)S(1)}, f32[2,32,256]{2,1,0:T(8,128)S(1)}, u32[]{:S(2)}, u32[]{:S(2)}) collective-permute-start(f32[2,32,256]{2,1,0:T(8,128)S(1)} %slice_subtract_fusion), channel_id=1, source_target_pairs={{0,6},{1,7},{2,0},{3,1},{4,2},{5,3},{6,4},{7,5},{8,14},{9,15},{10,... | collective-permute-start | bytes 196616 | tf_op jit(solution)/shard_map/ppermute | solution.py:21
  261.0 9.8 %collective-permute-start.15 = (f32[2,32,256]{2,1,0:T(8,128)S(1)}, f32[2,32,256]{2,1,0:T(8,128)S(1)}, u32[]{:S(2)}, u32[]{:S(2)}) collective-permute-start(f32[2,32,256]{2,1,0:T(8,128)S(1)} %slice_subtract_fusion), channel_id=1, source_target_pairs={{0,4},{1,5},{2,6},{3,7},{4,0},{5,1},{6,2},{7,3},{8,12},{9,13},{10,... | collective-permute-start | bytes 196616 | tf_op jit(solution)/shard_map/ppermute | solution.py:21
  261.6 9.1 %collective-permute-start.14 = (f32[2,32,256]{2,1,0:T(8,128)S(1)}, f32[2,32,256]{2,1,0:T(8,128)S(1)}, u32[]{:S(2)}, u32[]{:S(2)}) collective-permute-start(f32[2,32,256]{2,1,0:T(8,128)S(1)} %slice_subtract_fusion), channel_id=1, source_target_pairs={{0,2},{1,3},{2,4},{3,5},{4,6},{5,7},{6,0},{7,1},{8,10},{9,11},{10,... | collective-permute-start | bytes 196616 | tf_op jit(solution)/shard_map/ppermute | solution.py:21
  268.2 5.6 %collective-permute-start.21 = (f32[2,32,512]{2,1,0:T(8,128)S(1)}, f32[2,32,512]{2,1,0:T(8,128)S(1)}, u32[]{:S(2)}, u32[]{:S(2)}) collective-permute-start(f32[2,32,512]{2,1,0:T(8,128)S(1)} %collective-permute-done.18), channel_id=1, source_target_pairs={{0,6},{1,7},{2,0},{3,1},{4,2},{5,3},{6,4},{7,5},{8,14},{9,15},{10,... | collective-permute-start | bytes 393224 | tf_op jit(solution)/shard_map/ppermute | solution.py:21
  268.5 5.4 %collective-permute-start.20 = (f32[2,32,512]{2,1,0:T(8,128)S(1)}, f32[2,32,512]{2,1,0:T(8,128)S(1)}, u32[]{:S(2)}, u32[]{:S(2)}) collective-permute-start(f32[2,32,512]{2,1,0:T(8,128)S(1)} %collective-permute-done.18), channel_id=1, source_target_pairs={{0,4},{1,5},{2,6},{3,7},{4,0},{5,1},{6,2},{7,3},{8,12},{9,13},{10,... | collective-permute-start | bytes 393224 | tf_op jit(solution)/shard_map/ppermute | solution.py:21
  269.2 7.0 %collective-permute-start.19 = (f32[2,32,512]{2,1,0:T(8,128)S(1)}, f32[2,32,512]{2,1,0:T(8,128)S(1)}, u32[]{:S(2)}, u32[]{:S(2)}) collective-permute-start(f32[2,32,512]{2,1,0:T(8,128)S(1)} %collective-permute-done.18), channel_id=1, source_target_pairs={{0,2},{1,3},{2,4},{3,5},{4,6},{5,7},{6,0},{7,1},{8,10},{9,11},{10,... | collective-permute-start | bytes 393224 | tf_op jit(solution)/shard_map/ppermute | solution.py:21
  270.8 8.7 %copy-start.6 = (f32[2,256,256]{2,1,0:T(8,128)S(1)}, f32[2,256,256]{2,1,0:T(8,128)}, u32[]{:S(2)}) copy-start(f32[2,256,256]{2,1,0:T(8,128)} %param.14) | copy-start | bytes 1572868
  271.4 10.1 %collective-permute-start.17 = (f32[2,128,256]{2,1,0:T(8,128)S(1)}, f32[2,128,256]{2,1,0:T(8,128)}, u32[]{:S(2)}, u32[]{:S(2)}) collective-permute-start(f32[2,128,256]{2,1,0:T(8,128)S(1)} %bitcast.90), channel_id=1, source_target_pairs={{0,1},{1,0},{2,3},{3,2},{4,5},{5,4},{6,7},{7,6},{8,9},{9,8},{10,11... | collective-permute-start | bytes 786440 | tf_op jit(solution)/shard_map/ppermute | solution.py:57
  276.3 4.2 %copy-start.10 = (f32[2,256,256]{2,1,0:T(8,128)S(1)}, f32[2,256,256]{2,1,0:T(8,128)}, u32[]{:S(2)}) copy-start(f32[2,256,256]{2,1,0:T(8,128)} %copy-done.9) | copy-start | bytes 1572868
  277.0 6.4 %collective-permute-start.22 = (f32[2,128,512]{2,1,0:T(8,128)S(1)}, f32[2,128,512]{2,1,0:T(8,128)S(1)}, u32[]{:S(2)}, u32[]{:S(2)}) collective-permute-start(f32[2,128,512]{2,1,0:T(8,128)S(1)} %bitcast.83), channel_id=1, source_target_pairs={{0,1},{1,0},{2,3},{3,2},{4,5},{5,4},{6,7},{7,6},{8,9},{9,8},{10,11... | collective-permute-start | bytes 1572872 | tf_op jit(solution)/shard_map/ppermute | solution.py:57
  283.5 1.5 copy-start.5

commit v9 on v8

--- a/solution.py
+++ b/solution.py
@@ -195,6 +195,49 @@
     return taken.reshape(slots, -1, B, B)
 
 
+def _panel_product(which_ref, blocks_ref, factors_ref, out_ref, total):
+    m = pl.program_id(1)
+
+    @pl.when(m == 0)
+    def _():
+        total[...] = jnp.zeros_like(total)
+
+    total[...] += jnp.dot(
+        blocks_ref[0], factors_ref[0, 0], precision=HIGH, preferred_element_type=jnp.float32
+    )
+
+    @pl.when(m == pl.num_programs(1) - 1)
+    def _():
+        out_ref[0] = total[...]
+
+
+def panel_product(received, boths, row_blocks, slots, cols_here):
+    mine = lax.axis_index("own") * slots + jnp.arange(slots, dtype=jnp.int32)
+    sender = jnp.clip(row_blocks[mine] // cols_here, 0, received.shape[0] - 1)
+    groups = sender.shape[1]
+    width = boths.shape[-1]
+    grid_spec = pltpu.PrefetchScalarGridSpec(
+        num_scalar_prefetch=1,
+        grid=(slots, groups),
+        in_specs=[
+            pl.BlockSpec((1, B, B), lambda k, m, w: (w[k * groups + m], 0, 0)),
+            pl.BlockSpec((1, 1, B, width), lambda k, m, w: (m, k, 0, 0)),
+        ],
+        out_specs=pl.BlockSpec((1, B, width), lambda k, m, w: (k, 0, 0)),
+        scratch_shapes=[pltpu.VMEM((B, width), jnp.float32)],
+    )
+    return pl.pallas_call(
+        _panel_product,
+        out_shape=jax.ShapeDtypeStruct((slots, B, width), jnp.float32),
+        grid_spec=grid_spec,
+        cost_estimate=pl.CostEstimate(
+            flops=2 * slots * groups * B * B * width,
+            bytes_accessed=4 * slots * groups * (B * B + B * width),
+            transcendentals=0,
+        ),
+    )(sender.reshape(-1), received, boths)
+
+
 def on_device(
     sigma_anc, row_blocks, panel1, diag_inv1, mask1, parent_block2, panel2, diag_inv2, mask2
 ):
@@ -221,8 +264,7 @@
     up_parent = row_gather(payload[:, B:])
     up_parent = up_parent.transpose(1, 0, 2, 3).reshape(slots, B, B)
 
-    blocks1 = select_take(received, row_blocks, slots, cols_here)
-    kept = keep1[:, :, None] * product("kmij,mkjc->kic", blocks1, boths)
+    kept = keep1[:, :, None] * panel_product(received, boths, row_blocks, slots, cols_here)
     sel1_panel = -kept[:, :, :B]
     pre2 = -(product("kij,kjc->kic", sel1_panel, up_parent) + kept[:, :, B:])
     pre2_child = shifted(pre2, "own", 1)

time: 286 us -> 289 us (1.010)
  Pallas kernels: 11.3 us -> 23.3 us
  matrix products: 22.7 us -> 12.4 us
    pallas_call x1, Pallas kernels: 4.94 us -> 16.9 us  [panel_product(): pl.pallas_call(_panel_product, out_shape=jax.ShapeDtypeStruct((slots, B,...]
    dot_general x13 -> x12, matrix products: 22.7 us -> 12.4 us  [product(): return jnp.einsum(form, left, right, precision=HIGH)]
where the time goes in v9:
time: 289 us; the launch traced here: 288 us
  waiting for transfers between devices  172 us (60%)
  starting transfers between devices  44.2 us (15%)
  Pallas kernels  23.3 us (8%)
  other arithmetic  22.8 us (8%)
  local copies, waits for them, and re-layouts  12.5 us (4%)
  matrix products  12.4 us (4%)
    ppermute x15, waiting for transfers between devices, _towards(): lax.ppermute(value, 'row', [(i, (i + 2 * by) % length) for i in range(len...  106 us
    all_to_all x1, waiting for transfers between devices, on_device(): lax.all_to_all(outgoing, 'own', split_axis=0, concat_axis=0, tiled=True)  50.5 us
    pallas_call x1, Pallas kernels, panel_product(): pl.pallas_call(_panel_product, out_shape=jax.ShapeDtypeStruct((slots, B,...  16.9 us
    ppermute x15, starting transfers between devices, _towards(): lax.ppermute(value, 'row', [(i, (i + 2 * by) % length) for i in range(len...  14.7 us
    dot_general x12, matrix products, product(): return jnp.einsum(form, left, right, precision=HIGH)  12.4 us
    ppermute x3, waiting for transfers between devices, shifted(): lax.ppermute(shard, axis, [(i, (i + by) % length) for i in range(length)])  9.66 us
    ppermute x3, starting transfers between devices, shifted(): lax.ppermute(shard, axis, [(i, (i + by) % length) for i in range(length)])  8.76 us
    gather x2, local copies, waits for them, and re-layouts, row_gather(): return stacked[order].reshape((length,) + x.shape)  8.28 us
  transfers between devices with their start and end apart: 24, of which 13 were waited for; matrix products, arithmetic and copies ran while one was open for 12% of the time, Pallas kernels for 2%

profile of v9, /device:TPU:1, one launch (start us, length us, event | category | flops | bytes accessed | tf_op | source)
XLA Modules:
  0.0 288.1 jit_solution(14055329432179586540)
XLA Ops:
  0.7 0.7 convert_bitcast_fusion
  1.7 1.2 fusion.2
  2.9 1.7 convolution_multiply_fusion.1
  4.7 8.7 %collective-permute-start = (f32[2,288,256]{2,1,0:T(8,128)S(1)}, f32[2,288,256]{2,1,0:T(8,128)S(1)}, u32[]{:S(2)}, u32[]{:S(2)}) collective-permute-start(f32[2,288,256]{2,1,0:T(8,128)S(1)} %pad_maximum_fusion.3), channel_id=1, source_target_pairs={{0,248},{8,0},{16,8},{24,16},{32,24},{40,32},{48,40},{56,48},{64,5... | collective-permute-start | bytes 1769480 | tf_op jit(solution)/shard_map/ppermute | solution.py:16
  13.9 0.7 gather_fusion.1
  14.6 0.7 clamp_reduce_fusion
  15.3 6.4 %shard_map.128 = f32[32,256,256]{2,1,0:T(8,128)} custom-call(s32[32]{0:T(128)} %get-tuple-element.14.rows_ref, s32[32]{0:T(128)} %get-tuple-element.13.cols_ref, f32[2048,512]{1,0:T(8,128)} %src_ref.1), custom_call_target="tpu_custom_call" | custom-call | bytes 12582912 | tf_op jit(solution)/shard_map/pallas_call | solution.py:121
  21.7 3.7 %collective-permute-done = f32[2,288,256]{2,1,0:T(8,128)S(1)} collective-permute-done((f32[2,288,256]{2,1,0:T(8,128)S(1)}, f32[2,288,256]{2,1,0:T(8,128)S(1)}, u32[]{:S(2)}, u32[]{:S(2)}) %collective-permute-start) | collective-permute-done | bytes 589856 | tf_op jit(solution)/shard_map/ppermute | solution.py:16
  25.4 7.4 %all-to-all-start = ((f32[32,256,256]{2,1,0:T(8,128)}), f32[32,256,256]{2,1,0:T(8,128)}, u32[]{:S(2)}, u32[]{:S(2)}) async-start(f32[32,256,256]{2,1,0:T(8,128)} %shard_map.128), calls=%async_computation | async-start | bytes 16777216 | tf_op jit(solution)/shard_map/all_to_all | solution.py:257
  32.9 0.7 convolution_multiply_fusion
  33.6 1.8 fusion.15
  35.4 1.8 collective-permute-start.1
  37.2 2.6 collective-permute-done.1
  39.9 3.2 %maximum_select_fusion.1 = f32[2,2,256,512]{3,2,1,0:T(8,128)} fusion(f32[1,2,256,512]{3,2,1,0:T(8,128)} %bitcast.9, f32[1,2,256,512]{3,2,1,0:T(8,128)S(1)} %get-tuple-element.16, pred[]{:T(512)S(6)} %eq.23), kind=kLoop, calls=%fused_computation.8 | loop fusion | flops 1572864 | bytes 4194305 | tf_op jit(solution)/shard_map/jit(_where)/select_n | solution.py:70
  43.1 2.7 collective-permute-start.4
  45.8 0.3 collective-permute-start.3
  46.2 0.7 collective-permute-start.2
  46.9 0.9 slice_bitcast_fusion.1
  47.7 1.3 collective-permute-start.5
  49.0 0.6 gather_fusion
  49.9 2.1 collective-permute-start.8
  52.0 0.5 fusion.13.which_ref
  52.5 1.5 collective-permute-start.7
  54.0 87.1 %collective-permute-done.8 = f32[2,2,32,256]{3,2,1,0:T(8,128)S(1)} collective-permute-done((f32[2,2,32,256]{3,2,1,0:T(8,128)S(1)}, f32[2,2,32,256]{3,2,1,0:T(8,128)S(1)}, u32[]{:S(2)}, u32[]{:S(2)}) %collective-permute-start.8) | collective-permute-done | bytes 131104 | tf_op jit(solution)/shard_map/ppermute | solution.py:21
  141.1 0.8 collective-permute-done.7
  142.0 5.6 %collective-permute-done.6 = f32[2,2,32,256]{3,2,1,0:T(8,128)S(1)} collective-permute-done((f32[2,2,32,256]{3,2,1,0:T(8,128)S(1)}, f32[2,2,32,256]{3,2,1,0:T(8,128)S(1)}, u32[]{:S(2)}, u32[]{:S(2)}) %collective-permute-start.6) | collective-permute-done | bytes 131104 | tf_op jit(solution)/shard_map/ppermute | solution.py:21
  147.6 0.6 gather_fusion.3
  148.3 2.8 maximum_select_fusion
  151.2 5.8 %pad_maximum_fusion = f32[4,2,2,256,512]{4,3,2,1,0:T(8,128)} fusion(f32[1,2,2,256,512]{4,3,2,1,0:T(8,128)} %bitcast.12, f32[1,2,2,256,512]{4,3,2,1,0:T(8,128)} %bitcast.11, f32[1,2,2,256,512]{4,3,2,1,0:T(8,128)} %bitcast.10, f32[1,2,2,256,512]{4,3,2,1,0:T(8,128)S(1)} %maximum_select_fusion), kind=kLoop, calls=%fused_computation.6 | loop fusion | flops 6291456 | bytes 16777216 | tf_op jit(solution)/shard_map/stack | solution.py:71
  157.0 7.7 %gather_fusion.2 = f32[4,2,2,256,512]{4,3,2,1,0:T(8,128)} fusion(f32[4,2,2,256,512]{4,3,2,1,0:T(8,128)} %pad_maximum_fusion, s32[1024]{0:T(1024)S(1)} %pad_clamp_fusion), kind=kCustom, calls=%fused_computation.2 | custom fusion | bytes 16777232 | tf_op jit(solution)/shard_map/gather | solution.py:73
  164.7 50.5 %all-to-all-done.blocks_ref = f32[32,256,256]{2,1,0:T(8,128)} async-done(((f32[32,256,256]{2,1,0:T(8,128)}), f32[32,256,256]{2,1,0:T(8,128)}, u32[]{:S(2)}, u32[]{:S(2)}) %all-to-all-start) | async-done | bytes 8388640 | tf_op jit(solution)/shard_map/all_to_all | solution.py:257
  215.1 16.9 %shard_map.129 = f32[2,256,512]{2,1,0:T(8,128)} custom-call(s32[16]{0:T(128)} %fusion.13.which_ref, f32[32,256,256]{2,1,0:T(8,128)} %all-to-all-done.blocks_ref, f32[8,2,256,512]{3,2,1,0:T(8,128)} %bitcast.72), custom_call_target="tpu_custom_call" | custom-call | flops 1073741824 | bytes 12582912 | tf_op jit(solution)/shard_map/pallas_call | solution.py:229
  232.0 1.4 broadcast_multiply_fusion
  233.5 1.0 fusion.18
  234.6 1.0 fusion.17
  235.6 0.7 fusion.1
  236.3 1.0 fusion.19
  237.5 1.0 slice_select_fusion
  238.4 5.3 %collective-permute-start.10 = (f32[2,128,768]{2,1,0:T(8,128)}, f32[2,128,768]{2,1,0:T(8,128)}, u32[]{:S(2)}, u32[]{:S(2)}) collective-permute-start(f32[2,128,768]{2,1,0:T(8,128)} %slice_select_fusion), channel_id=1, source_target_pairs={{0,1},{1,0},{2,3},{3,2},{4,5},{5,4},{6,7},{7,6},{8,9},{9,8},{10,11... | collective-permute-start | bytes 2359304 | tf_op jit(solution)/shard_map/ppermute | solution.py:34
  243.7 2.3 collective-permute-done.10
  246.0 1.3 select_add_fusion
  247.3 2.8 collective-permute-start.13
  250.1 0.4 collective-permute-start.12
  250.6 0.6 collective-permute-start.11
  251.2 1.1 fusion.16
  252.2 5.9 %collective-permute-done.13 = f32[2,32,768]{2,1,0:T(8,128)S(1)} collective-permute-done((f32[2,32,768]{2,1,0:T(8,128)S(1)}, f32[2,32,768]{2,1,0:T(8,128)S(1)}, u32[]{:S(2)}, u32[]{:S(2)}) %collective-permute-start.13) | collective-permute-done | bytes 196640 | tf_op jit(solution)/shard_map/ppermute | solution.py:21
  258.1 4.6 %collective-permute-done.11 = f32[2,32,768]{2,1,0:T(8,128)S(1)} collective-permute-done((f32[2,32,768]{2,1,0:T(8,128)S(1)}, f32[2,32,768]{2,1,0:T(8,128)S(1)}, u32[]{:S(2)}, u32[]{:S(2)}) %collective-permute-start.11) | collective-permute-done | bytes 196640 | tf_op jit(solution)/shard_map/ppermute | solution.py:21
  262.8 0.4 add_negate_fusion
  263.3 1.0 collective-permute-start.16
  264.3 0.6 collective-permute-start.15
  264.9 0.4 collective-permute-start.14
  265.3 6.0 %collective-permute-done.18 = f32[2,32,512]{2,1,0:T(8,128)S(1)} collective-permute-done((f32[2,32,512]{2,1,0:T(8,128)S(1)}, f32[2,32,512]{2,1,0:T(8,128)S(1)}, u32[]{:S(2)}, u32[]{:S(2)}) %collective-permute-start.18) | collective-permute-done | bytes 131104 | tf_op jit(solution)/shard_map/ppermute | solution.py:16
  271.6 0.7 collective-permute-start.20
  272.3 0.4 collective-permute-start.19
  272.8 1.1 fusion.20
  273.9 0.6 gather_fusion.4
  274.5 2.4 collective-permute-start.17
  277.0 2.4 collective-permute-done.19
  279.5 0.6 gather_fusion.5
  280.1 2.5 collective-permute-start.22
  282.6 1.0 fusion.21
  283.7 0.9 broadcast_multiply_fusion.1
  284.6 1.9 maximum_select_fusion.3
  286.6 1.5 fusion
  (73 shorter events, 2.6 us)
Async XLA Ops:
  0.6 1.1 copy-start
  0.6 12.7 %copy-start.11 = (s32[64,8]{0,1:T(8,128)S(1)}, s32[64,8]{0,1:T(8,128)}, u32[]{:S(2)}) copy-start(s32[64,8]{0,1:T(8,128)} %param.10) | copy-start | bytes 6148
  4.7 20.7 %collective-permute-start = (f32[2,288,256]{2,1,0:T(8,128)S(1)}, f32[2,288,256]{2,1,0:T(8,128)S(1)}, u32[]{:S(2)}, u32[]{:S(2)}) collective-permute-start(f32[2,288,256]{2,1,0:T(8,128)S(1)} %pad_maximum_fusion.3), channel_id=1, source_target_pairs={{0,248},{8,0},{16,8},{24,16},{32,24},{40,32},{48,40},{56,48},{64,5... | collective-permute-start | bytes 1769480 | tf_op jit(solution)/shard_map/ppermute | solution.py:16
  21.7 11.2 %copy-start.12 = (s32[2,1]{0,1:T(1,128)S(1)}, s32[2,1]{0,1:T(1,128)}, u32[]{:S(2)}) copy-start(s32[2,1]{0,1:T(1,128)} %param.13) | copy-start | bytes 28
  21.7 11.2 %copy-start.2 = (f32[2,256,256]{2,1,0:T(8,128)S(1)}, f32[2,256,256]{2,1,0:T(8,128)}, u32[]{:S(2)}) copy-start(f32[2,256,256]{2,1,0:T(8,128)} %param.12) | copy-start | bytes 1572868
  25.4 8.2 %copy-start.7 = (f32[2,288,256]{2,1,0:T(8,128)}, f32[2,288,256]{2,1,0:T(8,128)S(1)}, u32[]{:S(2)}) copy-start(f32[2,288,256]{2,1,0:T(8,128)S(1)} %collective-permute-done) | copy-start | bytes 1769476
  25.4 7.5 %copy-start.8 = (f32[2,256,256]{2,1,0:T(8,128)S(1)}, f32[2,256,256]{2,1,0:T(8,128)}, u32[]{:S(2)}) copy-start(f32[2,256,256]{2,1,0:T(8,128)} %param.11) | copy-start | bytes 1572868
  25.4 189.8 %all-to-all-start = ((f32[32,256,256]{2,1,0:T(8,128)}), f32[32,256,256]{2,1,0:T(8,128)}, u32[]{:S(2)}, u32[]{:S(2)}) async-start(f32[32,256,256]{2,1,0:T(8,128)} %shard_map.128), calls=%async_computation | async-start | bytes 16777216 | tf_op jit(solution)/shard_map/all_to_all | solution.py:257
  35.4 4.5 %collective-permute-start.1 = (f32[2,256,512]{2,1,0:T(8,128)}, f32[2,256,512]{2,1,0:T(8,128)}, u32[]{:S(2)}, u32[]{:S(2)}) collective-permute-start(f32[2,256,512]{2,1,0:T(8,128)} %get-tuple-element.17), channel_id=1, source_target_pairs={{0,1},{1,0},{2,3},{3,2},{4,5},{5,4},{6,7},{7,6},{8,9},{9,8},{10,11... | collective-permute-start | bytes 3145736 | tf_op jit(solution)/shard_map/ppermute | solution.py:69
  43.1 108.0 %collective-permute-start.4 = (f32[2,2,256,512]{3,2,1,0:T(8,128)}, f32[2,2,256,512]{3,2,1,0:T(8,128)}, u32[]{:S(2)}, u32[]{:S(2)}) collective-permute-start(f32[2,2,256,512]{3,2,1,0:T(8,128)} %maximum_select_fusion.1), channel_id=1, source_target_pairs={{0,6},{1,7},{2,0},{3,1},{4,2},{5,3},{6,4},{7,5},{8,14},{9,15},{10,... | collective-permute-start | bytes 6291464 | tf_op jit(solution)/shard_map/ppermute | solution.py:21
  45.8 105.3 %collective-permute-start.3 = (f32[2,2,256,512]{3,2,1,0:T(8,128)}, f32[2,2,256,512]{3,2,1,0:T(8,128)}, u32[]{:S(2)}, u32[]{:S(2)}) collective-permute-start(f32[2,2,256,512]{3,2,1,0:T(8,128)} %maximum_select_fusion.1), channel_id=1, source_target_pairs={{0,4},{1,5},{2,6},{3,7},{4,0},{5,1},{6,2},{7,3},{8,12},{9,13},{10,... | collective-permute-start | bytes 6291464 | tf_op jit(solution)/shard_map/ppermute | solution.py:21
  46.2 105.0 %collective-permute-start.2 = (f32[2,2,256,512]{3,2,1,0:T(8,128)}, f32[2,2,256,512]{3,2,1,0:T(8,128)}, u32[]{:S(2)}, u32[]{:S(2)}) collective-permute-start(f32[2,2,256,512]{3,2,1,0:T(8,128)} %maximum_select_fusion.1), channel_id=1, source_target_pairs={{0,2},{1,3},{2,4},{3,5},{4,6},{5,7},{6,0},{7,1},{8,10},{9,11},{10,... | collective-permute-start | bytes 6291464 | tf_op jit(solution)/shard_map/ppermute | solution.py:21
  47.7 2.2 collective-permute-start.5
  49.9 91.1 %collective-permute-start.8 = (f32[2,2,32,256]{3,2,1,0:T(8,128)S(1)}, f32[2,2,32,256]{3,2,1,0:T(8,128)S(1)}, u32[]{:S(2)}, u32[]{:S(2)}) collective-permute-start(f32[2,2,32,256]{3,2,1,0:T(8,128)S(1)} %maximum_select_fusion.5), channel_id=1, source_target_pairs={{0,6},{1,7},{2,0},{3,1},{4,2},{5,3},{6,4},{7,5},{8,14},{9,15},{10,... | collective-permute-start | bytes 393224 | tf_op jit(solution)/shard_map/ppermute | solution.py:21
  52.5 89.4 %collective-permute-start.7 = (f32[2,2,32,256]{3,2,1,0:T(8,128)S(1)}, f32[2,2,32,256]{3,2,1,0:T(8,128)S(1)}, u32[]{:S(2)}, u32[]{:S(2)}) collective-permute-start(f32[2,2,32,256]{3,2,1,0:T(8,128)S(1)} %maximum_select_fusion.5), channel_id=1, source_target_pairs={{0,4},{1,5},{2,6},{3,7},{4,0},{5,1},{6,2},{7,3},{8,12},{9,13},{10,... | collective-permute-start | bytes 393224 | tf_op jit(solution)/shard_map/ppermute | solution.py:21
  141.1 6.5 %collective-permute-start.6 = (f32[2,2,32,256]{3,2,1,0:T(8,128)S(1)}, f32[2,2,32,256]{3,2,1,0:T(8,128)S(1)}, u32[]{:S(2)}, u32[]{:S(2)}) collective-permute-start(f32[2,2,32,256]{3,2,1,0:T(8,128)S(1)} %maximum_select_fusion.5), channel_id=1, source_target_pairs={{0,2},{1,3},{2,4},{3,5},{4,6},{5,7},{6,0},{7,1},{8,10},{9,11},{10,... | collective-permute-start | bytes 393224 | tf_op jit(solution)/shard_map/ppermute | solution.py:21
  148.3 87.3 %copy-start.3 = (f32[2,8,32,256]{3,2,1,0:T(8,128)}, f32[2,8,32,256]{3,2,1,0:T(8,128)S(1)}, u32[]{:S(2)}) copy-start(f32[2,8,32,256]{3,2,1,0:T(8,128)S(1)} %copy.78) | copy-start | bytes 1572868
  233.5 2.8 copy-start.1
  238.4 7.5 %collective-permute-start.10 = (f32[2,128,768]{2,1,0:T(8,128)}, f32[2,128,768]{2,1,0:T(8,128)}, u32[]{:S(2)}, u32[]{:S(2)}) collective-permute-start(f32[2,128,768]{2,1,0:T(8,128)} %slice_select_fusion), channel_id=1, source_target_pairs={{0,1},{1,0},{2,3},{3,2},{4,5},{5,4},{6,7},{7,6},{8,9},{9,8},{10,11... | collective-permute-start | bytes 2359304 | tf_op jit(solution)/shard_map/ppermute | solution.py:34
  243.7 19.0 %collective-permute-start.9 = (f32[2,256,256]{2,1,0:T(8,128)S(1)}, f32[2,256,256]{2,1,0:T(8,128)S(1)}, u32[]{:S(2)}, u32[]{:S(2)}) collective-permute-start(f32[2,256,256]{2,1,0:T(8,128)S(1)} %fusion.1), channel_id=1, source_target_pairs={{0,8},{8,16},{16,24},{24,32},{32,40},{40,48},{48,56},{56,64},{64,7... | collective-permute-start | bytes 1572872 | tf_op jit(solution)/shard_map/ppermute | solution.py:16
  247.2 15.5 %copy-start.4 = (f32[2,8,32,256]{3,2,1,0:T(8,128)S(1)}, f32[2,8,32,256]{3,2,1,0:T(8,128)}, u32[]{:S(2)}) copy-start(f32[2,8,32,256]{3,2,1,0:T(8,128)} %copy-done.3) | copy-start | bytes 1572868
  247.3 10.8 %collective-permute-start.13 = (f32[2,32,768]{2,1,0:T(8,128)S(1)}, f32[2,32,768]{2,1,0:T(8,128)S(1)}, u32[]{:S(2)}, u32[]{:S(2)}) collective-permute-start(f32[2,32,768]{2,1,0:T(8,128)S(1)} %get-tuple-element.19), channel_id=1, source_target_pairs={{0,6},{1,7},{2,0},{3,1},{4,2},{5,3},{6,4},{7,5},{8,14},{9,15},{10,... | collective-permute-start | bytes 589832 | tf_op jit(solution)/shard_map/ppermute | solution.py:21
  250.1 8.0 %collective-permute-start.12 = (f32[2,32,768]{2,1,0:T(8,128)S(1)}, f32[2,32,768]{2,1,0:T(8,128)S(1)}, u32[]{:S(2)}, u32[]{:S(2)}) collective-permute-start(f32[2,32,768]{2,1,0:T(8,128)S(1)} %get-tuple-element.20), channel_id=1, source_target_pairs={{0,4},{1,5},{2,6},{3,7},{4,0},{5,1},{6,2},{7,3},{8,12},{9,13},{10,... | collective-permute-start | bytes 589832 | tf_op jit(solution)/shard_map/ppermute | solution.py:21
  250.6 12.1 %collective-permute-start.11 = (f32[2,32,768]{2,1,0:T(8,128)S(1)}, f32[2,32,768]{2,1,0:T(8,128)S(1)}, u32[]{:S(2)}, u32[]{:S(2)}) collective-permute-start(f32[2,32,768]{2,1,0:T(8,128)S(1)} %get-tuple-element.18), channel_id=1, source_target_pairs={{0,2},{1,3},{2,4},{3,5},{4,6},{5,7},{6,0},{7,1},{8,10},{9,11},{10,... | collective-permute-start | bytes 589832 | tf_op jit(solution)/shard_map/ppermute | solution.py:21
  262.7 11.1 %copy-start.9 = (f32[2,256,256]{2,1,0:T(8,128)}, f32[2,256,256]{2,1,0:T(8,128)S(1)}, u32[]{:S(2)}) copy-start(f32[2,256,256]{2,1,0:T(8,128)S(1)} %collective-permute-done.9) | copy-start | bytes 1572868
  263.2 8.1 %collective-permute-start.18 = (f32[2,32,512]{2,1,0:T(8,128)S(1)}, f32[2,32,512]{2,1,0:T(8,128)S(1)}, u32[]{:S(2)}, u32[]{:S(2)}) collective-permute-start(f32[2,32,512]{2,1,0:T(8,128)S(1)} %pad_maximum_fusion.7), channel_id=1, source_target_pairs={{0,8},{8,16},{16,24},{24,32},{32,40},{40,48},{48,56},{56,64},{64,7... | collective-permute-start | bytes 393224 | tf_op jit(solution)/shard_map/ppermute | solution.py:16
  263.3 9.0 %collective-permute-start.16 = (f32[2,32,256]{2,1,0:T(8,128)S(1)}, f32[2,32,256]{2,1,0:T(8,128)S(1)}, u32[]{:S(2)}, u32[]{:S(2)}) collective-permute-start(f32[2,32,256]{2,1,0:T(8,128)S(1)} %slice_subtract_fusion), channel_id=1, source_target_pairs={{0,6},{1,7},{2,0},{3,1},{4,2},{5,3},{6,4},{7,5},{8,14},{9,15},{10,... | collective-permute-start | bytes 196616 | tf_op jit(solution)/shard_map/ppermute | solution.py:21
  264.3 9.5 %collective-permute-start.15 = (f32[2,32,256]{2,1,0:T(8,128)S(1)}, f32[2,32,256]{2,1,0:T(8,128)S(1)}, u32[]{:S(2)}, u32[]{:S(2)}) collective-permute-start(f32[2,32,256]{2,1,0:T(8,128)S(1)} %slice_subtract_fusion), channel_id=1, source_target_pairs={{0,4},{1,5},{2,6},{3,7},{4,0},{5,1},{6,2},{7,3},{8,12},{9,13},{10,... | collective-permute-start | bytes 196616 | tf_op jit(solution)/shard_map/ppermute | solution.py:21
  264.9 8.9 %collective-permute-start.14 = (f32[2,32,256]{2,1,0:T(8,128)S(1)}, f32[2,32,256]{2,1,0:T(8,128)S(1)}, u32[]{:S(2)}, u32[]{:S(2)}) collective-permute-start(f32[2,32,256]{2,1,0:T(8,128)S(1)} %slice_subtract_fusion), channel_id=1, source_target_pairs={{0,2},{1,3},{2,4},{3,5},{4,6},{5,7},{6,0},{7,1},{8,10},{9,11},{10,... | collective-permute-start | bytes 196616 | tf_op jit(solution)/shard_map/ppermute | solution.py:21
  271.3 5.6 %collective-permute-start.21 = (f32[2,32,512]{2,1,0:T(8,128)S(1)}, f32[2,32,512]{2,1,0:T(8,128)S(1)}, u32[]{:S(2)}, u32[]{:S(2)}) collective-permute-start(f32[2,32,512]{2,1,0:T(8,128)S(1)} %collective-permute-done.18), channel_id=1, source_target_pairs={{0,6},{1,7},{2,0},{3,1},{4,2},{5,3},{6,4},{7,5},{8,14},{9,15},{10,... | collective-permute-start | bytes 393224 | tf_op jit(solution)/shard_map/ppermute | solution.py:21
  271.6 5.4 %collective-permute-start.20 = (f32[2,32,512]{2,1,0:T(8,128)S(1)}, f32[2,32,512]{2,1,0:T(8,128)S(1)}, u32[]{:S(2)}, u32[]{:S(2)}) collective-permute-start(f32[2,32,512]{2,1,0:T(8,128)S(1)} %collective-permute-done.18), channel_id=1, source_target_pairs={{0,4},{1,5},{2,6},{3,7},{4,0},{5,1},{6,2},{7,3},{8,12},{9,13},{10,... | collective-permute-start | bytes 393224 | tf_op jit(solution)/shard_map/ppermute | solution.py:21
  272.3 7.1 %collective-permute-start.19 = (f32[2,32,512]{2,1,0:T(8,128)S(1)}, f32[2,32,512]{2,1,0:T(8,128)S(1)}, u32[]{:S(2)}, u32[]{:S(2)}) collective-permute-start(f32[2,32,512]{2,1,0:T(8,128)S(1)} %collective-permute-done.18), channel_id=1, source_target_pairs={{0,2},{1,3},{2,4},{3,5},{4,6},{5,7},{6,0},{7,1},{8,10},{9,11},{10,... | collective-permute-start | bytes 393224 | tf_op jit(solution)/shard_map/ppermute | solution.py:21
  273.9 8.7 %copy-start.6 = (f32[2,256,256]{2,1,0:T(8,128)S(1)}, f32[2,256,256]{2,1,0:T(8,128)}, u32[]{:S(2)}) copy-start(f32[2,256,256]{2,1,0:T(8,128)} %param.14) | copy-start | bytes 1572868
  274.5 10.1 %collective-permute-start.17 = (f32[2,128,256]{2,1,0:T(8,128)S(1)}, f32[2,128,256]{2,1,0:T(8,128)}, u32[]{:S(2)}, u32[]{:S(2)}) collective-permute-start(f32[2,128,256]{2,1,0:T(8,128)S(1)} %bitcast.82), channel_id=1, source_target_pairs={{0,1},{1,0},{2,3},{3,2},{4,5},{5,4},{6,7},{7,6},{8,9},{9,8},{10,11... | collective-permute-start | bytes 786440 | tf_op jit(solution)/shard_map/ppermute | solution.py:57
  279.5 4.2 %copy-start.10 = (f32[2,256,256]{2,1,0:T(8,128)S(1)}, f32[2,256,256]{2,1,0:T(8,128)}, u32[]{:S(2)}) copy-start(f32[2,256,256]{2,1,0:T(8,128)} %copy-done.9) | copy-start | bytes 1572868
  280.1 6.3 %collective-permute-start.22 = (f32[2,128,512]{2,1,0:T(8,128)S(1)}, f32[2,128,512]{2,1,0:T(8,128)S(1)}, u32[]{:S(2)}, u32[]{:S(2)}) collective-permute-start(f32[2,128,512]{2,1,0:T(8,128)S(1)} %bitcast.75), channel_id=1, source_target_pairs={{0,1},{1,0},{2,3},{3,2},{4,5},{5,4},{6,7},{7,6},{8,9},{9,8},{10,11... | collective-permute-start | bytes 1572872 | tf_op jit(solution)/shard_map/ppermute | solution.py:57
  286.6 1.5 copy-start.5

commit v10 on v8

--- a/solution.py
+++ b/solution.py
@@ -154,18 +154,15 @@
     return gather_blocks(sigma_local, chosen_row, chosen_col)
 
 
-def _take_blocks(which_ref, src_ref, out_ref, staged, sems_in, sem_out):
-    count = staged.shape[0]
+def _take_blocks(which_ref, src_ref, out_ref, sems):
+    count = out_ref.shape[0]
     copies = []
     for i in range(count):
-        copy = pltpu.make_async_copy(src_ref.at[which_ref[i]], staged.at[i], sems_in.at[i])
+        copy = pltpu.make_async_copy(src_ref.at[which_ref[i]], out_ref.at[i], sems.at[i])
         copy.start()
         copies.append(copy)
     for copy in copies:
         copy.wait()
-    store = pltpu.make_async_copy(staged, out_ref, sem_out)
-    store.start()
-    store.wait()
 
 
 def select_take(received, row_blocks, slots, cols_here):
@@ -178,11 +175,7 @@
         grid=(),
         in_specs=[pl.BlockSpec(memory_space=pl.ANY)],
         out_specs=pl.BlockSpec(memory_space=pl.ANY),
-        scratch_shapes=[
-            pltpu.VMEM((count, B, B), received.dtype),
-            pltpu.SemaphoreType.DMA((count,)),
-            pltpu.SemaphoreType.DMA(()),
-        ],
+        scratch_shapes=[pltpu.SemaphoreType.DMA((count,))],
     )
     taken = pl.pallas_call(
         _take_blocks,

time: 286 us -> 410 us (1.43)
  Pallas kernels: 11.3 us -> 135 us
    pallas_call x1, Pallas kernels: 4.94 us -> 129 us  [select_take(): pl.pallas_call(_take_blocks, out_shape=jax.ShapeDtypeStruct((count, B, B)...]
  transfers between devices with their start and end apart: 24 -> 24, of which waited for: 13 -> 13; matrix products, arithmetic and copies ran while one was open for 12% -> 9% of each run, Pallas kernels for 2% -> 2%
where the time goes in v10:
time: 410 us; the launch traced here: 409 us
  waiting for transfers between devices  172 us (42%)
  Pallas kernels  135 us (33%)
  starting transfers between devices  44 us (11%)
  matrix products  22.7 us (6%)
  other arithmetic  21.4 us (5%)
  local copies, waits for them, and re-layouts  12.5 us (3%)
    pallas_call x1, Pallas kernels, select_take(): pl.pallas_call(_take_blocks, out_shape=jax.ShapeDtypeStruct((count, B, B)...  129 us
    ppermute x15, waiting for transfers between devices, _towards(): lax.ppermute(value, 'row', [(i, (i + 2 * by) % length) for i in range(len...  106 us
    all_to_all x1, waiting for transfers between devices, on_device(): lax.all_to_all(outgoing, 'own', split_axis=0, concat_axis=0, tiled=True)  50.5 us
    dot_general x13, matrix products, product(): return jnp.einsum(form, left, right, precision=HIGH)  22.7 us
    ppermute x15, starting transfers between devices, _towards(): lax.ppermute(value, 'row', [(i, (i + 2 * by) % length) for i in range(len...  14.5 us
    ppermute x3, waiting for transfers between devices, shifted(): lax.ppermute(shard, axis, [(i, (i + by) % length) for i in range(length)])  9.88 us
    ppermute x3, starting transfers between devices, shifted(): lax.ppermute(shard, axis, [(i, (i + by) % length) for i in range(length)])  8.76 us
    gather x2, local copies, waits for them, and re-layouts, row_gather(): return stacked[order].reshape((length,) + x.shape)  8.28 us
  transfers between devices with their start and end apart: 24, of which 13 were waited for; matrix products, arithmetic and copies ran while one was open for 9% of the time, Pallas kernels for 2%

profile of v10, /device:TPU:1, one launch (start us, length us, event | category | flops | bytes accessed | tf_op | source)
XLA Modules:
  0.0 409.0 jit_solution(12129798222150015007)
XLA Ops:
  0.7 0.7 convert_bitcast_fusion
  1.7 1.2 fusion.10
  2.9 1.7 convolution_multiply_fusion.1
  4.7 8.7 %collective-permute-start = (f32[2,288,256]{2,1,0:T(8,128)S(1)}, f32[2,288,256]{2,1,0:T(8,128)S(1)}, u32[]{:S(2)}, u32[]{:S(2)}) collective-permute-start(f32[2,288,256]{2,1,0:T(8,128)S(1)} %pad_maximum_fusion.3), channel_id=1, source_target_pairs={{0,248},{8,0},{16,8},{24,16},{32,24},{40,32},{48,40},{56,48},{64,5... | collective-permute-start | bytes 1769480 | tf_op jit(solution)/shard_map/ppermute | solution.py:16
  13.9 0.7 gather_fusion.1
  14.6 0.7 clamp_reduce_fusion
  15.3 6.4 %shard_map.128 = f32[32,256,256]{2,1,0:T(8,128)} custom-call(s32[32]{0:T(128)} %get-tuple-element.14.rows_ref, s32[32]{0:T(128)} %get-tuple-element.13.cols_ref, f32[2048,512]{1,0:T(8,128)} %src_ref.1), custom_call_target="tpu_custom_call" | custom-call | bytes 12582912 | tf_op jit(solution)/shard_map/pallas_call | solution.py:121
  21.7 3.7 collective-permute-done
  25.4 7.4 %all-to-all-start = ((f32[32,256,256]{2,1,0:T(8,128)}), f32[32,256,256]{2,1,0:T(8,128)}, u32[]{:S(2)}, u32[]{:S(2)}) async-start(f32[32,256,256]{2,1,0:T(8,128)} %shard_map.128), calls=%async_computation | async-start | bytes 16777216 | tf_op jit(solution)/shard_map/all_to_all | solution.py:207
  32.9 0.7 convolution_multiply_fusion
  33.6 1.8 fusion.23
  35.4 1.8 collective-permute-start.1
  37.2 2.6 collective-permute-done.1
  39.9 3.2 maximum_select_fusion.1
  43.1 2.7 collective-permute-start.4
  45.8 0.3 collective-permute-start.3
  46.2 0.7 collective-permute-start.2
  46.9 0.9 slice_bitcast_fusion.1
  47.7 1.3 collective-permute-start.5
  49.0 0.6 gather_fusion
  49.9 2.1 collective-permute-start.8
  52.0 0.5 fusion.21.which_ref
  52.5 1.5 collective-permute-start.7
  54.0 87.1 %collective-permute-done.8 = f32[2,2,32,256]{3,2,1,0:T(8,128)S(1)} collective-permute-done((f32[2,2,32,256]{3,2,1,0:T(8,128)S(1)}, f32[2,2,32,256]{3,2,1,0:T(8,128)S(1)}, u32[]{:S(2)}, u32[]{:S(2)}) %collective-permute-start.8) | collective-permute-done | bytes 131104 | tf_op jit(solution)/shard_map/ppermute | solution.py:21
  141.1 0.8 collective-permute-done.7
  142.0 5.6 %collective-permute-done.6 = f32[2,2,32,256]{3,2,1,0:T(8,128)S(1)} collective-permute-done((f32[2,2,32,256]{3,2,1,0:T(8,128)S(1)}, f32[2,2,32,256]{3,2,1,0:T(8,128)S(1)}, u32[]{:S(2)}, u32[]{:S(2)}) %collective-permute-start.6) | collective-permute-done | bytes 131104 | tf_op jit(solution)/shard_map/ppermute | solution.py:21
  147.6 0.6 gather_fusion.3
  148.3 2.8 maximum_select_fusion
  151.2 5.8 %pad_maximum_fusion = f32[4,2,2,256,512]{4,3,2,1,0:T(8,128)} fusion(f32[1,2,2,256,512]{4,3,2,1,0:T(8,128)} %bitcast.13, f32[1,2,2,256,512]{4,3,2,1,0:T(8,128)} %bitcast.12, f32[1,2,2,256,512]{4,3,2,1,0:T(8,128)} %bitcast.11, f32[1,2,2,256,512]{4,3,2,1,0:T(8,128)S(1)} %maximum_select_fusion), kind=kLoop, calls=%fused_computation.6 | loop fusion | flops 6291456 | bytes 16777216 | tf_op jit(solution)/shard_map/stack | solution.py:71
  157.0 7.7 %gather_fusion.2 = f32[4,2,2,256,512]{4,3,2,1,0:T(8,128)} fusion(f32[4,2,2,256,512]{4,3,2,1,0:T(8,128)} %pad_maximum_fusion, s32[1024]{0:T(1024)S(1)} %pad_clamp_fusion), kind=kCustom, calls=%fused_computation.2 | custom fusion | bytes 16777232 | tf_op jit(solution)/shard_map/gather | solution.py:73
  164.7 50.5 %all-to-all-done.src_ref = f32[32,256,256]{2,1,0:T(8,128)} async-done(((f32[32,256,256]{2,1,0:T(8,128)}), f32[32,256,256]{2,1,0:T(8,128)}, u32[]{:S(2)}, u32[]{:S(2)}) %all-to-all-start) | async-done | bytes 8388640 | tf_op jit(solution)/shard_map/all_to_all | solution.py:207
  215.1 129.0 %shard_map.129 = f32[16,256,256]{2,1,0:T(8,128)} custom-call(s32[16]{0:T(128)} %fusion.21.which_ref, f32[32,256,256]{2,1,0:T(8,128)} %all-to-all-done.src_ref), custom_call_target="tpu_custom_call" | custom-call | bytes 8388608 | tf_op jit(solution)/shard_map/pallas_call | solution.py:180
  344.1 10.2 %fusion.5 = f32[2,256,512]{2,1,0:T(8,128)S(1)} fusion(f32[2,8,256,256]{3,2,1,0:T(8,128)} %bitcast.80, f32[8,2,256,512]{3,2,1,0:T(8,128)} %bitcast.79, f32[2]{0:T(128)S(1)} %convert_bitcast_fusion.1), kind=kOutput, calls=%fused_computation.13 | convolution fusion | flops 6442713088 | bytes 13631496 | tf_op jit(solution)/shard_map/kmij,mkjc->kic/dot_general | solution.py:87
  354.4 1.0 fusion.26
  355.5 1.0 fusion.25
  356.5 0.7 fusion.9
  357.2 1.0 fusion.27
  358.4 1.0 slice_select_fusion
  359.4 5.3 %collective-permute-start.10 = (f32[2,128,768]{2,1,0:T(8,128)}, f32[2,128,768]{2,1,0:T(8,128)}, u32[]{:S(2)}, u32[]{:S(2)}) collective-permute-start(f32[2,128,768]{2,1,0:T(8,128)} %slice_select_fusion), channel_id=1, source_target_pairs={{0,1},{1,0},{2,3},{3,2},{4,5},{5,4},{6,7},{7,6},{8,9},{9,8},{10,11... | collective-permute-start | bytes 2359304 | tf_op jit(solution)/shard_map/ppermute | solution.py:34
  364.6 2.3 collective-permute-done.10
  366.9 1.3 select_add_fusion
  368.2 2.8 collective-permute-start.13
  371.1 0.4 collective-permute-start.12
  371.5 0.6 collective-permute-start.11
  372.1 1.1 fusion.24
  373.2 5.9 %collective-permute-done.13 = f32[2,32,768]{2,1,0:T(8,128)S(1)} collective-permute-done((f32[2,32,768]{2,1,0:T(8,128)S(1)}, f32[2,32,768]{2,1,0:T(8,128)S(1)}, u32[]{:S(2)}, u32[]{:S(2)}) %collective-permute-start.13) | collective-permute-done | bytes 196640 | tf_op jit(solution)/shard_map/ppermute | solution.py:21
  379.0 4.6 %collective-permute-done.11 = f32[2,32,768]{2,1,0:T(8,128)S(1)} collective-permute-done((f32[2,32,768]{2,1,0:T(8,128)S(1)}, f32[2,32,768]{2,1,0:T(8,128)S(1)}, u32[]{:S(2)}, u32[]{:S(2)}) %collective-permute-start.11) | collective-permute-done | bytes 196640 | tf_op jit(solution)/shard_map/ppermute | solution.py:21
  383.7 0.4 add_negate_fusion
  384.2 0.8 collective-permute-start.16
  385.0 0.6 collective-permute-start.15
  385.6 0.4 collective-permute-start.14
  386.0 6.2 %collective-permute-done.18 = f32[2,32,512]{2,1,0:T(8,128)S(1)} collective-permute-done((f32[2,32,512]{2,1,0:T(8,128)S(1)}, f32[2,32,512]{2,1,0:T(8,128)S(1)}, u32[]{:S(2)}, u32[]{:S(2)}) %collective-permute-start.18) | collective-permute-done | bytes 131104 | tf_op jit(solution)/shard_map/ppermute | solution.py:16
  392.5 0.7 collective-permute-start.20
  393.3 0.4 collective-permute-start.19
  393.7 1.1 fusion.28
  394.8 0.6 gather_fusion.4
  395.4 2.4 collective-permute-start.17
  397.9 2.4 collective-permute-done.19
  400.3 0.6 gather_fusion.5
  401.0 2.5 collective-permute-start.22
  403.5 1.0 fusion.29
  404.6 0.9 broadcast_multiply_fusion
  405.5 1.9 maximum_select_fusion.3
  407.5 1.5 fusion.8
  (73 shorter events, 2.6 us)
Async XLA Ops:
  0.6 1.1 copy-start
  0.6 12.7 %copy-start.11 = (s32[64,8]{0,1:T(8,128)S(1)}, s32[64,8]{0,1:T(8,128)}, u32[]{:S(2)}) copy-start(s32[64,8]{0,1:T(8,128)} %param.10) | copy-start | bytes 6148
  4.7 20.7 %collective-permute-start = (f32[2,288,256]{2,1,0:T(8,128)S(1)}, f32[2,288,256]{2,1,0:T(8,128)S(1)}, u32[]{:S(2)}, u32[]{:S(2)}) collective-permute-start(f32[2,288,256]{2,1,0:T(8,128)S(1)} %pad_maximum_fusion.3), channel_id=1, source_target_pairs={{0,248},{8,0},{16,8},{24,16},{32,24},{40,32},{48,40},{56,48},{64,5... | collective-permute-start | bytes 1769480 | tf_op jit(solution)/shard_map/ppermute | solution.py:16
  21.7 11.2 %copy-start.12 = (s32[2,1]{0,1:T(1,128)S(1)}, s32[2,1]{0,1:T(1,128)}, u32[]{:S(2)}) copy-start(s32[2,1]{0,1:T(1,128)} %param.13) | copy-start | bytes 28
  21.7 11.2 %copy-start.2 = (f32[2,256,256]{2,1,0:T(8,128)S(1)}, f32[2,256,256]{2,1,0:T(8,128)}, u32[]{:S(2)}) copy-start(f32[2,256,256]{2,1,0:T(8,128)} %param.12) | copy-start | bytes 1572868
  25.4 8.2 %copy-start.7 = (f32[2,288,256]{2,1,0:T(8,128)}, f32[2,288,256]{2,1,0:T(8,128)S(1)}, u32[]{:S(2)}) copy-start(f32[2,288,256]{2,1,0:T(8,128)S(1)} %collective-permute-done) | copy-start | bytes 1769476
  25.4 7.5 %copy-start.8 = (f32[2,256,256]{2,1,0:T(8,128)S(1)}, f32[2,256,256]{2,1,0:T(8,128)}, u32[]{:S(2)}) copy-start(f32[2,256,256]{2,1,0:T(8,128)} %param.11) | copy-start | bytes 1572868
  25.4 189.8 %all-to-all-start = ((f32[32,256,256]{2,1,0:T(8,128)}), f32[32,256,256]{2,1,0:T(8,128)}, u32[]{:S(2)}, u32[]{:S(2)}) async-start(f32[32,256,256]{2,1,0:T(8,128)} %shard_map.128), calls=%async_computation | async-start | bytes 16777216 | tf_op jit(solution)/shard_map/all_to_all | solution.py:207
  35.4 4.5 %collective-permute-start.1 = (f32[2,256,512]{2,1,0:T(8,128)}, f32[2,256,512]{2,1,0:T(8,128)}, u32[]{:S(2)}, u32[]{:S(2)}) collective-permute-start(f32[2,256,512]{2,1,0:T(8,128)} %get-tuple-element.17), channel_id=1, source_target_pairs={{0,1},{1,0},{2,3},{3,2},{4,5},{5,4},{6,7},{7,6},{8,9},{9,8},{10,11... | collective-permute-start | bytes 3145736 | tf_op jit(solution)/shard_map/ppermute | solution.py:69
  43.1 108.0 %collective-permute-start.4 = (f32[2,2,256,512]{3,2,1,0:T(8,128)}, f32[2,2,256,512]{3,2,1,0:T(8,128)}, u32[]{:S(2)}, u32[]{:S(2)}) collective-permute-start(f32[2,2,256,512]{3,2,1,0:T(8,128)} %maximum_select_fusion.1), channel_id=1, source_target_pairs={{0,6},{1,7},{2,0},{3,1},{4,2},{5,3},{6,4},{7,5},{8,14},{9,15},{10,... | collective-permute-start | bytes 6291464 | tf_op jit(solution)/shard_map/ppermute | solution.py:21
  45.8 105.3 %collective-permute-start.3 = (f32[2,2,256,512]{3,2,1,0:T(8,128)}, f32[2,2,256,512]{3,2,1,0:T(8,128)}, u32[]{:S(2)}, u32[]{:S(2)}) collective-permute-start(f32[2,2,256,512]{3,2,1,0:T(8,128)} %maximum_select_fusion.1), channel_id=1, source_target_pairs={{0,4},{1,5},{2,6},{3,7},{4,0},{5,1},{6,2},{7,3},{8,12},{9,13},{10,... | collective-permute-start | bytes 6291464 | tf_op jit(solution)/shard_map/ppermute | solution.py:21
  46.2 105.0 %collective-permute-start.2 = (f32[2,2,256,512]{3,2,1,0:T(8,128)}, f32[2,2,256,512]{3,2,1,0:T(8,128)}, u32[]{:S(2)}, u32[]{:S(2)}) collective-permute-start(f32[2,2,256,512]{3,2,1,0:T(8,128)} %maximum_select_fusion.1), channel_id=1, source_target_pairs={{0,2},{1,3},{2,4},{3,5},{4,6},{5,7},{6,0},{7,1},{8,10},{9,11},{10,... | collective-permute-start | bytes 6291464 | tf_op jit(solution)/shard_map/ppermute | solution.py:21
  47.7 2.2 collective-permute-start.5
  49.9 91.1 %collective-permute-start.8 = (f32[2,2,32,256]{3,2,1,0:T(8,128)S(1)}, f32[2,2,32,256]{3,2,1,0:T(8,128)S(1)}, u32[]{:S(2)}, u32[]{:S(2)}) collective-permute-start(f32[2,2,32,256]{3,2,1,0:T(8,128)S(1)} %maximum_select_fusion.5), channel_id=1, source_target_pairs={{0,6},{1,7},{2,0},{3,1},{4,2},{5,3},{6,4},{7,5},{8,14},{9,15},{10,... | collective-permute-start | bytes 393224 | tf_op jit(solution)/shard_map/ppermute | solution.py:21
  52.5 89.4 %collective-permute-start.7 = (f32[2,2,32,256]{3,2,1,0:T(8,128)S(1)}, f32[2,2,32,256]{3,2,1,0:T(8,128)S(1)}, u32[]{:S(2)}, u32[]{:S(2)}) collective-permute-start(f32[2,2,32,256]{3,2,1,0:T(8,128)S(1)} %maximum_select_fusion.5), channel_id=1, source_target_pairs={{0,4},{1,5},{2,6},{3,7},{4,0},{5,1},{6,2},{7,3},{8,12},{9,13},{10,... | collective-permute-start | bytes 393224 | tf_op jit(solution)/shard_map/ppermute | solution.py:21
  141.1 6.5 %collective-permute-start.6 = (f32[2,2,32,256]{3,2,1,0:T(8,128)S(1)}, f32[2,2,32,256]{3,2,1,0:T(8,128)S(1)}, u32[]{:S(2)}, u32[]{:S(2)}) collective-permute-start(f32[2,2,32,256]{3,2,1,0:T(8,128)S(1)} %maximum_select_fusion.5), channel_id=1, source_target_pairs={{0,2},{1,3},{2,4},{3,5},{4,6},{5,7},{6,0},{7,1},{8,10},{9,11},{10,... | collective-permute-start | bytes 393224 | tf_op jit(solution)/shard_map/ppermute | solution.py:21
  148.3 208.3 %copy-start.3 = (f32[2,8,32,256]{3,2,1,0:T(8,128)}, f32[2,8,32,256]{3,2,1,0:T(8,128)S(1)}, u32[]{:S(2)}) copy-start(f32[2,8,32,256]{3,2,1,0:T(8,128)S(1)} %copy.82) | copy-start | bytes 1572868
  354.4 2.8 copy-start.1
  359.4 7.5 %collective-permute-start.10 = (f32[2,128,768]{2,1,0:T(8,128)}, f32[2,128,768]{2,1,0:T(8,128)}, u32[]{:S(2)}, u32[]{:S(2)}) collective-permute-start(f32[2,128,768]{2,1,0:T(8,128)} %slice_select_fusion), channel_id=1, source_target_pairs={{0,1},{1,0},{2,3},{3,2},{4,5},{5,4},{6,7},{7,6},{8,9},{9,8},{10,11... | collective-permute-start | bytes 2359304 | tf_op jit(solution)/shard_map/ppermute | solution.py:34
  364.6 19.0 %collective-permute-start.9 = (f32[2,256,256]{2,1,0:T(8,128)S(1)}, f32[2,256,256]{2,1,0:T(8,128)S(1)}, u32[]{:S(2)}, u32[]{:S(2)}) collective-permute-start(f32[2,256,256]{2,1,0:T(8,128)S(1)} %fusion.9), channel_id=1, source_target_pairs={{0,8},{8,16},{16,24},{24,32},{32,40},{40,48},{48,56},{56,64},{64,7... | collective-permute-start | bytes 1572872 | tf_op jit(solution)/shard_map/ppermute | solution.py:16
  368.2 15.5 %copy-start.4 = (f32[2,8,32,256]{3,2,1,0:T(8,128)S(1)}, f32[2,8,32,256]{3,2,1,0:T(8,128)}, u32[]{:S(2)}) copy-start(f32[2,8,32,256]{3,2,1,0:T(8,128)} %copy-done.3) | copy-start | bytes 1572868
  368.2 10.8 %collective-permute-start.13 = (f32[2,32,768]{2,1,0:T(8,128)S(1)}, f32[2,32,768]{2,1,0:T(8,128)S(1)}, u32[]{:S(2)}, u32[]{:S(2)}) collective-permute-start(f32[2,32,768]{2,1,0:T(8,128)S(1)} %get-tuple-element.19), channel_id=1, source_target_pairs={{0,6},{1,7},{2,0},{3,1},{4,2},{5,3},{6,4},{7,5},{8,14},{9,15},{10,... | collective-permute-start | bytes 589832 | tf_op jit(solution)/shard_map/ppermute | solution.py:21
  371.1 8.0 %collective-permute-start.12 = (f32[2,32,768]{2,1,0:T(8,128)S(1)}, f32[2,32,768]{2,1,0:T(8,128)S(1)}, u32[]{:S(2)}, u32[]{:S(2)}) collective-permute-start(f32[2,32,768]{2,1,0:T(8,128)S(1)} %get-tuple-element.20), channel_id=1, source_target_pairs={{0,4},{1,5},{2,6},{3,7},{4,0},{5,1},{6,2},{7,3},{8,12},{9,13},{10,... | collective-permute-start | bytes 589832 | tf_op jit(solution)/shard_map/ppermute | solution.py:21
  371.5 12.1 %collective-permute-start.11 = (f32[2,32,768]{2,1,0:T(8,128)S(1)}, f32[2,32,768]{2,1,0:T(8,128)S(1)}, u32[]{:S(2)}, u32[]{:S(2)}) collective-permute-start(f32[2,32,768]{2,1,0:T(8,128)S(1)} %get-tuple-element.18), channel_id=1, source_target_pairs={{0,2},{1,3},{2,4},{3,5},{4,6},{5,7},{6,0},{7,1},{8,10},{9,11},{10,... | collective-permute-start | bytes 589832 | tf_op jit(solution)/shard_map/ppermute | solution.py:21
  383.7 11.1 %copy-start.9 = (f32[2,256,256]{2,1,0:T(8,128)}, f32[2,256,256]{2,1,0:T(8,128)S(1)}, u32[]{:S(2)}) copy-start(f32[2,256,256]{2,1,0:T(8,128)S(1)} %collective-permute-done.9) | copy-start | bytes 1572868
  384.1 8.1 %collective-permute-start.18 = (f32[2,32,512]{2,1,0:T(8,128)S(1)}, f32[2,32,512]{2,1,0:T(8,128)S(1)}, u32[]{:S(2)}, u32[]{:S(2)}) collective-permute-start(f32[2,32,512]{2,1,0:T(8,128)S(1)} %pad_maximum_fusion.7), channel_id=1, source_target_pairs={{0,8},{8,16},{16,24},{24,32},{32,40},{40,48},{48,56},{56,64},{64,7... | collective-permute-start | bytes 393224 | tf_op jit(solution)/shard_map/ppermute | solution.py:16
  384.2 9.0 %collective-permute-start.16 = (f32[2,32,256]{2,1,0:T(8,128)S(1)}, f32[2,32,256]{2,1,0:T(8,128)S(1)}, u32[]{:S(2)}, u32[]{:S(2)}) collective-permute-start(f32[2,32,256]{2,1,0:T(8,128)S(1)} %slice_subtract_fusion), channel_id=1, source_target_pairs={{0,6},{1,7},{2,0},{3,1},{4,2},{5,3},{6,4},{7,5},{8,14},{9,15},{10,... | collective-permute-start | bytes 196616 | tf_op jit(solution)/shard_map/ppermute | solution.py:21
  385.0 9.8 %collective-permute-start.15 = (f32[2,32,256]{2,1,0:T(8,128)S(1)}, f32[2,32,256]{2,1,0:T(8,128)S(1)}, u32[]{:S(2)}, u32[]{:S(2)}) collective-permute-start(f32[2,32,256]{2,1,0:T(8,128)S(1)} %slice_subtract_fusion), channel_id=1, source_target_pairs={{0,4},{1,5},{2,6},{3,7},{4,0},{5,1},{6,2},{7,3},{8,12},{9,13},{10,... | collective-permute-start | bytes 196616 | tf_op jit(solution)/shard_map/ppermute | solution.py:21
  385.6 9.1 %collective-permute-start.14 = (f32[2,32,256]{2,1,0:T(8,128)S(1)}, f32[2,32,256]{2,1,0:T(8,128)S(1)}, u32[]{:S(2)}, u32[]{:S(2)}) collective-permute-start(f32[2,32,256]{2,1,0:T(8,128)S(1)} %slice_subtract_fusion), channel_id=1, source_target_pairs={{0,2},{1,3},{2,4},{3,5},{4,6},{5,7},{6,0},{7,1},{8,10},{9,11},{10,... | collective-permute-start | bytes 196616 | tf_op jit(solution)/shard_map/ppermute | solution.py:21
  392.2 5.6 %collective-permute-start.21 = (f32[2,32,512]{2,1,0:T(8,128)S(1)}, f32[2,32,512]{2,1,0:T(8,128)S(1)}, u32[]{:S(2)}, u32[]{:S(2)}) collective-permute-start(f32[2,32,512]{2,1,0:T(8,128)S(1)} %collective-permute-done.18), channel_id=1, source_target_pairs={{0,6},{1,7},{2,0},{3,1},{4,2},{5,3},{6,4},{7,5},{8,14},{9,15},{10,... | collective-permute-start | bytes 393224 | tf_op jit(solution)/shard_map/ppermute | solution.py:21
  392.5 5.4 %collective-permute-start.20 = (f32[2,32,512]{2,1,0:T(8,128)S(1)}, f32[2,32,512]{2,1,0:T(8,128)S(1)}, u32[]{:S(2)}, u32[]{:S(2)}) collective-permute-start(f32[2,32,512]{2,1,0:T(8,128)S(1)} %collective-permute-done.18), channel_id=1, source_target_pairs={{0,4},{1,5},{2,6},{3,7},{4,0},{5,1},{6,2},{7,3},{8,12},{9,13},{10,... | collective-permute-start | bytes 393224 | tf_op jit(solution)/shard_map/ppermute | solution.py:21
  393.3 7.0 %collective-permute-start.19 = (f32[2,32,512]{2,1,0:T(8,128)S(1)}, f32[2,32,512]{2,1,0:T(8,128)S(1)}, u32[]{:S(2)}, u32[]{:S(2)}) collective-permute-start(f32[2,32,512]{2,1,0:T(8,128)S(1)} %collective-permute-done.18), channel_id=1, source_target_pairs={{0,2},{1,3},{2,4},{3,5},{4,6},{5,7},{6,0},{7,1},{8,10},{9,11},{10,... | collective-permute-start | bytes 393224 | tf_op jit(solution)/shard_map/ppermute | solution.py:21
  394.8 8.7 %copy-start.6 = (f32[2,256,256]{2,1,0:T(8,128)S(1)}, f32[2,256,256]{2,1,0:T(8,128)}, u32[]{:S(2)}) copy-start(f32[2,256,256]{2,1,0:T(8,128)} %param.14) | copy-start | bytes 1572868
  395.4 10.1 %collective-permute-start.17 = (f32[2,128,256]{2,1,0:T(8,128)S(1)}, f32[2,128,256]{2,1,0:T(8,128)}, u32[]{:S(2)}, u32[]{:S(2)}) collective-permute-start(f32[2,128,256]{2,1,0:T(8,128)S(1)} %bitcast.90), channel_id=1, source_target_pairs={{0,1},{1,0},{2,3},{3,2},{4,5},{5,4},{6,7},{7,6},{8,9},{9,8},{10,11... | collective-permute-start | bytes 786440 | tf_op jit(solution)/shard_map/ppermute | solution.py:57
  400.3 4.2 %copy-start.10 = (f32[2,256,256]{2,1,0:T(8,128)S(1)}, f32[2,256,256]{2,1,0:T(8,128)}, u32[]{:S(2)}) copy-start(f32[2,256,256]{2,1,0:T(8,128)} %copy-done.9) | copy-start | bytes 1572868
  401.0 6.4 %collective-permute-start.22 = (f32[2,128,512]{2,1,0:T(8,128)S(1)}, f32[2,128,512]{2,1,0:T(8,128)S(1)}, u32[]{:S(2)}, u32[]{:S(2)}) collective-permute-start(f32[2,128,512]{2,1,0:T(8,128)S(1)} %bitcast.83), channel_id=1, source_target_pairs={{0,1},{1,0},{2,3},{3,2},{4,5},{5,4},{6,7},{7,6},{8,9},{9,8},{10,11... | collective-permute-start | bytes 1572872 | tf_op jit(solution)/shard_map/ppermute | solution.py:57
  407.5 1.5 copy-start.5

commit v11 on v8

--- a/solution.py
+++ b/solution.py
@@ -207,18 +207,21 @@
     piece = B // row_count
     up_own = lax.dynamic_slice_in_dim(parent_block2, row_here * piece, piece, axis=1)
     up_own = product("kij,kjc->kic", up_own, diag_inv2)
-    payload = shifted(jnp.concatenate([factor2_own, up_own], axis=1), "own", -1)
+    factor2_child = shifted(factor2_own, "own", -1)
+    up_child = shifted(up_own, "own", -1)
 
     outgoing = select_send(sigma_anc, row_blocks, slots)
-    payload, outgoing = lax.optimization_barrier((payload, outgoing))
+    factor2_child, up_child, outgoing = lax.optimization_barrier(
+        (factor2_child, up_child, outgoing)
+    )
     received = lax.all_to_all(outgoing, "own", split_axis=0, concat_axis=0, tiled=True)
 
     keep1 = mask1.astype(jnp.float32)
     factor1 = keep1[:, :, None] * product("kij,kjc->kic", panel1, diag_inv1)
-    factor2 = keep1[:, :, None] * payload[:, :B]
+    factor2 = keep1[:, :, None] * factor2_child
     both = jnp.concatenate([factor1, factor2], axis=-1)
     boths = row_gather(both)
-    up_parent = row_gather(payload[:, B:])
+    up_parent = row_gather(up_child)
     up_parent = up_parent.transpose(1, 0, 2, 3).reshape(slots, B, B)
 
     blocks1 = select_take(received, row_blocks, slots, cols_here)

time: 286 us -> 284 us (level)
    ppermute x3 -> x4, waiting for transfers between devices: 9.88 us -> 7.93 us  [shifted(): lax.ppermute(shard, axis, [(i, (i + by) % length) for i in range(length)])]
    ppermute x3 -> x4, starting transfers between devices: 8.76 us -> 9.57 us  [shifted(): lax.ppermute(shard, axis, [(i, (i + by) % length) for i in range(length)])]
  transfers between devices with their start and end apart: 24 -> 25, of which waited for: 13 -> 13; matrix products, arithmetic and copies ran while one was open for 12% -> 13% of each run, Pallas kernels for 2% -> 2%
where the time goes in v11:
time: 284 us
  waiting for transfers between devices  171 us (60%)
  starting transfers between devices  44.5 us (16%)
  matrix products  22.7 us (8%)
  other arithmetic  21.3 us (8%)
  local copies, waits for them, and re-layouts  11.7 us (4%)
  Pallas kernels  11.3 us (4%)
    ppermute x15, waiting for transfers between devices, _towards(): lax.ppermute(value, 'row', [(i, (i + 2 * by) % length) for i in range(len...  108 us
    all_to_all x1, waiting for transfers between devices, on_device(): lax.all_to_all(outgoing, 'own', split_axis=0, concat_axis=0, tiled=True)  50.2 us
    dot_general x13, matrix products, product(): return jnp.einsum(form, left, right, precision=HIGH)  22.7 us
    ppermute x15, starting transfers between devices, _towards(): lax.ppermute(value, 'row', [(i, (i + 2 * by) % length) for i in range(len...  14.7 us
    ppermute x4, starting transfers between devices, shifted(): lax.ppermute(shard, axis, [(i, (i + by) % length) for i in range(length)])  9.57 us
    gather x2, local copies, waits for them, and re-layouts, row_gather(): return stacked[order].reshape((length,) + x.shape)  8.28 us
    ppermute x4, waiting for transfers between devices, shifted(): lax.ppermute(shard, axis, [(i, (i + by) % length) for i in range(length)])  7.93 us
    all_to_all x1, starting transfers between devices, on_device(): lax.all_to_all(outgoing, 'own', split_axis=0, concat_axis=0, tiled=True)  7.32 us
  transfers between devices with their start and end apart: 25, of which 13 were waited for; matrix products, arithmetic and copies ran while one was open for 13% of the time, Pallas kernels for 2%

profile of v11, /device:TPU:1, one launch (start us, length us, event | category | flops | bytes accessed | tf_op | source)
XLA Modules:
  0.0 284.0 jit_solution(8560249679986122539)
XLA Ops:
  0.7 0.7 convert_bitcast_fusion
  1.7 1.7 convolution_multiply_fusion.1
  3.4 8.7 %collective-permute-start = (f32[2,256,256]{2,1,0:T(8,128)S(1)}, f32[2,256,256]{2,1,0:T(8,128)S(1)}, u32[]{:S(2)}, u32[]{:S(2)}) collective-permute-start(f32[2,256,256]{2,1,0:T(8,128)S(1)} %convolution_multiply_fusion.1), channel_id=1, source_target_pairs={{0,248},{8,0},{16,8},{24,16},{32,24},{40,32},{48,40},{56,48},{64,5... | collective-permute-start | bytes 1572872 | tf_op jit(solution)/shard_map/ppermute | solution.py:16
  12.1 1.2 fusion.10
  13.3 0.8 collective-permute-start.1
  14.6 0.7 gather_fusion.1
  15.3 0.7 clamp_reduce_fusion
  16.0 6.4 %shard_map.128 = f32[32,256,256]{2,1,0:T(8,128)} custom-call(s32[32]{0:T(128)} %get-tuple-element.16.rows_ref, s32[32]{0:T(128)} %get-tuple-element.15.cols_ref, f32[2048,512]{1,0:T(8,128)} %src_ref.1), custom_call_target="tpu_custom_call" | custom-call | bytes 12582912 | tf_op jit(solution)/shard_map/pallas_call | solution.py:121
  22.4 1.6 collective-permute-done.1
  24.1 7.3 %all-to-all-start = ((f32[32,256,256]{2,1,0:T(8,128)}), f32[32,256,256]{2,1,0:T(8,128)}, u32[]{:S(2)}, u32[]{:S(2)}) async-start(f32[32,256,256]{2,1,0:T(8,128)} %shard_map.128), calls=%async_computation | async-start | bytes 16777216 | tf_op jit(solution)/shard_map/all_to_all | solution.py:217
  31.4 0.7 convolution_multiply_fusion
  32.2 1.7 fusion.23
  33.9 1.8 collective-permute-start.2
  35.8 2.6 collective-permute-done.2
  38.4 3.2 %maximum_select_fusion.1 = f32[2,2,256,512]{3,2,1,0:T(8,128)} fusion(f32[1,2,256,512]{3,2,1,0:T(8,128)} %bitcast.10, f32[1,2,256,512]{3,2,1,0:T(8,128)S(1)} %get-tuple-element.18, pred[]{:T(512)S(6)} %eq.23), kind=kLoop, calls=%fused_computation.10 | loop fusion | flops 1572864 | bytes 4194305 | tf_op jit(solution)/shard_map/jit(_where)/select_n | solution.py:70
  41.6 2.7 collective-permute-start.5
  44.4 0.3 collective-permute-start.4
  44.7 0.7 collective-permute-start.3
  45.4 1.2 collective-permute-start.6
  46.6 0.6 gather_fusion
  47.5 2.1 collective-permute-start.9
  49.6 0.5 fusion.21.which_ref
  50.1 1.5 collective-permute-start.8
  51.6 88.0 %collective-permute-done.9 = f32[2,2,32,256]{3,2,1,0:T(8,128)S(1)} collective-permute-done((f32[2,2,32,256]{3,2,1,0:T(8,128)S(1)}, f32[2,2,32,256]{3,2,1,0:T(8,128)S(1)}, u32[]{:S(2)}, u32[]{:S(2)}) %collective-permute-start.9) | collective-permute-done | bytes 131104 | tf_op jit(solution)/shard_map/ppermute | solution.py:21
  139.7 0.8 collective-permute-done.8
  140.5 5.6 %collective-permute-done.7 = f32[2,2,32,256]{3,2,1,0:T(8,128)S(1)} collective-permute-done((f32[2,2,32,256]{3,2,1,0:T(8,128)S(1)}, f32[2,2,32,256]{3,2,1,0:T(8,128)S(1)}, u32[]{:S(2)}, u32[]{:S(2)}) %collective-permute-start.7) | collective-permute-done | bytes 131104 | tf_op jit(solution)/shard_map/ppermute | solution.py:21
  146.2 0.6 gather_fusion.3
  146.8 2.8 %maximum_select_fusion = f32[1,2,2,256,512]{4,3,2,1,0:T(8,128)S(1)} fusion(f32[1,1,2,256,512]{4,3,2,1,0:T(8,128)} %bitcast.8, f32[1,1,2,256,512]{4,3,2,1,0:T(8,128)} %get-tuple-element.17, pred[]{:T(512)S(6)} %eq.23), kind=kLoop, calls=%fused_computation.9 | loop fusion | flops 1572864 | bytes 4194305 | tf_op jit(solution)/shard_map/jit(_where)/select_n | solution.py:70
  149.7 5.8 %pad_maximum_fusion = f32[4,2,2,256,512]{4,3,2,1,0:T(8,128)} fusion(f32[1,2,2,256,512]{4,3,2,1,0:T(8,128)} %bitcast.13, f32[1,2,2,256,512]{4,3,2,1,0:T(8,128)} %bitcast.12, f32[1,2,2,256,512]{4,3,2,1,0:T(8,128)} %bitcast.11, f32[1,2,2,256,512]{4,3,2,1,0:T(8,128)S(1)} %maximum_select_fusion), kind=kLoop, calls=%fused_computation.6 | loop fusion | flops 6291456 | bytes 16777216 | tf_op jit(solution)/shard_map/stack | solution.py:71
  155.5 7.7 %gather_fusion.2 = f32[4,2,2,256,512]{4,3,2,1,0:T(8,128)} fusion(f32[4,2,2,256,512]{4,3,2,1,0:T(8,128)} %pad_maximum_fusion, s32[1024]{0:T(1024)S(1)} %pad_clamp_fusion), kind=kCustom, calls=%fused_computation.2 | custom fusion | bytes 16777232 | tf_op jit(solution)/shard_map/gather | solution.py:73
  163.2 50.2 %all-to-all-done.src_ref = f32[32,256,256]{2,1,0:T(8,128)} async-done(((f32[32,256,256]{2,1,0:T(8,128)}), f32[32,256,256]{2,1,0:T(8,128)}, u32[]{:S(2)}, u32[]{:S(2)}) %all-to-all-start) | async-done | bytes 8388640 | tf_op jit(solution)/shard_map/all_to_all | solution.py:217
  213.4 4.9 %shard_map.129 = f32[16,256,256]{2,1,0:T(8,128)} custom-call(s32[16]{0:T(128)} %fusion.21.which_ref, f32[32,256,256]{2,1,0:T(8,128)} %all-to-all-done.src_ref), custom_call_target="tpu_custom_call" | custom-call | bytes 8388608 | tf_op jit(solution)/shard_map/pallas_call | solution.py:187
  218.4 10.2 %fusion.5 = f32[2,256,512]{2,1,0:T(8,128)S(1)} fusion(f32[2,8,256,256]{3,2,1,0:T(8,128)} %bitcast.78, f32[8,2,256,512]{3,2,1,0:T(8,128)} %bitcast.77, f32[2]{0:T(128)S(1)} %convert_bitcast_fusion.1), kind=kOutput, calls=%fused_computation.13 | convolution fusion | flops 6442713088 | bytes 13631496 | tf_op jit(solution)/shard_map/kmij,mkjc->kic/dot_general | solution.py:87
  228.7 1.0 fusion.26
  229.8 1.0 fusion.25
  230.8 0.7 fusion.9
  231.5 1.0 fusion.27
  232.7 1.0 slice_select_fusion
  233.7 5.6 %collective-permute-start.11 = (f32[2,128,768]{2,1,0:T(8,128)}, f32[2,128,768]{2,1,0:T(8,128)}, u32[]{:S(2)}, u32[]{:S(2)}) collective-permute-start(f32[2,128,768]{2,1,0:T(8,128)} %slice_select_fusion), channel_id=1, source_target_pairs={{0,1},{1,0},{2,3},{3,2},{4,5},{5,4},{6,7},{7,6},{8,9},{9,8},{10,11... | collective-permute-start | bytes 2359304 | tf_op jit(solution)/shard_map/ppermute | solution.py:34
  239.3 2.3 collective-permute-done.11
  241.5 1.3 select_add_fusion
  242.9 2.8 collective-permute-start.14
  245.7 0.3 collective-permute-start.13
  246.0 0.7 collective-permute-start.12
  246.7 1.1 fusion.24
  247.8 5.9 %collective-permute-done.14 = f32[2,32,768]{2,1,0:T(8,128)S(1)} collective-permute-done((f32[2,32,768]{2,1,0:T(8,128)S(1)}, f32[2,32,768]{2,1,0:T(8,128)S(1)}, u32[]{:S(2)}, u32[]{:S(2)}) %collective-permute-start.14) | collective-permute-done | bytes 196640 | tf_op jit(solution)/shard_map/ppermute | solution.py:21
  253.7 4.6 %collective-permute-done.12 = f32[2,32,768]{2,1,0:T(8,128)S(1)} collective-permute-done((f32[2,32,768]{2,1,0:T(8,128)S(1)}, f32[2,32,768]{2,1,0:T(8,128)S(1)}, u32[]{:S(2)}, u32[]{:S(2)}) %collective-permute-start.12) | collective-permute-done | bytes 196640 | tf_op jit(solution)/shard_map/ppermute | solution.py:21
  258.3 0.4 add_negate_fusion
  258.9 1.0 collective-permute-start.17
  259.8 0.3 collective-permute-start.16
  260.2 0.7 collective-permute-start.15
  260.9 6.3 %collective-permute-done.19 = f32[2,32,512]{2,1,0:T(8,128)S(1)} collective-permute-done((f32[2,32,512]{2,1,0:T(8,128)S(1)}, f32[2,32,512]{2,1,0:T(8,128)S(1)}, u32[]{:S(2)}, u32[]{:S(2)}) %collective-permute-start.19) | collective-permute-done | bytes 131104 | tf_op jit(solution)/shard_map/ppermute | solution.py:16
  267.5 0.3 collective-permute-start.21
  267.8 0.8 collective-permute-start.20
  268.7 1.1 fusion.28
  269.8 0.6 gather_fusion.4
  270.4 2.3 collective-permute-start.18
  272.9 2.9 %collective-permute-done.20 = f32[2,32,512]{2,1,0:T(8,128)S(1)} collective-permute-done((f32[2,32,512]{2,1,0:T(8,128)S(1)}, f32[2,32,512]{2,1,0:T(8,128)S(1)}, u32[]{:S(2)}, u32[]{:S(2)}) %collective-permute-start.20) | collective-permute-done | bytes 131104 | tf_op jit(solution)/shard_map/ppermute | solution.py:21
  275.9 0.6 gather_fusion.5
  276.5 2.0 collective-permute-start.23
  278.5 1.0 fusion.29
  279.5 0.9 broadcast_multiply_fusion.1
  280.4 1.9 maximum_select_fusion.3
  282.5 1.5 fusion.8
  (71 shorter events, 2.6 us)
Async XLA Ops:
  0.6 1.1 copy-start
  0.6 13.5 %copy-start.10 = (s32[64,8]{0,1:T(8,128)S(1)}, s32[64,8]{0,1:T(8,128)}, u32[]{:S(2)}) copy-start(s32[64,8]{0,1:T(8,128)} %param.10) | copy-start | bytes 6148
  3.4 20.7 %collective-permute-start = (f32[2,256,256]{2,1,0:T(8,128)S(1)}, f32[2,256,256]{2,1,0:T(8,128)S(1)}, u32[]{:S(2)}, u32[]{:S(2)}) collective-permute-start(f32[2,256,256]{2,1,0:T(8,128)S(1)} %convolution_multiply_fusion.1), channel_id=1, source_target_pairs={{0,248},{8,0},{16,8},{24,16},{32,24},{40,32},{48,40},{56,48},{64,5... | collective-permute-start | bytes 1572872 | tf_op jit(solution)/shard_map/ppermute | solution.py:16
  13.3 10.7 %collective-permute-start.1 = (f32[2,32,256]{2,1,0:T(8,128)S(1)}, f32[2,32,256]{2,1,0:T(8,128)S(1)}, u32[]{:S(2)}, u32[]{:S(2)}) collective-permute-start(f32[2,32,256]{2,1,0:T(8,128)S(1)} %fusion.10), channel_id=1, source_target_pairs={{0,248},{8,0},{16,8},{24,16},{32,24},{40,32},{48,40},{56,48},{64,5... | collective-permute-start | bytes 196616 | tf_op jit(solution)/shard_map/ppermute | solution.py:16
  22.4 9.0 %copy-start.11 = (s32[2,1]{0,1:T(1,128)S(1)}, s32[2,1]{0,1:T(1,128)}, u32[]{:S(2)}) copy-start(s32[2,1]{0,1:T(1,128)} %param.13) | copy-start | bytes 28
  22.4 9.0 %copy-start.2 = (f32[2,256,256]{2,1,0:T(8,128)S(1)}, f32[2,256,256]{2,1,0:T(8,128)}, u32[]{:S(2)}) copy-start(f32[2,256,256]{2,1,0:T(8,128)} %param.12) | copy-start | bytes 1572868
  22.4 9.0 %copy-start.7 = (f32[2,256,256]{2,1,0:T(8,128)S(1)}, f32[2,256,256]{2,1,0:T(8,128)}, u32[]{:S(2)}) copy-start(f32[2,256,256]{2,1,0:T(8,128)} %param.11) | copy-start | bytes 1572868
  24.1 189.4 %all-to-all-start = ((f32[32,256,256]{2,1,0:T(8,128)}), f32[32,256,256]{2,1,0:T(8,128)}, u32[]{:S(2)}, u32[]{:S(2)}) async-start(f32[32,256,256]{2,1,0:T(8,128)} %shard_map.128), calls=%async_computation | async-start | bytes 16777216 | tf_op jit(solution)/shard_map/all_to_all | solution.py:217
  33.9 4.5 %collective-permute-start.2 = (f32[2,256,512]{2,1,0:T(8,128)}, f32[2,256,512]{2,1,0:T(8,128)}, u32[]{:S(2)}, u32[]{:S(2)}) collective-permute-start(f32[2,256,512]{2,1,0:T(8,128)} %get-tuple-element.19), channel_id=1, source_target_pairs={{0,1},{1,0},{2,3},{3,2},{4,5},{5,4},{6,7},{7,6},{8,9},{9,8},{10,11... | collective-permute-start | bytes 3145736 | tf_op jit(solution)/shard_map/ppermute | solution.py:69
  41.6 108.1 %collective-permute-start.5 = (f32[2,2,256,512]{3,2,1,0:T(8,128)}, f32[2,2,256,512]{3,2,1,0:T(8,128)}, u32[]{:S(2)}, u32[]{:S(2)}) collective-permute-start(f32[2,2,256,512]{3,2,1,0:T(8,128)} %maximum_select_fusion.1), channel_id=1, source_target_pairs={{0,6},{1,7},{2,0},{3,1},{4,2},{5,3},{6,4},{7,5},{8,14},{9,15},{10,... | collective-permute-start | bytes 6291464 | tf_op jit(solution)/shard_map/ppermute | solution.py:21
  44.4 105.3 %collective-permute-start.4 = (f32[2,2,256,512]{3,2,1,0:T(8,128)}, f32[2,2,256,512]{3,2,1,0:T(8,128)}, u32[]{:S(2)}, u32[]{:S(2)}) collective-permute-start(f32[2,2,256,512]{3,2,1,0:T(8,128)} %maximum_select_fusion.1), channel_id=1, source_target_pairs={{0,4},{1,5},{2,6},{3,7},{4,0},{5,1},{6,2},{7,3},{8,12},{9,13},{10,... | collective-permute-start | bytes 6291464 | tf_op jit(solution)/shard_map/ppermute | solution.py:21
  44.7 105.0 %collective-permute-start.3 = (f32[2,2,256,512]{3,2,1,0:T(8,128)}, f32[2,2,256,512]{3,2,1,0:T(8,128)}, u32[]{:S(2)}, u32[]{:S(2)}) collective-permute-start(f32[2,2,256,512]{3,2,1,0:T(8,128)} %maximum_select_fusion.1), channel_id=1, source_target_pairs={{0,2},{1,3},{2,4},{3,5},{4,6},{5,7},{6,0},{7,1},{8,10},{9,11},{10,... | collective-permute-start | bytes 6291464 | tf_op jit(solution)/shard_map/ppermute | solution.py:21
  45.4 2.1 collective-permute-start.6
  47.5 92.1 %collective-permute-start.9 = (f32[2,2,32,256]{3,2,1,0:T(8,128)S(1)}, f32[2,2,32,256]{3,2,1,0:T(8,128)S(1)}, u32[]{:S(2)}, u32[]{:S(2)}) collective-permute-start(f32[2,2,32,256]{3,2,1,0:T(8,128)S(1)} %maximum_select_fusion.5), channel_id=1, source_target_pairs={{0,6},{1,7},{2,0},{3,1},{4,2},{5,3},{6,4},{7,5},{8,14},{9,15},{10,... | collective-permute-start | bytes 393224 | tf_op jit(solution)/shard_map/ppermute | solution.py:21
  50.1 90.4 %collective-permute-start.8 = (f32[2,2,32,256]{3,2,1,0:T(8,128)S(1)}, f32[2,2,32,256]{3,2,1,0:T(8,128)S(1)}, u32[]{:S(2)}, u32[]{:S(2)}) collective-permute-start(f32[2,2,32,256]{3,2,1,0:T(8,128)S(1)} %maximum_select_fusion.5), channel_id=1, source_target_pairs={{0,4},{1,5},{2,6},{3,7},{4,0},{5,1},{6,2},{7,3},{8,12},{9,13},{10,... | collective-permute-start | bytes 393224 | tf_op jit(solution)/shard_map/ppermute | solution.py:21
  139.6 6.5 %collective-permute-start.7 = (f32[2,2,32,256]{3,2,1,0:T(8,128)S(1)}, f32[2,2,32,256]{3,2,1,0:T(8,128)S(1)}, u32[]{:S(2)}, u32[]{:S(2)}) collective-permute-start(f32[2,2,32,256]{3,2,1,0:T(8,128)S(1)} %maximum_select_fusion.5), channel_id=1, source_target_pairs={{0,2},{1,3},{2,4},{3,5},{4,6},{5,7},{6,0},{7,1},{8,10},{9,11},{10,... | collective-permute-start | bytes 393224 | tf_op jit(solution)/shard_map/ppermute | solution.py:21
  146.8 84.0 %copy-start.3 = (f32[2,8,32,256]{3,2,1,0:T(8,128)}, f32[2,8,32,256]{3,2,1,0:T(8,128)S(1)}, u32[]{:S(2)}) copy-start(f32[2,8,32,256]{3,2,1,0:T(8,128)S(1)} %copy.82) | copy-start | bytes 1572868
  228.7 2.8 copy-start.1
  233.7 7.8 %collective-permute-start.11 = (f32[2,128,768]{2,1,0:T(8,128)}, f32[2,128,768]{2,1,0:T(8,128)}, u32[]{:S(2)}, u32[]{:S(2)}) collective-permute-start(f32[2,128,768]{2,1,0:T(8,128)} %slice_select_fusion), channel_id=1, source_target_pairs={{0,1},{1,0},{2,3},{3,2},{4,5},{5,4},{6,7},{7,6},{8,9},{9,8},{10,11... | collective-permute-start | bytes 2359304 | tf_op jit(solution)/shard_map/ppermute | solution.py:34
  239.3 19.0 %collective-permute-start.10 = (f32[2,256,256]{2,1,0:T(8,128)S(1)}, f32[2,256,256]{2,1,0:T(8,128)S(1)}, u32[]{:S(2)}, u32[]{:S(2)}) collective-permute-start(f32[2,256,256]{2,1,0:T(8,128)S(1)} %fusion.9), channel_id=1, source_target_pairs={{0,8},{8,16},{16,24},{24,32},{32,40},{40,48},{48,56},{56,64},{64,7... | collective-permute-start | bytes 1572872 | tf_op jit(solution)/shard_map/ppermute | solution.py:16
  242.8 15.5 %copy-start.4 = (f32[2,8,32,256]{3,2,1,0:T(8,128)S(1)}, f32[2,8,32,256]{3,2,1,0:T(8,128)}, u32[]{:S(2)}) copy-start(f32[2,8,32,256]{3,2,1,0:T(8,128)} %copy-done.3) | copy-start | bytes 1572868
  242.9 10.8 %collective-permute-start.14 = (f32[2,32,768]{2,1,0:T(8,128)S(1)}, f32[2,32,768]{2,1,0:T(8,128)S(1)}, u32[]{:S(2)}, u32[]{:S(2)}) collective-permute-start(f32[2,32,768]{2,1,0:T(8,128)S(1)} %get-tuple-element.21), channel_id=1, source_target_pairs={{0,6},{1,7},{2,0},{3,1},{4,2},{5,3},{6,4},{7,5},{8,14},{9,15},{10,... | collective-permute-start | bytes 589832 | tf_op jit(solution)/shard_map/ppermute | solution.py:21
  245.7 8.0 %collective-permute-start.13 = (f32[2,32,768]{2,1,0:T(8,128)S(1)}, f32[2,32,768]{2,1,0:T(8,128)S(1)}, u32[]{:S(2)}, u32[]{:S(2)}) collective-permute-start(f32[2,32,768]{2,1,0:T(8,128)S(1)} %get-tuple-element.22), channel_id=1, source_target_pairs={{0,4},{1,5},{2,6},{3,7},{4,0},{5,1},{6,2},{7,3},{8,12},{9,13},{10,... | collective-permute-start | bytes 589832 | tf_op jit(solution)/shard_map/ppermute | solution.py:21
  246.0 12.2 %collective-permute-start.12 = (f32[2,32,768]{2,1,0:T(8,128)S(1)}, f32[2,32,768]{2,1,0:T(8,128)S(1)}, u32[]{:S(2)}, u32[]{:S(2)}) collective-permute-start(f32[2,32,768]{2,1,0:T(8,128)S(1)} %get-tuple-element.20), channel_id=1, source_target_pairs={{0,2},{1,3},{2,4},{3,5},{4,6},{5,7},{6,0},{7,1},{8,10},{9,11},{10,... | collective-permute-start | bytes 589832 | tf_op jit(solution)/shard_map/ppermute | solution.py:21
  258.3 11.5 %copy-start.8 = (f32[2,256,256]{2,1,0:T(8,128)}, f32[2,256,256]{2,1,0:T(8,128)S(1)}, u32[]{:S(2)}) copy-start(f32[2,256,256]{2,1,0:T(8,128)S(1)} %collective-permute-done.10) | copy-start | bytes 1572868
  258.8 8.4 %collective-permute-start.19 = (f32[2,32,512]{2,1,0:T(8,128)S(1)}, f32[2,32,512]{2,1,0:T(8,128)S(1)}, u32[]{:S(2)}, u32[]{:S(2)}) collective-permute-start(f32[2,32,512]{2,1,0:T(8,128)S(1)} %pad_maximum_fusion.6), channel_id=1, source_target_pairs={{0,8},{8,16},{16,24},{24,32},{32,40},{40,48},{48,56},{56,64},{64,7... | collective-permute-start | bytes 393224 | tf_op jit(solution)/shard_map/ppermute | solution.py:16
  258.9 9.0 %collective-permute-start.17 = (f32[2,32,256]{2,1,0:T(8,128)S(1)}, f32[2,32,256]{2,1,0:T(8,128)S(1)}, u32[]{:S(2)}, u32[]{:S(2)}) collective-permute-start(f32[2,32,256]{2,1,0:T(8,128)S(1)} %slice_subtract_fusion), channel_id=1, source_target_pairs={{0,6},{1,7},{2,0},{3,1},{4,2},{5,3},{6,4},{7,5},{8,14},{9,15},{10,... | collective-permute-start | bytes 196616 | tf_op jit(solution)/shard_map/ppermute | solution.py:21
  259.8 9.9 %collective-permute-start.16 = (f32[2,32,256]{2,1,0:T(8,128)S(1)}, f32[2,32,256]{2,1,0:T(8,128)S(1)}, u32[]{:S(2)}, u32[]{:S(2)}) collective-permute-start(f32[2,32,256]{2,1,0:T(8,128)S(1)} %slice_subtract_fusion), channel_id=1, source_target_pairs={{0,4},{1,5},{2,6},{3,7},{4,0},{5,1},{6,2},{7,3},{8,12},{9,13},{10,... | collective-permute-start | bytes 196616 | tf_op jit(solution)/shard_map/ppermute | solution.py:21
  260.2 9.5 %collective-permute-start.15 = (f32[2,32,256]{2,1,0:T(8,128)S(1)}, f32[2,32,256]{2,1,0:T(8,128)S(1)}, u32[]{:S(2)}, u32[]{:S(2)}) collective-permute-start(f32[2,32,256]{2,1,0:T(8,128)S(1)} %slice_subtract_fusion), channel_id=1, source_target_pairs={{0,2},{1,3},{2,4},{3,5},{4,6},{5,7},{6,0},{7,1},{8,10},{9,11},{10,... | collective-permute-start | bytes 196616 | tf_op jit(solution)/shard_map/ppermute | solution.py:21
  267.2 5.5 %collective-permute-start.22 = (f32[2,32,512]{2,1,0:T(8,128)S(1)}, f32[2,32,512]{2,1,0:T(8,128)S(1)}, u32[]{:S(2)}, u32[]{:S(2)}) collective-permute-start(f32[2,32,512]{2,1,0:T(8,128)S(1)} %collective-permute-done.19), channel_id=1, source_target_pairs={{0,6},{1,7},{2,0},{3,1},{4,2},{5,3},{6,4},{7,5},{8,14},{9,15},{10,... | collective-permute-start | bytes 393224 | tf_op jit(solution)/shard_map/ppermute | solution.py:21
  267.5 5.4 %collective-permute-start.21 = (f32[2,32,512]{2,1,0:T(8,128)S(1)}, f32[2,32,512]{2,1,0:T(8,128)S(1)}, u32[]{:S(2)}, u32[]{:S(2)}) collective-permute-start(f32[2,32,512]{2,1,0:T(8,128)S(1)} %collective-permute-done.19), channel_id=1, source_target_pairs={{0,4},{1,5},{2,6},{3,7},{4,0},{5,1},{6,2},{7,3},{8,12},{9,13},{10,... | collective-permute-start | bytes 393224 | tf_op jit(solution)/shard_map/ppermute | solution.py:21
  267.8 8.0 %collective-permute-start.20 = (f32[2,32,512]{2,1,0:T(8,128)S(1)}, f32[2,32,512]{2,1,0:T(8,128)S(1)}, u32[]{:S(2)}, u32[]{:S(2)}) collective-permute-start(f32[2,32,512]{2,1,0:T(8,128)S(1)} %collective-permute-done.19), channel_id=1, source_target_pairs={{0,2},{1,3},{2,4},{3,5},{4,6},{5,7},{6,0},{7,1},{8,10},{9,11},{10,... | collective-permute-start | bytes 393224 | tf_op jit(solution)/shard_map/ppermute | solution.py:21
  269.8 8.7 %copy-start.6 = (f32[2,256,256]{2,1,0:T(8,128)S(1)}, f32[2,256,256]{2,1,0:T(8,128)}, u32[]{:S(2)}) copy-start(f32[2,256,256]{2,1,0:T(8,128)} %param.14) | copy-start | bytes 1572868
  270.4 10.0 %collective-permute-start.18 = (f32[2,128,256]{2,1,0:T(8,128)S(1)}, f32[2,128,256]{2,1,0:T(8,128)}, u32[]{:S(2)}, u32[]{:S(2)}) collective-permute-start(f32[2,128,256]{2,1,0:T(8,128)S(1)} %bitcast.88), channel_id=1, source_target_pairs={{0,1},{1,0},{2,3},{3,2},{4,5},{5,4},{6,7},{7,6},{8,9},{9,8},{10,11... | collective-permute-start | bytes 786440 | tf_op jit(solution)/shard_map/ppermute | solution.py:57
  275.8 3.7 %copy-start.9 = (f32[2,256,256]{2,1,0:T(8,128)S(1)}, f32[2,256,256]{2,1,0:T(8,128)}, u32[]{:S(2)}) copy-start(f32[2,256,256]{2,1,0:T(8,128)} %copy-done.8) | copy-start | bytes 1572868
  276.5 5.8 %collective-permute-start.23 = (f32[2,128,512]{2,1,0:T(8,128)S(1)}, f32[2,128,512]{2,1,0:T(8,128)S(1)}, u32[]{:S(2)}, u32[]{:S(2)}) collective-permute-start(f32[2,128,512]{2,1,0:T(8,128)S(1)} %bitcast.81), channel_id=1, source_target_pairs={{0,1},{1,0},{2,3},{3,2},{4,5},{5,4},{6,7},{7,6},{8,9},{9,8},{10,11... | collective-permute-start | bytes 1572872 | tf_op jit(solution)/shard_map/ppermute | solution.py:57
  282.5 1.5 copy-start.5

commit v12 on v8

--- a/solution.py
+++ b/solution.py
@@ -203,11 +203,12 @@
     row_count = lax.axis_size("row")
     row_here = lax.axis_index("row")
     keep_own2 = mask2.astype(jnp.float32)
-    factor2_own = keep_own2[:, :, None] * product("kij,kjc->kic", panel2, diag_inv2)
     piece = B // row_count
-    up_own = lax.dynamic_slice_in_dim(parent_block2, row_here * piece, piece, axis=1)
-    up_own = product("kij,kjc->kic", up_own, diag_inv2)
-    payload = shifted(jnp.concatenate([factor2_own, up_own], axis=1), "own", -1)
+    diag2_own = lax.dynamic_slice_in_dim(diag_inv2, row_here * piece, piece, axis=1)
+    top2_own = lax.dynamic_slice_in_dim(parent_block2, row_here * piece, piece, axis=1)
+    payload = shifted(
+        jnp.concatenate([keep_own2[:, :, None] * panel2, diag2_own, top2_own], axis=1), "own", -1
+    )
 
     outgoing = select_send(sigma_anc, row_blocks, slots)
     payload, outgoing = lax.optimization_barrier((payload, outgoing))
@@ -215,10 +216,13 @@
 
     keep1 = mask1.astype(jnp.float32)
     factor1 = keep1[:, :, None] * product("kij,kjc->kic", panel1, diag_inv1)
-    factor2 = keep1[:, :, None] * payload[:, :B]
+    diag2_child = row_gather(payload[:, B : B + piece])
+    diag2_child = diag2_child.transpose(1, 0, 2, 3).reshape(slots, B, B)
+    factor2 = keep1[:, :, None] * product("kij,kjc->kic", payload[:, :B], diag2_child)
+    up_rows = product("kij,kjc->kic", payload[:, B + piece :], diag2_child)
     both = jnp.concatenate([factor1, factor2], axis=-1)
     boths = row_gather(both)
-    up_parent = row_gather(payload[:, B:])
+    up_parent = row_gather(up_rows)
     up_parent = up_parent.transpose(1, 0, 2, 3).reshape(slots, B, B)
 
     blocks1 = select_take(received, row_blocks, slots, cols_here)

time: 286 us -> 285 us (level)
    all_to_all x1, waiting for transfers between devices: 50.5 us -> 40.5 us  [on_device(): lax.all_to_all(outgoing, 'own', split_axis=0, concat_axis=0, tiled=True)]
    ppermute x15 -> x18, waiting for transfers between devices: 106 us -> 113 us  [_towards(): lax.ppermute(value, 'row', [(i, (i + 2 * by) % length) for i in range(len...]
    select_n x4 -> x6, other arithmetic: 6.1 us -> 3.46 us  [row_gather(): pair = jnp.where(core == 0, jnp.stack([x, got]), jnp.stack([got, x]))]
    ppermute x15 -> x18, starting transfers between devices: 14.5 us -> 16.4 us  [_towards(): lax.ppermute(value, 'row', [(i, (i + 2 * by) % length) for i in range(len...]
    gather x2 -> x3, local copies, waits for them, and re-layouts: 8.28 us -> 9.65 us  [row_gather(): return stacked[order].reshape((length,) + x.shape)]
    another operation x2 -> x3, other arithmetic: 5.83 us -> 5.59 us  [row_gather(): stacked = jnp.stack([pair] + [_towards(pair, by) for by in range(1, chips)])]
  transfers between devices with their start and end apart: 24 -> 28, of which waited for: 13 -> 17; matrix products, arithmetic and copies ran while one was open for 12% -> 13% of each run, Pallas kernels for 2% -> 2%
where the time goes in v12:
time: 285 us; the launch traced here: 284 us
  waiting for transfers between devices  171 us (60%)
  starting transfers between devices  45.7 us (16%)
  matrix products  21.6 us (8%)
  other arithmetic  19 us (7%)
  local copies, waits for them, and re-layouts  14.7 us (5%)
  Pallas kernels  11.3 us (4%)
    ppermute x18, waiting for transfers between devices, _towards(): lax.ppermute(value, 'row', [(i, (i + 2 * by) % length) for i in range(len...  113 us
    all_to_all x1, waiting for transfers between devices, on_device(): lax.all_to_all(outgoing, 'own', split_axis=0, concat_axis=0, tiled=True)  40.5 us
    dot_general x13, matrix products, product(): return jnp.einsum(form, left, right, precision=HIGH)  21.6 us
    ppermute x18, starting transfers between devices, _towards(): lax.ppermute(value, 'row', [(i, (i + 2 * by) % length) for i in range(len...  16.4 us
    ppermute x3, waiting for transfers between devices, shifted(): lax.ppermute(shard, axis, [(i, (i + by) % length) for i in range(length)])  11.3 us
    gather x3, local copies, waits for them, and re-layouts, row_gather(): return stacked[order].reshape((length,) + x.shape)  9.65 us
    ppermute x3, starting transfers between devices, shifted(): lax.ppermute(shard, axis, [(i, (i + by) % length) for i in range(length)])  8.76 us
    all_to_all x1, starting transfers between devices, on_device(): lax.all_to_all(outgoing, 'own', split_axis=0, concat_axis=0, tiled=True)  7.32 us
  transfers between devices with their start and end apart: 28, of which 17 were waited for; matrix products, arithmetic and copies ran while one was open for 13% of the time, Pallas kernels for 2%

profile of v12, /device:TPU:1, one launch (start us, length us, event | category | flops | bytes accessed | tf_op | source)
XLA Modules:
  0.0 284.3 jit_solution(11537077566695551806)
XLA Ops:
  0.7 0.7 convert_bitcast_fusion
  1.4 1.1 broadcast_multiply_fusion.1
  2.5 0.9 constant_dynamic-slice_fusion.4
  3.5 8.7 %collective-permute-start = (f32[2,320,256]{2,1,0:T(8,128)S(1)}, f32[2,320,256]{2,1,0:T(8,128)S(1)}, u32[]{:S(2)}, u32[]{:S(2)}) collective-permute-start(f32[2,320,256]{2,1,0:T(8,128)S(1)} %pad_maximum_fusion.3), channel_id=1, source_target_pairs={{0,248},{8,0},{16,8},{24,16},{32,24},{40,32},{48,40},{56,48},{64,5... | collective-permute-start | bytes 1966088 | tf_op jit(solution)/shard_map/ppermute | solution.py:16
  12.7 0.7 gather_fusion.1
  13.3 0.7 clamp_reduce_fusion
  14.1 6.4 %shard_map.128 = f32[32,256,256]{2,1,0:T(8,128)} custom-call(s32[32]{0:T(128)} %get-tuple-element.14.rows_ref, s32[32]{0:T(128)} %get-tuple-element.13.cols_ref, f32[2048,512]{1,0:T(8,128)} %src_ref.1), custom_call_target="tpu_custom_call" | custom-call | bytes 12582912 | tf_op jit(solution)/shard_map/pallas_call | solution.py:121
  20.5 5.1 %collective-permute-done = f32[2,320,256]{2,1,0:T(8,128)S(1)} collective-permute-done((f32[2,320,256]{2,1,0:T(8,128)S(1)}, f32[2,320,256]{2,1,0:T(8,128)S(1)}, u32[]{:S(2)}, u32[]{:S(2)}) %collective-permute-start) | collective-permute-done | bytes 655392 | tf_op jit(solution)/shard_map/ppermute | solution.py:16
  25.6 7.3 %all-to-all-start = ((f32[32,256,256]{2,1,0:T(8,128)}), f32[32,256,256]{2,1,0:T(8,128)}, u32[]{:S(2)}, u32[]{:S(2)}) async-start(f32[32,256,256]{2,1,0:T(8,128)} %shard_map.128), calls=%async_computation | async-start | bytes 16777216 | tf_op jit(solution)/shard_map/all_to_all | solution.py:215
  32.9 1.0 convolution_multiply_fusion.1
  34.0 1.9 collective-permute-start.1
  35.9 0.9 collective-permute-done.1
  36.8 2.8 collective-permute-start.4
  40.0 0.7 collective-permute-start.2
  40.7 4.1 %collective-permute-done.4 = f32[2,2,32,256]{3,2,1,0:T(8,128)S(1)} collective-permute-done((f32[2,2,32,256]{3,2,1,0:T(8,128)S(1)}, f32[2,2,32,256]{3,2,1,0:T(8,128)S(1)}, u32[]{:S(2)}, u32[]{:S(2)}) %collective-permute-start.4) | collective-permute-done | bytes 131104 | tf_op jit(solution)/shard_map/ppermute | solution.py:21
  44.8 0.8 collective-permute-done.3
  45.7 3.8 %collective-permute-done.2 = f32[2,2,32,256]{3,2,1,0:T(8,128)S(1)} collective-permute-done((f32[2,2,32,256]{3,2,1,0:T(8,128)S(1)}, f32[2,2,32,256]{3,2,1,0:T(8,128)S(1)}, u32[]{:S(2)}, u32[]{:S(2)}) %collective-permute-start.2) | collective-permute-done | bytes 131104 | tf_op jit(solution)/shard_map/ppermute | solution.py:21
  50.2 1.1 convolution_multiply_fusion
  51.2 1.2 fusion.23
  52.8 2.3 collective-permute-done.5
  55.1 1.6 maximum_select_fusion.1
  57.3 0.8 collective-permute-start.6
  58.2 1.2 fusion.11
  59.4 1.0 collective-permute-start.9
  60.4 0.9 collective-permute-done.9
  61.4 2.4 collective-permute-start.12
  64.5 1.5 collective-permute-start.11
  66.0 85.7 %collective-permute-done.12 = f32[2,2,32,256]{3,2,1,0:T(8,128)S(1)} collective-permute-done((f32[2,2,32,256]{3,2,1,0:T(8,128)S(1)}, f32[2,2,32,256]{3,2,1,0:T(8,128)S(1)}, u32[]{:S(2)}, u32[]{:S(2)}) %collective-permute-start.12) | collective-permute-done | bytes 131104 | tf_op jit(solution)/shard_map/ppermute | solution.py:21
  152.2 0.9 collective-permute-done.11
  153.1 4.0 %collective-permute-done.10 = f32[2,2,32,256]{3,2,1,0:T(8,128)S(1)} collective-permute-done((f32[2,2,32,256]{3,2,1,0:T(8,128)S(1)}, f32[2,2,32,256]{3,2,1,0:T(8,128)S(1)}, u32[]{:S(2)}, u32[]{:S(2)}) %collective-permute-start.10) | collective-permute-done | bytes 131104 | tf_op jit(solution)/shard_map/ppermute | solution.py:21
  157.1 1.4 gather_fusion.4
  158.5 1.1 copy.89
  159.6 1.9 maximum_select_fusion
  161.5 5.5 %pad_maximum_fusion = f32[4,2,2,256,512]{3,4,2,1,0:T(8,128)} fusion(f32[1,2,2,256,512]{3,4,2,1,0:T(8,128)} %bitcast.24, f32[1,2,2,256,512]{3,4,2,1,0:T(8,128)} %bitcast.23, f32[1,2,2,256,512]{3,4,2,1,0:T(8,128)} %bitcast.22, f32[1,2,2,256,512]{3,4,2,1,0:T(8,128)S(1)} %maximum_select_fusion), kind=kLoop, calls=%fused_computation.7 | loop fusion | flops 6291456 | bytes 16777216 | tf_op jit(solution)/shard_map/stack | solution.py:71
  167.0 7.7 %gather_fusion.3 = f32[4,2,2,256,512]{3,4,2,1,0:T(8,128)} fusion(f32[4,2,2,256,512]{3,4,2,1,0:T(8,128)} %pad_maximum_fusion, s32[1024]{0:T(1024)S(1)} %pad_clamp_fusion), kind=kCustom, calls=%fused_computation.3 | custom fusion | bytes 16777232 | tf_op jit(solution)/shard_map/gather | solution.py:73
  174.7 40.5 %all-to-all-done.src_ref = f32[32,256,256]{2,1,0:T(8,128)} async-done(((f32[32,256,256]{2,1,0:T(8,128)}), f32[32,256,256]{2,1,0:T(8,128)}, u32[]{:S(2)}, u32[]{:S(2)}) %all-to-all-start) | async-done | bytes 8388640 | tf_op jit(solution)/shard_map/all_to_all | solution.py:215
  215.2 4.9 %shard_map.129 = f32[16,256,256]{2,1,0:T(8,128)} custom-call(s32[16]{0:T(128)} %fusion.21.which_ref, f32[32,256,256]{2,1,0:T(8,128)} %all-to-all-done.src_ref), custom_call_target="tpu_custom_call" | custom-call | bytes 8388608 | tf_op jit(solution)/shard_map/pallas_call | solution.py:187
  220.1 10.3 %fusion.5 = f32[2,256,512]{2,1,0:T(8,128)S(1)} fusion(f32[2,8,256,256]{3,2,1,0:T(8,128)} %bitcast.90, f32[8,2,256,512]{2,3,1,0:T(8,128)} %bitcast.89, f32[2]{0:T(128)S(1)} %convert_bitcast_fusion.1), kind=kOutput, calls=%fused_computation.14 | convolution fusion | flops 6442713088 | bytes 13631496 | tf_op jit(solution)/shard_map/kmij,mkjc->kic/dot_general | solution.py:87
  230.5 1.0 fusion.26
  231.5 0.7 fusion.25
  232.2 0.7 fusion.9
  232.9 0.7 fusion.27
  233.6 1.0 slice_select_fusion
  234.6 5.3 %collective-permute-start.14 = (f32[2,128,768]{2,1,0:T(8,128)}, f32[2,128,768]{2,1,0:T(8,128)}, u32[]{:S(2)}, u32[]{:S(2)}) collective-permute-start(f32[2,128,768]{2,1,0:T(8,128)} %slice_select_fusion), channel_id=1, source_target_pairs={{0,1},{1,0},{2,3},{3,2},{4,5},{5,4},{6,7},{7,6},{8,9},{9,8},{10,11... | collective-permute-start | bytes 2359304 | tf_op jit(solution)/shard_map/ppermute | solution.py:34
  239.9 2.3 collective-permute-done.14
  242.2 1.3 select_add_fusion
  243.5 2.8 collective-permute-start.17
  246.7 0.7 collective-permute-start.15
  247.4 1.1 fusion.24
  248.4 5.9 %collective-permute-done.17 = f32[2,32,768]{2,1,0:T(8,128)S(1)} collective-permute-done((f32[2,32,768]{2,1,0:T(8,128)S(1)}, f32[2,32,768]{2,1,0:T(8,128)S(1)}, u32[]{:S(2)}, u32[]{:S(2)}) %collective-permute-start.17) | collective-permute-done | bytes 196640 | tf_op jit(solution)/shard_map/ppermute | solution.py:21
  254.3 4.6 %collective-permute-done.15 = f32[2,32,768]{2,1,0:T(8,128)S(1)} collective-permute-done((f32[2,32,768]{2,1,0:T(8,128)S(1)}, f32[2,32,768]{2,1,0:T(8,128)S(1)}, u32[]{:S(2)}, u32[]{:S(2)}) %collective-permute-start.15) | collective-permute-done | bytes 196640 | tf_op jit(solution)/shard_map/ppermute | solution.py:21
  259.5 0.8 collective-permute-start.20
  260.6 0.7 collective-permute-start.18
  261.3 6.2 %collective-permute-done.22 = f32[2,32,512]{2,1,0:T(8,128)S(1)} collective-permute-done((f32[2,32,512]{2,1,0:T(8,128)S(1)}, f32[2,32,512]{2,1,0:T(8,128)S(1)}, u32[]{:S(2)}, u32[]{:S(2)}) %collective-permute-start.22) | collective-permute-done | bytes 131104 | tf_op jit(solution)/shard_map/ppermute | solution.py:16
  268.1 0.8 collective-permute-start.23
  269.0 1.1 fusion.28
  270.7 2.4 collective-permute-start.21
  273.2 2.7 collective-permute-done.23
  275.9 0.6 gather_fusion.6
  276.6 2.2 collective-permute-start.26
  278.8 1.0 fusion.29
  279.9 0.9 broadcast_multiply_fusion
  280.8 1.9 maximum_select_fusion.3
  282.8 1.5 fusion.8
  (83 shorter events, 7.1 us)
Async XLA Ops:
  0.6 32.3 %copy-start = (f32[2,256,256]{2,1,0:T(8,128)S(1)}, f32[2,256,256]{2,1,0:T(8,128)}, u32[]{:S(2)}) copy-start(f32[2,256,256]{2,1,0:T(8,128)} %param.12) | copy-start | bytes 1572868
  0.6 11.5 %copy-start.9 = (s32[64,8]{0,1:T(8,128)S(1)}, s32[64,8]{0,1:T(8,128)}, u32[]{:S(2)}) copy-start(s32[64,8]{0,1:T(8,128)} %param.10) | copy-start | bytes 6148
  3.5 22.1 %collective-permute-start = (f32[2,320,256]{2,1,0:T(8,128)S(1)}, f32[2,320,256]{2,1,0:T(8,128)S(1)}, u32[]{:S(2)}, u32[]{:S(2)}) collective-permute-start(f32[2,320,256]{2,1,0:T(8,128)S(1)} %pad_maximum_fusion.3), channel_id=1, source_target_pairs={{0,248},{8,0},{16,8},{24,16},{32,24},{40,32},{48,40},{56,48},{64,5... | collective-permute-start | bytes 1966088 | tf_op jit(solution)/shard_map/ppermute | solution.py:16
  20.5 12.4 %copy-start.10 = (s32[2,1]{0,1:T(1,128)S(1)}, s32[2,1]{0,1:T(1,128)}, u32[]{:S(2)}) copy-start(s32[2,1]{0,1:T(1,128)} %param.13) | copy-start | bytes 28
  20.5 12.5 %copy-start.6 = (f32[2,256,256]{2,1,0:T(8,128)S(1)}, f32[2,256,256]{2,1,0:T(8,128)}, u32[]{:S(2)}) copy-start(f32[2,256,256]{2,1,0:T(8,128)} %param.11) | copy-start | bytes 1572868
  25.6 24.6 %copy-start.5 = (f32[2,320,256]{2,1,0:T(8,128)}, f32[2,320,256]{2,1,0:T(8,128)S(1)}, u32[]{:S(2)}) copy-start(f32[2,320,256]{2,1,0:T(8,128)S(1)} %collective-permute-done) | copy-start | bytes 1966084
  25.6 189.6 %all-to-all-start = ((f32[32,256,256]{2,1,0:T(8,128)}), f32[32,256,256]{2,1,0:T(8,128)}, u32[]{:S(2)}, u32[]{:S(2)}) async-start(f32[32,256,256]{2,1,0:T(8,128)} %shard_map.128), calls=%async_computation | async-start | bytes 16777216 | tf_op jit(solution)/shard_map/all_to_all | solution.py:215
  34.0 2.8 collective-permute-start.1
  36.8 8.0 %collective-permute-start.4 = (f32[2,2,32,256]{3,2,1,0:T(8,128)S(1)}, f32[2,2,32,256]{3,2,1,0:T(8,128)S(1)}, u32[]{:S(2)}, u32[]{:S(2)}) collective-permute-start(f32[2,2,32,256]{3,2,1,0:T(8,128)S(1)} %maximum_select_fusion.5), channel_id=1, source_target_pairs={{0,6},{1,7},{2,0},{3,1},{4,2},{5,3},{6,4},{7,5},{8,14},{9,15},{10,... | collective-permute-start | bytes 393224 | tf_op jit(solution)/shard_map/ppermute | solution.py:21
  39.6 6.0 %collective-permute-start.3 = (f32[2,2,32,256]{3,2,1,0:T(8,128)S(1)}, f32[2,2,32,256]{3,2,1,0:T(8,128)S(1)}, u32[]{:S(2)}, u32[]{:S(2)}) collective-permute-start(f32[2,2,32,256]{3,2,1,0:T(8,128)S(1)} %maximum_select_fusion.5), channel_id=1, source_target_pairs={{0,4},{1,5},{2,6},{3,7},{4,0},{5,1},{6,2},{7,3},{8,12},{9,13},{10,... | collective-permute-start | bytes 393224 | tf_op jit(solution)/shard_map/ppermute | solution.py:21
  40.0 9.5 %collective-permute-start.2 = (f32[2,2,32,256]{3,2,1,0:T(8,128)S(1)}, f32[2,2,32,256]{3,2,1,0:T(8,128)S(1)}, u32[]{:S(2)}, u32[]{:S(2)}) collective-permute-start(f32[2,2,32,256]{3,2,1,0:T(8,128)S(1)} %maximum_select_fusion.5), channel_id=1, source_target_pairs={{0,2},{1,3},{2,4},{3,5},{4,6},{5,7},{6,0},{7,1},{8,10},{9,11},{10,... | collective-permute-start | bytes 393224 | tf_op jit(solution)/shard_map/ppermute | solution.py:21
  52.5 2.7 collective-permute-start.5
  56.7 104.8 %collective-permute-start.8 = (f32[2,2,256,512]{2,3,1,0:T(8,128)}, f32[2,2,256,512]{2,3,1,0:T(8,128)}, u32[]{:S(2)}, u32[]{:S(2)}) collective-permute-start(f32[2,2,256,512]{2,3,1,0:T(8,128)} %maximum_select_fusion.1), channel_id=1, source_target_pairs={{0,6},{1,7},{2,0},{3,1},{4,2},{5,3},{6,4},{7,5},{8,14},{9,15},{10,... | collective-permute-start | bytes 6291464 | tf_op jit(solution)/shard_map/ppermute | solution.py:21
  57.0 104.5 %collective-permute-start.7 = (f32[2,2,256,512]{2,3,1,0:T(8,128)}, f32[2,2,256,512]{2,3,1,0:T(8,128)}, u32[]{:S(2)}, u32[]{:S(2)}) collective-permute-start(f32[2,2,256,512]{2,3,1,0:T(8,128)} %maximum_select_fusion.1), channel_id=1, source_target_pairs={{0,4},{1,5},{2,6},{3,7},{4,0},{5,1},{6,2},{7,3},{8,12},{9,13},{10,... | collective-permute-start | bytes 6291464 | tf_op jit(solution)/shard_map/ppermute | solution.py:21
  57.3 104.1 %collective-permute-start.6 = (f32[2,2,256,512]{2,3,1,0:T(8,128)}, f32[2,2,256,512]{2,3,1,0:T(8,128)}, u32[]{:S(2)}, u32[]{:S(2)}) collective-permute-start(f32[2,2,256,512]{2,3,1,0:T(8,128)} %maximum_select_fusion.1), channel_id=1, source_target_pairs={{0,2},{1,3},{2,4},{3,5},{4,6},{5,7},{6,0},{7,1},{8,10},{9,11},{10,... | collective-permute-start | bytes 6291464 | tf_op jit(solution)/shard_map/ppermute | solution.py:21
  59.4 1.9 collective-permute-start.9
  61.4 90.3 %collective-permute-start.12 = (f32[2,2,32,256]{3,2,1,0:T(8,128)S(1)}, f32[2,2,32,256]{3,2,1,0:T(8,128)S(1)}, u32[]{:S(2)}, u32[]{:S(2)}) collective-permute-start(f32[2,2,32,256]{3,2,1,0:T(8,128)S(1)} %maximum_select_fusion.7), channel_id=1, source_target_pairs={{0,6},{1,7},{2,0},{3,1},{4,2},{5,3},{6,4},{7,5},{8,14},{9,15},{10,... | collective-permute-start | bytes 393224 | tf_op jit(solution)/shard_map/ppermute | solution.py:21
  64.5 88.6 %collective-permute-start.11 = (f32[2,2,32,256]{3,2,1,0:T(8,128)S(1)}, f32[2,2,32,256]{3,2,1,0:T(8,128)S(1)}, u32[]{:S(2)}, u32[]{:S(2)}) collective-permute-start(f32[2,2,32,256]{3,2,1,0:T(8,128)S(1)} %maximum_select_fusion.7), channel_id=1, source_target_pairs={{0,4},{1,5},{2,6},{3,7},{4,0},{5,1},{6,2},{7,3},{8,12},{9,13},{10,... | collective-permute-start | bytes 393224 | tf_op jit(solution)/shard_map/ppermute | solution.py:21
  151.6 5.4 %collective-permute-start.10 = (f32[2,2,32,256]{3,2,1,0:T(8,128)S(1)}, f32[2,2,32,256]{3,2,1,0:T(8,128)S(1)}, u32[]{:S(2)}, u32[]{:S(2)}) collective-permute-start(f32[2,2,32,256]{3,2,1,0:T(8,128)S(1)} %maximum_select_fusion.7), channel_id=1, source_target_pairs={{0,2},{1,3},{2,4},{3,5},{4,6},{5,7},{6,0},{7,1},{8,10},{9,11},{10,... | collective-permute-start | bytes 393224 | tf_op jit(solution)/shard_map/ppermute | solution.py:21
  230.5 2.4 copy-start.1
  234.6 7.5 %collective-permute-start.14 = (f32[2,128,768]{2,1,0:T(8,128)}, f32[2,128,768]{2,1,0:T(8,128)}, u32[]{:S(2)}, u32[]{:S(2)}) collective-permute-start(f32[2,128,768]{2,1,0:T(8,128)} %slice_select_fusion), channel_id=1, source_target_pairs={{0,1},{1,0},{2,3},{3,2},{4,5},{5,4},{6,7},{7,6},{8,9},{9,8},{10,11... | collective-permute-start | bytes 2359304 | tf_op jit(solution)/shard_map/ppermute | solution.py:34
  239.9 19.0 %collective-permute-start.13 = (f32[2,256,256]{2,1,0:T(8,128)S(1)}, f32[2,256,256]{2,1,0:T(8,128)S(1)}, u32[]{:S(2)}, u32[]{:S(2)}) collective-permute-start(f32[2,256,256]{2,1,0:T(8,128)S(1)} %fusion.9), channel_id=1, source_target_pairs={{0,8},{8,16},{16,24},{24,32},{32,40},{40,48},{48,56},{56,64},{64,7... | collective-permute-start | bytes 1572872 | tf_op jit(solution)/shard_map/ppermute | solution.py:16
  243.5 25.5 %copy-start.2 = (f32[2,256,256]{2,1,0:T(8,128)S(1)}, f32[2,256,256]{2,1,0:T(8,128)}, u32[]{:S(2)}) copy-start(f32[2,256,256]{2,1,0:T(8,128)} %param.16) | copy-start | bytes 1572868
  243.5 10.8 %collective-permute-start.17 = (f32[2,32,768]{2,1,0:T(8,128)S(1)}, f32[2,32,768]{2,1,0:T(8,128)S(1)}, u32[]{:S(2)}, u32[]{:S(2)}) collective-permute-start(f32[2,32,768]{2,1,0:T(8,128)S(1)} %get-tuple-element.19), channel_id=1, source_target_pairs={{0,6},{1,7},{2,0},{3,1},{4,2},{5,3},{6,4},{7,5},{8,14},{9,15},{10,... | collective-permute-start | bytes 589832 | tf_op jit(solution)/shard_map/ppermute | solution.py:21
  246.3 8.0 %collective-permute-start.16 = (f32[2,32,768]{2,1,0:T(8,128)S(1)}, f32[2,32,768]{2,1,0:T(8,128)S(1)}, u32[]{:S(2)}, u32[]{:S(2)}) collective-permute-start(f32[2,32,768]{2,1,0:T(8,128)S(1)} %get-tuple-element.20), channel_id=1, source_target_pairs={{0,4},{1,5},{2,6},{3,7},{4,0},{5,1},{6,2},{7,3},{8,12},{9,13},{10,... | collective-permute-start | bytes 589832 | tf_op jit(solution)/shard_map/ppermute | solution.py:21
  246.7 12.2 %collective-permute-start.15 = (f32[2,32,768]{2,1,0:T(8,128)S(1)}, f32[2,32,768]{2,1,0:T(8,128)S(1)}, u32[]{:S(2)}, u32[]{:S(2)}) collective-permute-start(f32[2,32,768]{2,1,0:T(8,128)S(1)} %get-tuple-element.18), channel_id=1, source_target_pairs={{0,2},{1,3},{2,4},{3,5},{4,6},{5,7},{6,0},{7,1},{8,10},{9,11},{10,... | collective-permute-start | bytes 589832 | tf_op jit(solution)/shard_map/ppermute | solution.py:21
  258.9 11.1 %copy-start.7 = (f32[2,256,256]{2,1,0:T(8,128)}, f32[2,256,256]{2,1,0:T(8,128)S(1)}, u32[]{:S(2)}) copy-start(f32[2,256,256]{2,1,0:T(8,128)S(1)} %collective-permute-done.13) | copy-start | bytes 1572868
  259.4 8.1 %collective-permute-start.22 = (f32[2,32,512]{2,1,0:T(8,128)S(1)}, f32[2,32,512]{2,1,0:T(8,128)S(1)}, u32[]{:S(2)}, u32[]{:S(2)}) collective-permute-start(f32[2,32,512]{2,1,0:T(8,128)S(1)} %pad_maximum_fusion.8), channel_id=1, source_target_pairs={{0,8},{8,16},{16,24},{24,32},{32,40},{40,48},{48,56},{56,64},{64,7... | collective-permute-start | bytes 393224 | tf_op jit(solution)/shard_map/ppermute | solution.py:16
  259.5 8.7 %collective-permute-start.20 = (f32[2,32,256]{2,1,0:T(8,128)S(1)}, f32[2,32,256]{2,1,0:T(8,128)S(1)}, u32[]{:S(2)}, u32[]{:S(2)}) collective-permute-start(f32[2,32,256]{2,1,0:T(8,128)S(1)} %slice_subtract_fusion), channel_id=1, source_target_pairs={{0,6},{1,7},{2,0},{3,1},{4,2},{5,3},{6,4},{7,5},{8,14},{9,15},{10,... | collective-permute-start | bytes 196616 | tf_op jit(solution)/shard_map/ppermute | solution.py:21
  260.2 9.8 %collective-permute-start.19 = (f32[2,32,256]{2,1,0:T(8,128)S(1)}, f32[2,32,256]{2,1,0:T(8,128)S(1)}, u32[]{:S(2)}, u32[]{:S(2)}) collective-permute-start(f32[2,32,256]{2,1,0:T(8,128)S(1)} %slice_subtract_fusion), channel_id=1, source_target_pairs={{0,4},{1,5},{2,6},{3,7},{4,0},{5,1},{6,2},{7,3},{8,12},{9,13},{10,... | collective-permute-start | bytes 196616 | tf_op jit(solution)/shard_map/ppermute | solution.py:21
  260.6 9.4 %collective-permute-start.18 = (f32[2,32,256]{2,1,0:T(8,128)S(1)}, f32[2,32,256]{2,1,0:T(8,128)S(1)}, u32[]{:S(2)}, u32[]{:S(2)}) collective-permute-start(f32[2,32,256]{2,1,0:T(8,128)S(1)} %slice_subtract_fusion), channel_id=1, source_target_pairs={{0,2},{1,3},{2,4},{3,5},{4,6},{5,7},{6,0},{7,1},{8,10},{9,11},{10,... | collective-permute-start | bytes 196616 | tf_op jit(solution)/shard_map/ppermute | solution.py:21
  267.5 5.6 %collective-permute-start.25 = (f32[2,32,512]{2,1,0:T(8,128)S(1)}, f32[2,32,512]{2,1,0:T(8,128)S(1)}, u32[]{:S(2)}, u32[]{:S(2)}) collective-permute-start(f32[2,32,512]{2,1,0:T(8,128)S(1)} %collective-permute-done.22), channel_id=1, source_target_pairs={{0,6},{1,7},{2,0},{3,1},{4,2},{5,3},{6,4},{7,5},{8,14},{9,15},{10,... | collective-permute-start | bytes 393224 | tf_op jit(solution)/shard_map/ppermute | solution.py:21
  267.8 5.4 %collective-permute-start.24 = (f32[2,32,512]{2,1,0:T(8,128)S(1)}, f32[2,32,512]{2,1,0:T(8,128)S(1)}, u32[]{:S(2)}, u32[]{:S(2)}) collective-permute-start(f32[2,32,512]{2,1,0:T(8,128)S(1)} %collective-permute-done.22), channel_id=1, source_target_pairs={{0,4},{1,5},{2,6},{3,7},{4,0},{5,1},{6,2},{7,3},{8,12},{9,13},{10,... | collective-permute-start | bytes 393224 | tf_op jit(solution)/shard_map/ppermute | solution.py:21
  268.1 7.7 %collective-permute-start.23 = (f32[2,32,512]{2,1,0:T(8,128)S(1)}, f32[2,32,512]{2,1,0:T(8,128)S(1)}, u32[]{:S(2)}, u32[]{:S(2)}) collective-permute-start(f32[2,32,512]{2,1,0:T(8,128)S(1)} %collective-permute-done.22), channel_id=1, source_target_pairs={{0,2},{1,3},{2,4},{3,5},{4,6},{5,7},{6,0},{7,1},{8,10},{9,11},{10,... | collective-permute-start | bytes 393224 | tf_op jit(solution)/shard_map/ppermute | solution.py:21
  270.1 8.7 %copy-start.4 = (f32[2,256,256]{2,1,0:T(8,128)S(1)}, f32[2,256,256]{2,1,0:T(8,128)}, u32[]{:S(2)}) copy-start(f32[2,256,256]{2,1,0:T(8,128)} %param.14) | copy-start | bytes 1572868
  270.7 10.1 %collective-permute-start.21 = (f32[2,128,256]{2,1,0:T(8,128)S(1)}, f32[2,128,256]{2,1,0:T(8,128)}, u32[]{:S(2)}, u32[]{:S(2)}) collective-permute-start(f32[2,128,256]{2,1,0:T(8,128)S(1)} %bitcast.105), channel_id=1, source_target_pairs={{0,1},{1,0},{2,3},{3,2},{4,5},{5,4},{6,7},{7,6},{8,9},{9,8},{10,11... | collective-permute-start | bytes 786440 | tf_op jit(solution)/shard_map/ppermute | solution.py:57
  276.5 3.3 %copy-start.8 = (f32[2,256,256]{2,1,0:T(8,128)S(1)}, f32[2,256,256]{2,1,0:T(8,128)}, u32[]{:S(2)}) copy-start(f32[2,256,256]{2,1,0:T(8,128)} %copy-done.7) | copy-start | bytes 1572868
  276.6 6.1 %collective-permute-start.26 = (f32[2,128,512]{2,1,0:T(8,128)S(1)}, f32[2,128,512]{2,1,0:T(8,128)S(1)}, u32[]{:S(2)}, u32[]{:S(2)}) collective-permute-start(f32[2,128,512]{2,1,0:T(8,128)S(1)} %bitcast.97), channel_id=1, source_target_pairs={{0,1},{1,0},{2,3},{3,2},{4,5},{5,4},{6,7},{7,6},{8,9},{9,8},{10,11... | collective-permute-start | bytes 1572872 | tf_op jit(solution)/shard_map/ppermute | solution.py:57
  282.8 1.5 copy-start.3

commit v13 on v11

--- a/solution.py
+++ b/solution.py
@@ -55,9 +55,10 @@
         piece.shape[0], chips * piece.shape[1], piece.shape[2]
     )
     got = lax.ppermute(part, "row", [(i, i ^ 1) for i in range(length)])
-    return jnp.where(
-        core == 0, jnp.concatenate([part, got], axis=1), jnp.concatenate([got, part], axis=1)
-    )
+    half = part.shape[1]
+    full = jnp.zeros((part.shape[0], 2 * half, part.shape[2]), part.dtype)
+    full = lax.dynamic_update_slice_in_dim(full, part, core * half, axis=1)
+    return lax.dynamic_update_slice_in_dim(full, got, (1 - core) * half, axis=1)
 
 
 def row_gather(x):

time: 284 us -> 284 us (level)
  transfers between devices with their start and end apart: 25 -> 25, of which waited for: 13 -> 12; matrix products, arithmetic and copies ran while one was open for 13% -> 12% of each run, Pallas kernels for 2% -> 2%
where the time goes in v13:
time: 284 us; the launch traced here: 283 us
  waiting for transfers between devices  170 us (60%)
  starting transfers between devices  45.7 us (16%)
  matrix products  22.6 us (8%)
  other arithmetic  19.4 us (7%)
  local copies, waits for them, and re-layouts  12.9 us (5%)
  Pallas kernels  11.3 us (4%)
    ppermute x15, waiting for transfers between devices, _towards(): lax.ppermute(value, 'row', [(i, (i + 2 * by) % length) for i in range(len...  108 us
    all_to_all x1, waiting for transfers between devices, on_device(): lax.all_to_all(outgoing, 'own', split_axis=0, concat_axis=0, tiled=True)  50.2 us
    dot_general x13, matrix products, product(): return jnp.einsum(form, left, right, precision=HIGH)  22.6 us
    ppermute x15, starting transfers between devices, _towards(): lax.ppermute(value, 'row', [(i, (i + 2 * by) % length) for i in range(len...  16.5 us
    ppermute x4, starting transfers between devices, shifted(): lax.ppermute(shard, axis, [(i, (i + by) % length) for i in range(length)])  9.57 us
    gather x2, local copies, waits for them, and re-layouts, row_gather(): return stacked[order].reshape((length,) + x.shape)  8.28 us
    all_to_all x1, starting transfers between devices, on_device(): lax.all_to_all(outgoing, 'own', split_axis=0, concat_axis=0, tiled=True)  7.32 us
    ppermute x4, waiting for transfers between devices, shifted(): lax.ppermute(shard, axis, [(i, (i + by) % length) for i in range(length)])  6.56 us
  transfers between devices with their start and end apart: 25, of which 12 were waited for; matrix products, arithmetic and copies ran while one was open for 12% of the time, Pallas kernels for 2%

profile of v13, /device:TPU:1, one launch (start us, length us, event | category | flops | bytes accessed | tf_op | source)
XLA Modules:
  0.0 283.2 jit_solution(4033936385526249509)
XLA Ops:
  0.7 0.7 convert_bitcast_fusion
  1.7 1.7 convolution_multiply_fusion.1
  3.4 8.7 %collective-permute-start = (f32[2,256,256]{2,1,0:T(8,128)S(1)}, f32[2,256,256]{2,1,0:T(8,128)S(1)}, u32[]{:S(2)}, u32[]{:S(2)}) collective-permute-start(f32[2,256,256]{2,1,0:T(8,128)S(1)} %convolution_multiply_fusion.1), channel_id=1, source_target_pairs={{0,248},{8,0},{16,8},{24,16},{32,24},{40,32},{48,40},{56,48},{64,5... | collective-permute-start | bytes 1572872 | tf_op jit(solution)/shard_map/ppermute | solution.py:16
  12.1 1.2 fusion.10
  13.3 0.8 collective-permute-start.1
  14.6 0.7 gather_fusion.1
  15.3 0.7 clamp_reduce_fusion
  16.0 6.4 %shard_map.128 = f32[32,256,256]{2,1,0:T(8,128)} custom-call(s32[32]{0:T(128)} %get-tuple-element.16.rows_ref, s32[32]{0:T(128)} %get-tuple-element.15.cols_ref, f32[2048,512]{1,0:T(8,128)} %src_ref.1), custom_call_target="tpu_custom_call" | custom-call | bytes 12582912 | tf_op jit(solution)/shard_map/pallas_call | solution.py:122
  22.4 1.6 collective-permute-done.1
  24.1 7.3 %all-to-all-start = ((f32[32,256,256]{2,1,0:T(8,128)}), f32[32,256,256]{2,1,0:T(8,128)}, u32[]{:S(2)}, u32[]{:S(2)}) async-start(f32[32,256,256]{2,1,0:T(8,128)} %shard_map.128), calls=%async_computation | async-start | bytes 16777216 | tf_op jit(solution)/shard_map/all_to_all | solution.py:218
  31.4 0.7 convolution_multiply_fusion
  32.2 1.8 fusion.23
  34.0 1.8 collective-permute-start.2
  35.8 2.6 collective-permute-done.2
  38.4 3.2 %maximum_select_fusion.1 = f32[2,2,256,512]{3,2,1,0:T(8,128)} fusion(f32[1,2,256,512]{3,2,1,0:T(8,128)} %bitcast.10, f32[1,2,256,512]{3,2,1,0:T(8,128)S(1)} %get-tuple-element.18, pred[]{:T(512)S(6)} %eq.21), kind=kLoop, calls=%fused_computation.10 | loop fusion | flops 1572864 | bytes 4194305 | tf_op jit(solution)/shard_map/jit(_where)/select_n | solution.py:71
  41.7 2.7 collective-permute-start.5
  44.4 0.3 collective-permute-start.4
  44.7 0.7 collective-permute-start.3
  45.4 1.2 collective-permute-start.6
  46.7 0.6 gather_fusion
  47.6 2.1 collective-permute-start.9
  49.6 0.5 fusion.21.which_ref
  50.2 1.5 collective-permute-start.8
  51.7 88.0 %collective-permute-done.9 = f32[2,2,32,256]{3,2,1,0:T(8,128)S(1)} collective-permute-done((f32[2,2,32,256]{3,2,1,0:T(8,128)S(1)}, f32[2,2,32,256]{3,2,1,0:T(8,128)S(1)}, u32[]{:S(2)}, u32[]{:S(2)}) %collective-permute-start.9) | collective-permute-done | bytes 131104 | tf_op jit(solution)/shard_map/ppermute | solution.py:21
  139.7 0.8 collective-permute-done.8
  140.5 5.6 %collective-permute-done.7 = f32[2,2,32,256]{3,2,1,0:T(8,128)S(1)} collective-permute-done((f32[2,2,32,256]{3,2,1,0:T(8,128)S(1)}, f32[2,2,32,256]{3,2,1,0:T(8,128)S(1)}, u32[]{:S(2)}, u32[]{:S(2)}) %collective-permute-start.7) | collective-permute-done | bytes 131104 | tf_op jit(solution)/shard_map/ppermute | solution.py:21
  146.2 0.6 gather_fusion.3
  146.9 2.8 %maximum_select_fusion = f32[1,2,2,256,512]{4,3,2,1,0:T(8,128)S(1)} fusion(f32[1,1,2,256,512]{4,3,2,1,0:T(8,128)} %bitcast.8, f32[1,1,2,256,512]{4,3,2,1,0:T(8,128)} %get-tuple-element.17, pred[]{:T(512)S(6)} %eq.21), kind=kLoop, calls=%fused_computation.9 | loop fusion | flops 1572864 | bytes 4194305 | tf_op jit(solution)/shard_map/jit(_where)/select_n | solution.py:71
  149.7 5.8 %pad_maximum_fusion = f32[4,2,2,256,512]{4,3,2,1,0:T(8,128)} fusion(f32[1,2,2,256,512]{4,3,2,1,0:T(8,128)} %bitcast.13, f32[1,2,2,256,512]{4,3,2,1,0:T(8,128)} %bitcast.12, f32[1,2,2,256,512]{4,3,2,1,0:T(8,128)} %bitcast.11, f32[1,2,2,256,512]{4,3,2,1,0:T(8,128)S(1)} %maximum_select_fusion), kind=kLoop, calls=%fused_computation.6 | loop fusion | flops 6291456 | bytes 16777216 | tf_op jit(solution)/shard_map/stack | solution.py:72
  155.5 7.7 %gather_fusion.2 = f32[4,2,2,256,512]{4,3,2,1,0:T(8,128)} fusion(f32[4,2,2,256,512]{4,3,2,1,0:T(8,128)} %pad_maximum_fusion, s32[1024]{0:T(1024)S(1)} %pad_clamp_fusion), kind=kCustom, calls=%fused_computation.2 | custom fusion | bytes 16777232 | tf_op jit(solution)/shard_map/gather | solution.py:74
  163.2 50.2 %all-to-all-done.src_ref = f32[32,256,256]{2,1,0:T(8,128)} async-done(((f32[32,256,256]{2,1,0:T(8,128)}), f32[32,256,256]{2,1,0:T(8,128)}, u32[]{:S(2)}, u32[]{:S(2)}) %all-to-all-start) | async-done | bytes 8388640 | tf_op jit(solution)/shard_map/all_to_all | solution.py:218
  213.4 4.9 %shard_map.129 = f32[16,256,256]{2,1,0:T(8,128)} custom-call(s32[16]{0:T(128)} %fusion.21.which_ref, f32[32,256,256]{2,1,0:T(8,128)} %all-to-all-done.src_ref), custom_call_target="tpu_custom_call" | custom-call | bytes 8388608 | tf_op jit(solution)/shard_map/pallas_call | solution.py:188
  218.4 10.2 %fusion.5 = f32[2,256,512]{2,1,0:T(8,128)S(1)} fusion(f32[2,8,256,256]{3,2,1,0:T(8,128)} %bitcast.78, f32[8,2,256,512]{3,2,1,0:T(8,128)} %bitcast.77, f32[2]{0:T(128)S(1)} %convert_bitcast_fusion.1), kind=kOutput, calls=%fused_computation.13 | convolution fusion | flops 6442713088 | bytes 13631496 | tf_op jit(solution)/shard_map/kmij,mkjc->kic/dot_general | solution.py:88
  228.7 1.0 fusion.26
  229.8 1.0 fusion.25
  230.8 0.7 fusion.9
  231.5 1.0 fusion.27
  232.7 1.0 slice_select_fusion
  233.7 5.6 %collective-permute-start.11 = (f32[2,128,768]{2,1,0:T(8,128)}, f32[2,128,768]{2,1,0:T(8,128)}, u32[]{:S(2)}, u32[]{:S(2)}) collective-permute-start(f32[2,128,768]{2,1,0:T(8,128)} %slice_select_fusion), channel_id=1, source_target_pairs={{0,1},{1,0},{2,3},{3,2},{4,5},{5,4},{6,7},{7,6},{8,9},{9,8},{10,11... | collective-permute-start | bytes 2359304 | tf_op jit(solution)/shard_map/ppermute | solution.py:34
  239.3 2.3 collective-permute-done.11
  241.5 1.3 select_add_fusion
  242.9 2.8 collective-permute-start.14
  245.7 0.3 collective-permute-start.13
  246.0 0.7 collective-permute-start.12
  246.7 1.1 fusion.24
  247.8 5.9 %collective-permute-done.14 = f32[2,32,768]{2,1,0:T(8,128)S(1)} collective-permute-done((f32[2,32,768]{2,1,0:T(8,128)S(1)}, f32[2,32,768]{2,1,0:T(8,128)S(1)}, u32[]{:S(2)}, u32[]{:S(2)}) %collective-permute-start.14) | collective-permute-done | bytes 196640 | tf_op jit(solution)/shard_map/ppermute | solution.py:21
  253.7 4.6 %collective-permute-done.12 = f32[2,32,768]{2,1,0:T(8,128)S(1)} collective-permute-done((f32[2,32,768]{2,1,0:T(8,128)S(1)}, f32[2,32,768]{2,1,0:T(8,128)S(1)}, u32[]{:S(2)}, u32[]{:S(2)}) %collective-permute-start.12) | collective-permute-done | bytes 196640 | tf_op jit(solution)/shard_map/ppermute | solution.py:21
  258.3 1.0 collective-permute-start.17
  259.3 0.4 add_negate_fusion
  259.8 1.1 fusion.28
  260.9 0.4 collective-permute-start.16
  261.3 0.7 collective-permute-start.15
  262.0 4.9 %collective-permute-done.19 = f32[2,32,512]{2,1,0:T(8,128)S(1)} collective-permute-done((f32[2,32,512]{2,1,0:T(8,128)S(1)}, f32[2,32,512]{2,1,0:T(8,128)S(1)}, u32[]{:S(2)}, u32[]{:S(2)}) %collective-permute-start.19) | collective-permute-done | bytes 131104 | tf_op jit(solution)/shard_map/ppermute | solution.py:16
  266.9 0.5 collective-permute-start.22
  267.4 2.8 collective-permute-start.21
  270.2 1.0 fusion.29
  271.3 0.6 gather_fusion.4
  271.9 2.1 collective-permute-start.18
  274.0 3.2 %collective-permute-done.20 = f32[2,32,512]{2,1,0:T(8,128)S(1)} collective-permute-done((f32[2,32,512]{2,1,0:T(8,128)S(1)}, f32[2,32,512]{2,1,0:T(8,128)S(1)}, u32[]{:S(2)}, u32[]{:S(2)}) %collective-permute-start.20) | collective-permute-done | bytes 131104 | tf_op jit(solution)/shard_map/ppermute | solution.py:21
  277.2 0.6 gather_fusion.5
  277.9 1.6 collective-permute-start.23
  279.5 0.9 broadcast_multiply_fusion.1
  280.6 1.0 constant_dynamic-update-slice_fusion.2
  281.7 1.5 fusion.8
  (77 shorter events, 2.3 us)
Async XLA Ops:
  0.6 1.1 copy-start
  0.6 13.5 %copy-start.11 = (s32[64,8]{0,1:T(8,128)S(1)}, s32[64,8]{0,1:T(8,128)}, u32[]{:S(2)}) copy-start(s32[64,8]{0,1:T(8,128)} %param.10) | copy-start | bytes 6148
  3.4 20.7 %collective-permute-start = (f32[2,256,256]{2,1,0:T(8,128)S(1)}, f32[2,256,256]{2,1,0:T(8,128)S(1)}, u32[]{:S(2)}, u32[]{:S(2)}) collective-permute-start(f32[2,256,256]{2,1,0:T(8,128)S(1)} %convolution_multiply_fusion.1), channel_id=1, source_target_pairs={{0,248},{8,0},{16,8},{24,16},{32,24},{40,32},{48,40},{56,48},{64,5... | collective-permute-start | bytes 1572872 | tf_op jit(solution)/shard_map/ppermute | solution.py:16
  13.3 10.7 %collective-permute-start.1 = (f32[2,32,256]{2,1,0:T(8,128)S(1)}, f32[2,32,256]{2,1,0:T(8,128)S(1)}, u32[]{:S(2)}, u32[]{:S(2)}) collective-permute-start(f32[2,32,256]{2,1,0:T(8,128)S(1)} %fusion.10), channel_id=1, source_target_pairs={{0,248},{8,0},{16,8},{24,16},{32,24},{40,32},{48,40},{56,48},{64,5... | collective-permute-start | bytes 196616 | tf_op jit(solution)/shard_map/ppermute | solution.py:16
  22.4 9.0 %copy-start.12 = (s32[2,1]{0,1:T(1,128)S(1)}, s32[2,1]{0,1:T(1,128)}, u32[]{:S(2)}) copy-start(s32[2,1]{0,1:T(1,128)} %param.13) | copy-start | bytes 28
  22.4 9.0 %copy-start.2 = (f32[2,256,256]{2,1,0:T(8,128)S(1)}, f32[2,256,256]{2,1,0:T(8,128)}, u32[]{:S(2)}) copy-start(f32[2,256,256]{2,1,0:T(8,128)} %param.12) | copy-start | bytes 1572868
  22.4 9.0 %copy-start.8 = (f32[2,256,256]{2,1,0:T(8,128)S(1)}, f32[2,256,256]{2,1,0:T(8,128)}, u32[]{:S(2)}) copy-start(f32[2,256,256]{2,1,0:T(8,128)} %param.11) | copy-start | bytes 1572868
  24.1 189.4 %all-to-all-start = ((f32[32,256,256]{2,1,0:T(8,128)}), f32[32,256,256]{2,1,0:T(8,128)}, u32[]{:S(2)}, u32[]{:S(2)}) async-start(f32[32,256,256]{2,1,0:T(8,128)} %shard_map.128), calls=%async_computation | async-start | bytes 16777216 | tf_op jit(solution)/shard_map/all_to_all | solution.py:218
  34.0 4.5 %collective-permute-start.2 = (f32[2,256,512]{2,1,0:T(8,128)}, f32[2,256,512]{2,1,0:T(8,128)}, u32[]{:S(2)}, u32[]{:S(2)}) collective-permute-start(f32[2,256,512]{2,1,0:T(8,128)} %get-tuple-element.19), channel_id=1, source_target_pairs={{0,1},{1,0},{2,3},{3,2},{4,5},{5,4},{6,7},{7,6},{8,9},{9,8},{10,11... | collective-permute-start | bytes 3145736 | tf_op jit(solution)/shard_map/ppermute | solution.py:70
  41.7 108.1 %collective-permute-start.5 = (f32[2,2,256,512]{3,2,1,0:T(8,128)}, f32[2,2,256,512]{3,2,1,0:T(8,128)}, u32[]{:S(2)}, u32[]{:S(2)}) collective-permute-start(f32[2,2,256,512]{3,2,1,0:T(8,128)} %maximum_select_fusion.1), channel_id=1, source_target_pairs={{0,6},{1,7},{2,0},{3,1},{4,2},{5,3},{6,4},{7,5},{8,14},{9,15},{10,... | collective-permute-start | bytes 6291464 | tf_op jit(solution)/shard_map/ppermute | solution.py:21
  44.4 105.3 %collective-permute-start.4 = (f32[2,2,256,512]{3,2,1,0:T(8,128)}, f32[2,2,256,512]{3,2,1,0:T(8,128)}, u32[]{:S(2)}, u32[]{:S(2)}) collective-permute-start(f32[2,2,256,512]{3,2,1,0:T(8,128)} %maximum_select_fusion.1), channel_id=1, source_target_pairs={{0,4},{1,5},{2,6},{3,7},{4,0},{5,1},{6,2},{7,3},{8,12},{9,13},{10,... | collective-permute-start | bytes 6291464 | tf_op jit(solution)/shard_map/ppermute | solution.py:21
  44.7 105.0 %collective-permute-start.3 = (f32[2,2,256,512]{3,2,1,0:T(8,128)}, f32[2,2,256,512]{3,2,1,0:T(8,128)}, u32[]{:S(2)}, u32[]{:S(2)}) collective-permute-start(f32[2,2,256,512]{3,2,1,0:T(8,128)} %maximum_select_fusion.1), channel_id=1, source_target_pairs={{0,2},{1,3},{2,4},{3,5},{4,6},{5,7},{6,0},{7,1},{8,10},{9,11},{10,... | collective-permute-start | bytes 6291464 | tf_op jit(solution)/shard_map/ppermute | solution.py:21
  45.4 2.1 collective-permute-start.6
  47.6 92.1 %collective-permute-start.9 = (f32[2,2,32,256]{3,2,1,0:T(8,128)S(1)}, f32[2,2,32,256]{3,2,1,0:T(8,128)S(1)}, u32[]{:S(2)}, u32[]{:S(2)}) collective-permute-start(f32[2,2,32,256]{3,2,1,0:T(8,128)S(1)} %maximum_select_fusion.3), channel_id=1, source_target_pairs={{0,6},{1,7},{2,0},{3,1},{4,2},{5,3},{6,4},{7,5},{8,14},{9,15},{10,... | collective-permute-start | bytes 393224 | tf_op jit(solution)/shard_map/ppermute | solution.py:21
  50.2 90.4 %collective-permute-start.8 = (f32[2,2,32,256]{3,2,1,0:T(8,128)S(1)}, f32[2,2,32,256]{3,2,1,0:T(8,128)S(1)}, u32[]{:S(2)}, u32[]{:S(2)}) collective-permute-start(f32[2,2,32,256]{3,2,1,0:T(8,128)S(1)} %maximum_select_fusion.3), channel_id=1, source_target_pairs={{0,4},{1,5},{2,6},{3,7},{4,0},{5,1},{6,2},{7,3},{8,12},{9,13},{10,... | collective-permute-start | bytes 393224 | tf_op jit(solution)/shard_map/ppermute | solution.py:21
  139.7 6.5 %collective-permute-start.7 = (f32[2,2,32,256]{3,2,1,0:T(8,128)S(1)}, f32[2,2,32,256]{3,2,1,0:T(8,128)S(1)}, u32[]{:S(2)}, u32[]{:S(2)}) collective-permute-start(f32[2,2,32,256]{3,2,1,0:T(8,128)S(1)} %maximum_select_fusion.3), channel_id=1, source_target_pairs={{0,2},{1,3},{2,4},{3,5},{4,6},{5,7},{6,0},{7,1},{8,10},{9,11},{10,... | collective-permute-start | bytes 393224 | tf_op jit(solution)/shard_map/ppermute | solution.py:21
  146.8 84.0 %copy-start.3 = (f32[2,8,32,256]{3,2,1,0:T(8,128)}, f32[2,8,32,256]{3,2,1,0:T(8,128)S(1)}, u32[]{:S(2)}) copy-start(f32[2,8,32,256]{3,2,1,0:T(8,128)S(1)} %copy.82) | copy-start | bytes 1572868
  228.7 2.8 copy-start.1
  233.7 7.8 %collective-permute-start.11 = (f32[2,128,768]{2,1,0:T(8,128)}, f32[2,128,768]{2,1,0:T(8,128)}, u32[]{:S(2)}, u32[]{:S(2)}) collective-permute-start(f32[2,128,768]{2,1,0:T(8,128)} %slice_select_fusion), channel_id=1, source_target_pairs={{0,1},{1,0},{2,3},{3,2},{4,5},{5,4},{6,7},{7,6},{8,9},{9,8},{10,11... | collective-permute-start | bytes 2359304 | tf_op jit(solution)/shard_map/ppermute | solution.py:34
  239.3 19.0 %collective-permute-start.10 = (f32[2,256,256]{2,1,0:T(8,128)S(1)}, f32[2,256,256]{2,1,0:T(8,128)S(1)}, u32[]{:S(2)}, u32[]{:S(2)}) collective-permute-start(f32[2,256,256]{2,1,0:T(8,128)S(1)} %fusion.9), channel_id=1, source_target_pairs={{0,8},{8,16},{16,24},{24,32},{32,40},{40,48},{48,56},{56,64},{64,7... | collective-permute-start | bytes 1572872 | tf_op jit(solution)/shard_map/ppermute | solution.py:16
  242.8 16.5 %copy-start.4 = (f32[2,8,32,256]{3,2,1,0:T(8,128)S(1)}, f32[2,8,32,256]{3,2,1,0:T(8,128)}, u32[]{:S(2)}) copy-start(f32[2,8,32,256]{3,2,1,0:T(8,128)} %copy-done.3) | copy-start | bytes 1572868
  242.9 10.8 %collective-permute-start.14 = (f32[2,32,768]{2,1,0:T(8,128)S(1)}, f32[2,32,768]{2,1,0:T(8,128)S(1)}, u32[]{:S(2)}, u32[]{:S(2)}) collective-permute-start(f32[2,32,768]{2,1,0:T(8,128)S(1)} %get-tuple-element.21), channel_id=1, source_target_pairs={{0,6},{1,7},{2,0},{3,1},{4,2},{5,3},{6,4},{7,5},{8,14},{9,15},{10,... | collective-permute-start | bytes 589832 | tf_op jit(solution)/shard_map/ppermute | solution.py:21
  245.7 8.0 %collective-permute-start.13 = (f32[2,32,768]{2,1,0:T(8,128)S(1)}, f32[2,32,768]{2,1,0:T(8,128)S(1)}, u32[]{:S(2)}, u32[]{:S(2)}) collective-permute-start(f32[2,32,768]{2,1,0:T(8,128)S(1)} %get-tuple-element.22), channel_id=1, source_target_pairs={{0,4},{1,5},{2,6},{3,7},{4,0},{5,1},{6,2},{7,3},{8,12},{9,13},{10,... | collective-permute-start | bytes 589832 | tf_op jit(solution)/shard_map/ppermute | solution.py:21
  246.0 12.2 %collective-permute-start.12 = (f32[2,32,768]{2,1,0:T(8,128)S(1)}, f32[2,32,768]{2,1,0:T(8,128)S(1)}, u32[]{:S(2)}, u32[]{:S(2)}) collective-permute-start(f32[2,32,768]{2,1,0:T(8,128)S(1)} %get-tuple-element.20), channel_id=1, source_target_pairs={{0,2},{1,3},{2,4},{3,5},{4,6},{5,7},{6,0},{7,1},{8,10},{9,11},{10,... | collective-permute-start | bytes 589832 | tf_op jit(solution)/shard_map/ppermute | solution.py:21
  247.8 22.4 %copy-start.6 = (f32[2,256,256]{2,1,0:T(8,128)S(1)}, f32[2,256,256]{2,1,0:T(8,128)}, u32[]{:S(2)}) copy-start(f32[2,256,256]{2,1,0:T(8,128)} %param.14) | copy-start | bytes 1572868
  258.3 11.9 %copy-start.9 = (f32[2,256,256]{2,1,0:T(8,128)}, f32[2,256,256]{2,1,0:T(8,128)S(1)}, u32[]{:S(2)}) copy-start(f32[2,256,256]{2,1,0:T(8,128)S(1)} %collective-permute-done.10) | copy-start | bytes 1572868
  258.3 11.9 %collective-permute-start.17 = (f32[2,32,256]{2,1,0:T(8,128)S(1)}, f32[2,32,256]{2,1,0:T(8,128)S(1)}, u32[]{:S(2)}, u32[]{:S(2)}) collective-permute-start(f32[2,32,256]{2,1,0:T(8,128)S(1)} %slice_subtract_fusion), channel_id=1, source_target_pairs={{0,6},{1,7},{2,0},{3,1},{4,2},{5,3},{6,4},{7,5},{8,14},{9,15},{10,... | collective-permute-start | bytes 196616 | tf_op jit(solution)/shard_map/ppermute | solution.py:21
  259.7 7.2 %collective-permute-start.19 = (f32[2,32,512]{2,1,0:T(8,128)S(1)}, f32[2,32,512]{2,1,0:T(8,128)S(1)}, u32[]{:S(2)}, u32[]{:S(2)}) collective-permute-start(f32[2,32,512]{2,1,0:T(8,128)S(1)} %pad_maximum_fusion.6), channel_id=1, source_target_pairs={{0,8},{8,16},{16,24},{24,32},{32,40},{40,48},{48,56},{56,64},{64,7... | collective-permute-start | bytes 393224 | tf_op jit(solution)/shard_map/ppermute | solution.py:16
  260.9 10.4 %collective-permute-start.16 = (f32[2,32,256]{2,1,0:T(8,128)S(1)}, f32[2,32,256]{2,1,0:T(8,128)S(1)}, u32[]{:S(2)}, u32[]{:S(2)}) collective-permute-start(f32[2,32,256]{2,1,0:T(8,128)S(1)} %slice_subtract_fusion), channel_id=1, source_target_pairs={{0,4},{1,5},{2,6},{3,7},{4,0},{5,1},{6,2},{7,3},{8,12},{9,13},{10,... | collective-permute-start | bytes 196616 | tf_op jit(solution)/shard_map/ppermute | solution.py:21
  261.3 10.0 %collective-permute-start.15 = (f32[2,32,256]{2,1,0:T(8,128)S(1)}, f32[2,32,256]{2,1,0:T(8,128)S(1)}, u32[]{:S(2)}, u32[]{:S(2)}) collective-permute-start(f32[2,32,256]{2,1,0:T(8,128)S(1)} %slice_subtract_fusion), channel_id=1, source_target_pairs={{0,2},{1,3},{2,4},{3,5},{4,6},{5,7},{6,0},{7,1},{8,10},{9,11},{10,... | collective-permute-start | bytes 196616 | tf_op jit(solution)/shard_map/ppermute | solution.py:21
  266.9 7.0 %collective-permute-start.22 = (f32[2,32,512]{2,1,0:T(8,128)S(1)}, f32[2,32,512]{2,1,0:T(8,128)S(1)}, u32[]{:S(2)}, u32[]{:S(2)}) collective-permute-start(f32[2,32,512]{2,1,0:T(8,128)S(1)} %collective-permute-done.19), channel_id=1, source_target_pairs={{0,6},{1,7},{2,0},{3,1},{4,2},{5,3},{6,4},{7,5},{8,14},{9,15},{10,... | collective-permute-start | bytes 393224 | tf_op jit(solution)/shard_map/ppermute | solution.py:21
  267.4 6.6 %collective-permute-start.21 = (f32[2,32,512]{2,1,0:T(8,128)S(1)}, f32[2,32,512]{2,1,0:T(8,128)S(1)}, u32[]{:S(2)}, u32[]{:S(2)}) collective-permute-start(f32[2,32,512]{2,1,0:T(8,128)S(1)} %collective-permute-done.19), channel_id=1, source_target_pairs={{0,4},{1,5},{2,6},{3,7},{4,0},{5,1},{6,2},{7,3},{8,12},{9,13},{10,... | collective-permute-start | bytes 393224 | tf_op jit(solution)/shard_map/ppermute | solution.py:21
  270.2 7.0 %collective-permute-start.20 = (f32[2,32,512]{2,1,0:T(8,128)S(1)}, f32[2,32,512]{2,1,0:T(8,128)S(1)}, u32[]{:S(2)}, u32[]{:S(2)}) collective-permute-start(f32[2,32,512]{2,1,0:T(8,128)S(1)} %collective-permute-done.19), channel_id=1, source_target_pairs={{0,2},{1,3},{2,4},{3,5},{4,6},{5,7},{6,0},{7,1},{8,10},{9,11},{10,... | collective-permute-start | bytes 393224 | tf_op jit(solution)/shard_map/ppermute | solution.py:21
  271.3 8.2 %copy-start.10 = (f32[2,256,256]{2,1,0:T(8,128)S(1)}, f32[2,256,256]{2,1,0:T(8,128)}, u32[]{:S(2)}) copy-start(f32[2,256,256]{2,1,0:T(8,128)} %copy-done.9) | copy-start | bytes 1572868
  271.9 8.7 %collective-permute-start.18 = (f32[2,128,256]{2,1,0:T(8,128)S(1)}, f32[2,128,256]{2,1,0:T(8,128)}, u32[]{:S(2)}, u32[]{:S(2)}) collective-permute-start(f32[2,128,256]{2,1,0:T(8,128)S(1)} %bitcast.87), channel_id=1, source_target_pairs={{0,1},{1,0},{2,3},{3,2},{4,5},{5,4},{6,7},{7,6},{8,9},{9,8},{10,11... | collective-permute-start | bytes 786440 | tf_op jit(solution)/shard_map/ppermute | solution.py:57
  277.9 3.7 %collective-permute-start.23 = (f32[2,128,512]{2,1,0:T(8,128)S(1)}, f32[2,128,512]{2,1,0:T(8,128)S(1)}, u32[]{:S(2)}, u32[]{:S(2)}) collective-permute-start(f32[2,128,512]{2,1,0:T(8,128)S(1)} %bitcast.81), channel_id=1, source_target_pairs={{0,1},{1,0},{2,3},{3,2},{4,5},{5,4},{6,7},{7,6},{8,9},{9,8},{10,11... | collective-permute-start | bytes 1572872 | tf_op jit(solution)/shard_map/ppermute | solution.py:57
  281.6 1.6 copy-start.7
  281.7 1.5 copy-start.5
